TPU v7x, 128 devices: a whole 4x4x4 slice. The times are simulated.
128 devices in a mesh: slab: 32 (over z, y, x_hi), gy: 4 (over x_lo, core).
Axes of the slice: x: 4 (x_hi: 2, x_lo: 2; x = x_hi * 2 + x_lo), y: 4, z: 4, core: 2. Of those that a mesh axis runs over, the one named last changes fastest.
Arguments:
- electrostatic_voltages: float32 [256, 256, 1024], P('slab', 'gy'), may hold values from -6 to 6
- initial_electrons: float32 [256, 256, 1024], P('slab', 'gy'), may hold values from 0.5 to 2
- creation_amounts: float32 [256, 256, 1024], P('slab', 'gy'), may hold values from 0.2 to 5
- annihilation_coefficient: float32 [256, 256, 1024], P('slab', 'gy'), may hold values from 0.5 to 2
- crystal_orientation_class: int32 [256, 256, 1024], P('slab', 'gy'), may hold values from 0 to 3
- crystal_barrier_shift: float32 [4], replicated, may hold values from -1.5 to 1.5
- restrict_matrix_first: float32 [128, 256], replicated, may hold values from 0 to 1, as said below
- restrict_matrix_second: float32 [128, 64], P('gy'), may hold values from 0 to 1, as said below
- restrict_matrix_third: float32 [256, 1024], replicated, may hold values from 0 to 1, as said below
- cooling_coefficient: float32 [256, 128, 128], P('slab', 'gy'), may hold values from 0.05 to 1
- initial_warming: float32 [256, 128, 128], P('slab', 'gy'), may hold values from 0.5 to 1.5
Outputs:
- density_out: float32 [256, 256, 1024], P('slab', 'gy')
- thermal_out: float32 [256, 128, 128], P('slab', 'gy')
- fine_mesh_warming: float32 [256, 256, 1024], P('slab', 'gy')
Inputs may be any that keep to these rules, and one draw needn't show every extreme that they name: `restrict_matrix_first`: row a is nonnegative, nonzero at most on columns 2a - 1 to 2a + 2, and sums to 1. `restrict_matrix_second`: row b, with t = b % 32, is nonnegative, nonzero at most on columns 2t - 1 to 2t + 2, and sums to 1. `restrict_matrix_third`: row c is nonnegative, nonzero at most on columns 4c - 2 to 4c + 5, and sums to 1.
All inputs are finite; a program needn't handle non-finite values.
Results may differ from a plain program's by a relative error of at most 0.0003.
Values sent between devices are 32-bit elements; how exact they have to be, the bound alone decides.
No kernel may reach another device: no remote copies, remote signals or barrier semaphores. Data moves between devices by JAX's collectives and lax.ppermute only.
A program may use at most 64 MiB of HBM per device.

v0:
```python
import jax
import jax.numpy as jnp
from jax import lax
from jax.sharding import PartitionSpec as P

GRAINS = 4
HEAT_SWEEPS = 3
BAND = 6


def face_halos(block, sides):
    halos = []
    for axis, dim in sides:
        count = lax.axis_size(axis)
        forward = [(i, i + 1) for i in range(count - 1)]
        backward = [(i + 1, i) for i in range(count - 1)]
        size = block.shape[dim]
        low = lax.ppermute(lax.slice_in_dim(block, size - 1, size, axis=dim), axis, forward)
        high = lax.ppermute(lax.slice_in_dim(block, 0, 1, axis=dim), axis, backward)
        halos.append((low, high))
    return halos


def neighbours_of(block, halos, lead=0):
    out = []
    for k, (low, high) in enumerate(halos):
        dim = lead + k
        size = block.shape[dim]
        out.append(jnp.concatenate([lax.slice_in_dim(block, 1, size, axis=dim), high], axis=dim))
        out.append(jnp.concatenate([low, lax.slice_in_dim(block, 0, size - 1, axis=dim)], axis=dim))
    last = block.ndim - 1
    size = block.shape[last]
    zero = jnp.zeros_like(lax.slice_in_dim(block, 0, 1, axis=last))
    out.append(jnp.concatenate([lax.slice_in_dim(block, 1, size, axis=last), zero], axis=last))
    out.append(jnp.concatenate([zero, lax.slice_in_dim(block, 0, size - 1, axis=last)], axis=last))
    return out


def bernoulli(value):
    small = jnp.abs(value) < 0.0001
    safe = jnp.where(small, jnp.float32(1.0), value)
    return jnp.where(small, 1.0 - 0.5 * value, safe / jnp.expm1(safe))


def per_device(
    electrostatic_voltages,
    initial_electrons,
    creation_amounts,
    annihilation_coefficient,
    crystal_orientation_class,
    crystal_barrier_shift,
    restrict_matrix_first,
    restrict_matrix_second,
    restrict_matrix_third,
    cooling_coefficient,
    initial_warming,
):
    upper_limit = lax.Precision.HIGHEST
    slab_cells = electrostatic_voltages.shape[0]
    slabs = lax.axis_size("slab")
    me = lax.axis_index("slab")
    effective = electrostatic_voltages
    for grain in range(GRAINS):
        effective = effective + jnp.where(
            crystal_orientation_class == grain, crystal_barrier_shift[grain], jnp.float32(0.0)
        )
    device_sides = (("slab", 0), ("gy", 1))
    both = jnp.stack([effective, initial_electrons])
    both_halos = face_halos(both, (("slab", 1), ("gy", 2)))
    beside_both = neighbours_of(both, both_halos, lead=1)
    beside_all = [b[0] for b in beside_both]
    voltage_gradients = [leftover_portion - effective for leftover_portion in beside_all]
    bernoulli_coefficients = [bernoulli(voltage_gradient) for voltage_gradient in voltage_gradients]
    denominator_quantity = annihilation_coefficient
    for bernoulli_coefficient, voltage_gradient in zip(bernoulli_coefficients, voltage_gradients):
        denominator_quantity = denominator_quantity + (bernoulli_coefficient + voltage_gradient)

    def sweep(beside):
        fraction_top_quantity = creation_amounts
        for bernoulli_coefficient, leftover_portion in zip(bernoulli_coefficients, beside):
            fraction_top_quantity = fraction_top_quantity + bernoulli_coefficient * leftover_portion
        return fraction_top_quantity / denominator_quantity

    electron_concentration = sweep([b[1] for b in beside_both])
    electron_concentration = sweep(
        neighbours_of(electron_concentration, face_halos(electron_concentration, device_sides))
    )
    n_final = electron_concentration
    y_low, y_high = face_halos(n_final, (("gy", 1),))[0]
    zero_x = jnp.zeros_like(n_final[:1])
    beside_final = neighbours_of(n_final, [(zero_x, zero_x), (y_low, y_high)])
    joule_power_input = jnp.zeros_like(n_final)
    for bernoulli_coefficient, voltage_gradient, leftover_portion in zip(
        bernoulli_coefficients, voltage_gradients, beside_final
    ):
        joule_power_input = joule_power_input + voltage_gradient * (
            bernoulli_coefficient * leftover_portion
            - (bernoulli_coefficient + voltage_gradient) * n_final
        )
    joule_power_input = 0.5 * joule_power_input
    up_x, down_x = voltage_gradients[0], voltage_gradients[1]
    bup_x, bdown_x = bernoulli_coefficients[0], bernoulli_coefficients[1]
    heat_left = -0.5 * (down_x[:1] * ((bdown_x[:1] + down_x[:1]) * n_final[:1]))
    heat_right = -0.5 * (up_x[-1:] * ((bup_x[-1:] + up_x[-1:]) * n_final[-1:]))
    heat_ext = jnp.concatenate([heat_left, joule_power_input, heat_right], axis=0)

    padded_first = jnp.pad(restrict_matrix_first, ((1, 1), (1, 1)))
    ratio = slab_cells // 2
    columns_ext = lax.dynamic_slice(
        padded_first, (me * ratio, me * slab_cells), (BAND, slab_cells + 2)
    )
    columns = columns_ext[:, 1 : 1 + slab_cells]
    along_y = jnp.einsum(
        "ty,xyz->xtz", restrict_matrix_second, heat_ext, precision=upper_limit
    )
    along_z = jnp.einsum("cz,xtz->ctx", restrict_matrix_third, along_y, precision=upper_limit)
    piece = jnp.einsum("ctx,ax->cta", along_z, columns_ext, precision=upper_limit)
    chunk_c = piece.shape[0] // slabs
    piece = piece.reshape(slabs, chunk_c, piece.shape[1], BAND)
    got = lax.all_to_all(piece, "slab", 0, 0, tiled=False)
    main = got[..., 1 : 1 + ratio]
    zero_row = jnp.zeros_like(got[:1, ..., 0])
    left = jnp.concatenate([got[1:, ..., 0], zero_row], axis=0)
    right = jnp.concatenate([zero_row, got[:-1, ..., ratio + 1]], axis=0)
    main = main.at[..., ratio - 1].add(left)
    main = main.at[..., 0].add(right)
    source = jnp.transpose(main, (1, 2, 0, 3)).reshape(chunk_c, main.shape[2], slabs * ratio)

    stacked = jnp.stack([initial_warming, source, 6.0 + cooling_coefficient])
    depths = (HEAT_SWEEPS, 8)
    for (axis, dim), depth in zip((("slab", 1), ("gy", 2)), depths):
        count = lax.axis_size(axis)
        forward = [(i, i + 1) for i in range(count - 1)]
        backward = [(i + 1, i) for i in range(count - 1)]
        size = stacked.shape[dim]
        low = lax.ppermute(lax.slice_in_dim(stacked, size - depth, size, axis=dim), axis, forward)
        high = lax.ppermute(lax.slice_in_dim(stacked, 0, depth, axis=dim), axis, backward)
        stacked = jnp.concatenate([low, stacked, high], axis=dim)
    tc, tb = initial_warming.shape[0], initial_warming.shape[1]
    c_index = lax.broadcasted_iota(jnp.int32, stacked.shape[1:], 0) + (me * tc - depths[0])
    b_index = lax.broadcasted_iota(jnp.int32, stacked.shape[1:], 1) + (
        lax.axis_index("gy") * tb - depths[1]
    )
    inside = (
        (c_index >= 0)
        & (c_index < slabs * tc)
        & (b_index >= 0)
        & (b_index < lax.axis_size("gy") * tb)
    )
    warm = stacked[0]
    source_ext, scale_ext = stacked[1], stacked[2]
    for repeat in range(HEAT_SWEEPS):
        padded = jnp.pad(warm, 1)
        total = source_ext
        for leftover_portion in (
            padded[2:, 1:-1, 1:-1],
            padded[:-2, 1:-1, 1:-1],
            padded[1:-1, 2:, 1:-1],
            padded[1:-1, :-2, 1:-1],
            padded[1:-1, 1:-1, 2:],
            padded[1:-1, 1:-1, :-2],
        ):
            total = total + leftover_portion
        warm = jnp.where(inside, total / scale_ext, 0.0)
    warming_distribution = warm[depths[0] : depths[0] + tc, depths[1] : depths[1] + tb]

    padded_warm = jnp.pad(warming_distribution, ((0, 0), (0, 0), (1, 1)))
    windows = jnp.stack(
        [padded_warm[..., ratio * s : ratio * s + BAND] for s in range(slabs)]
    )
    got_warm = lax.all_to_all(windows, "slab", 0, 0, tiled=False)
    got_warm = got_warm.reshape(slabs * chunk_c, got_warm.shape[2], BAND)
    spread = jnp.einsum("cta,ax->ctx", got_warm, columns, precision=upper_limit)
    raised_field = jnp.einsum(
        "ctx,cz->xtz", spread, restrict_matrix_third, precision=upper_limit
    )
    fine_mesh_warming = 16.0 * jnp.einsum(
        "hc,qhk->qck", restrict_matrix_second, raised_field, precision=upper_limit
    )
    return (electron_concentration, warming_distribution, fine_mesh_warming)


def solution(mesh):
    in_specs = (
        P("slab", "gy", None),
        P("slab", "gy", None),
        P("slab", "gy", None),
        P("slab", "gy", None),
        P("slab", "gy", None),
        P(),
        P(),
        P("gy", None),
        P(),
        P("slab", "gy", None),
        P("slab", "gy", None),
    )
    out_specs = (P("slab", "gy", None), P("slab", "gy", None), P("slab", "gy", None))
    return jax.shard_map(
        per_device, mesh=mesh, in_specs=in_specs, out_specs=out_specs, check_vma=False
    )
```

profile of v0, /device:TPU:1, one launch (start us, length us, event | category | flops | bytes accessed | tf_op | source)
XLA Modules:
  0.0 230.4 jit_solution(8800347407193820350)
XLA Ops:
  2.0 5.7 %select_add_fusion = f32[8,64,1024]{2,1,0:T(8,128)S(1)} fusion(f32[8,64,1024]{2,1,0:T(8,128)} %param.15, s32[8,64,1024]{2,1,0:T(8,128)} %param.19, f32[]{:T(128)} %bitcast.3, f32[]{:T(128)} %bitcast.2, f32[]{:T(128)} %bitcast.1, f32[]{:T(128)} %bitcast), kind=kLoop, calls=%fused_computation.124 | loop fusion | flops 6291456 | bytes 6291472 | tf_op jit(solution)/shard_map/add | solution.py:64
  7.8 4.5 %collective-permute-start.3 = (f32[2,8,1,1024]{3,2,1,0:T(1,128)S(1)}, f32[2,8,1,1024]{3,2,1,0:T(1,128)S(1)}, u32[]{:S(2)}, u32[]{:S(2)}) collective-permute-start(f32[2,8,1,1024]{3,2,1,0:T(1,128)S(1)} %get-tuple-element.44), channel_id=1, source_target_pairs={{0,1},{1,2},{2,3},{4,5},{5,6},{6,7},{8,9},{9,10},{10,11},{12,13},{... | collective-permute-start | bytes 196616 | tf_op jit(solution)/shard_map/ppermute | solution.py:18
  15.3 5.2 %collective-permute-start.1 = (f32[2,1,64,1024]{3,2,1,0:T(8,128)}, f32[2,1,64,1024]{3,2,1,0:T(8,128)}, u32[]{:S(2)}, u32[]{:S(2)}) collective-permute-start(f32[2,1,64,1024]{3,2,1,0:T(8,128)} %get-tuple-element.40), channel_id=1, source_target_pairs={{0,4},{4,8},{8,12},{12,16},{16,20},{20,24},{24,28},{28,32},{32,36}... | collective-permute-start | bytes 1572872 | tf_op jit(solution)/shard_map/ppermute | solution.py:18
  21.8 3.1 %fusion = f32[2,8,64,1023]{3,2,1,0:T(8,128)} fusion(f32[1,8,64,1024]{3,2,1,0:T(8,128)S(1)} %bitcast.272, f32[1,8,64,1024]{3,2,1,0:T(8,128)S(1)} %bitcast.279), kind=kLoop, calls=%fused_computation.18 | loop fusion | flops 1047552 | bytes 8384512 | tf_op jit(solution)/shard_map/stack | solution.py:68
  24.9 3.3 %fusion.3 = (f32[2,7,64,1024]{3,2,1,0:T(8,128)}, f32[2,7,64,1024]{3,2,1,0:T(8,128)}) fusion(f32[1,8,64,1024]{3,2,1,0:T(8,128)S(1)} %bitcast.273, f32[1,8,64,1024]{3,2,1,0:T(8,128)S(1)} %bitcast.280), kind=kLoop, calls=%fused_computation.33 | loop fusion | flops 1835008 | bytes 11534336 | tf_op jit(solution)/shard_map/stack | solution.py:68
  28.3 2.9 %select_maximum_fusion = f32[2,8,64,1024]{3,2,1,0:T(8,128)S(1)} fusion(f32[1,8,64,1024]{3,2,1,0:T(8,128)} %bitcast.276, f32[1,8,64,1024]{3,2,1,0:T(8,128)S(1)} %bitcast.274), kind=kLoop, calls=%fused_computation.21 | loop fusion | flops 4194304 | bytes 8388608 | tf_op jit(solution)/shard_map/stack | solution.py:68
  32.3 11.1 %collective-permute-done = f32[2,1,64,1024]{3,2,1,0:T(8,128)} collective-permute-done((f32[2,1,64,1024]{3,2,1,0:T(8,128)}, f32[2,1,64,1024]{3,2,1,0:T(8,128)}, u32[]{:S(2)}, u32[]{:S(2)}) %collective-permute-start) | collective-permute-done | bytes 524320 | tf_op jit(solution)/shard_map/ppermute | solution.py:19
  43.5 4.8 %fusion.11 = (f32[8,64,1024]{2,1,0:T(8,128)}, f32[8,64,1024]{2,1,0:T(8,128)S(1)}, f32[8,64,1024]{2,1,0:T(8,128)}, f32[8,64,1024]{2,1,0:T(8,128)S(1)}) fusion(f32[8,64,1024]{2,1,0:T(8,128)S(1)} %select_add_fusion, f32[2,1,64,1024]{3,2,1,0:T(8,128)} %collective-permute-done, f32[2,7,64,1024]{3,2,1,0:T(8,128)S(1)} %copy-done.5, ...), kind=kLoop, calls=%fused_computation.47 | loop fusion | flops 9437184 | bytes 18874368 | tf_op jit(solution)/shard_map/jit(_where)/select_n | solution.py:42
  48.4 10.2 %fusion.23 = f32[8,64,1024]{2,1,0:T(8,128)S(1)} fusion(f32[2,8,64,1023]{3,2,1,0:T(8,128)S(1)} %copy-done.4, f32[2,8,64,1024]{3,2,1,0:T(8,128)S(1)} %select_maximum_fusion, f32[2,8,63,1024]{3,2,1,0:T(8,128)S(1)} %get-tuple-element.42, f32[2,8,1,1024]{3,2,1,0:T(1,128)S(1)} %collective-permute-done.3, f32[2,8,1,1024]{3,2,1,0:T(1,128)S(1)} %collective-permute-done.2, ...), kind=kLoop, calls=%fused_computation.59 | loop fusion | flops 40370176 | bytes 37744640 | tf_op jit(solution)/shard_map/div | solution.py:82
  59.2 2.1 fusion.132
  62.6 5.5 %collective-permute-start.5 = (f32[1,64,1024]{2,1,0:T(8,128)S(1)}, f32[1,64,1024]{2,1,0:T(8,128)S(1)}, u32[]{:S(2)}, u32[]{:S(2)}) collective-permute-start(f32[1,64,1024]{2,1,0:T(8,128)S(1)} %get-tuple-element.61), channel_id=1, source_target_pairs={{0,4},{4,8},{8,12},{12,16},{16,20},{20,24},{24,28},{28,32},{32,36}... | collective-permute-start | bytes 786440 | tf_op jit(solution)/shard_map/ppermute | solution.py:18
  70.0 4.8 %collective-permute-start.7 = (f32[8,1,1024]{2,1,0:T(1,128)S(1)}, f32[8,1,1024]{2,1,0:T(1,128)S(1)}, u32[]{:S(2)}, u32[]{:S(2)}) collective-permute-start(f32[8,1,1024]{2,1,0:T(1,128)S(1)} %get-tuple-element.57), channel_id=1, source_target_pairs={{0,1},{1,2},{2,3},{4,5},{5,6},{6,7},{8,9},{9,10},{10,11},{12,13},{... | collective-permute-start | bytes 98312 | tf_op jit(solution)/shard_map/ppermute | solution.py:18
  74.8 2.2 fusion.136
  77.1 11.4 %fusion.56 = f32[8,64,1024]{2,1,0:T(8,128)S(1)} fusion(f32[8,64,1024]{2,1,0:T(8,128)S(1)} %copy-done.7, f32[1,64,1024]{2,1,0:T(8,128)S(1)} %collective-permute-done.4, f32[7,64,1024]{2,1,0:T(8,128)} %get-tuple-element.64, f32[7,64,1024]{2,1,0:T(8,128)} %get-tuple-element.63, f32[1,64,1024]{2,1,0:T(8,128)S(1)} %collective-permute-done.5, ...), kind=kLoop, calls=%fused_computation.99 | loop fusion | flops 40370176 | bytes 39837696 | tf_op jit(solution)/shard_map/div | solution.py:82
  90.0 2.3 fusion.128
  94.2 3.6 %collective-permute-start.9 = (f32[8,1,1024]{2,1,0:T(1,128)S(1)}, f32[8,1,1024]{2,1,0:T(1,128)S(1)}, u32[]{:S(2)}, u32[]{:S(2)}) collective-permute-start(f32[8,1,1024]{2,1,0:T(1,128)S(1)} %get-tuple-element.51), channel_id=1, source_target_pairs={{0,1},{1,2},{2,3},{4,5},{5,6},{6,7},{8,9},{9,10},{10,11},{12,13},{... | collective-permute-start | bytes 98312 | tf_op jit(solution)/shard_map/ppermute | solution.py:18
  99.1 11.2 %fusion.63 = f32[8,64,1024]{2,1,0:T(8,128)S(1)} fusion(f32[8,1,1024]{2,1,0:T(1,128)S(1)} %collective-permute-done.8, f32[8,63,1024]{2,1,0:T(8,128)S(1)} %get-tuple-element.54, f32[8,63,1024]{2,1,0:T(8,128)S(1)} %get-tuple-element.53, f32[8,1,1024]{2,1,0:T(1,128)S(1)} %collective-permute-done.9, f32[8,64,1024]{2,1,0:T(8,128)S(1)} %fusion.56, ...), kind=kLoop, calls=%fused_computation.110 | loop fusion | flops 45088768 | bytes 37216256 | tf_op jit(solution)/shard_map/mul | solution.py:100
  115.2 12.8 %all-to-all-start = ((f32[32,1,1536]{2,1,0:T(1,128)}), f32[32,1,1536]{2,1,0:T(1,128)S(1)}, u32[]{:S(2)}, u32[]{:S(2)}) async-start(f32[32,1,1536]{2,1,0:T(1,128)} %reshape.92), calls=%async_computation | async-start | bytes 393216 | tf_op jit(solution)/shard_map/all_to_all | solution.py:120
  128.0 9.7 %all-to-all-done = f32[32,1,1536]{2,1,0:T(1,128)S(1)} async-done(((f32[32,1,1536]{2,1,0:T(1,128)}), f32[32,1,1536]{2,1,0:T(1,128)S(1)}, u32[]{:S(2)}, u32[]{:S(2)}) %all-to-all-start) | async-done | bytes 196640 | tf_op jit(solution)/shard_map/all_to_all | solution.py:120
  141.9 5.5 %collective-permute-start.10 = (f32[3,3,32,128]{3,2,1,0:T(8,128)S(1)}, f32[3,3,32,128]{3,2,1,0:T(8,128)S(1)}, u32[]{:S(2)}, u32[]{:S(2)}) collective-permute-start(f32[3,3,32,128]{3,2,1,0:T(8,128)S(1)} %get-tuple-element.71), channel_id=1, source_target_pairs={{0,4},{4,8},{8,12},{12,16},{16,20},{20,24},{24,28},{28,32},{32,36}... | collective-permute-start | bytes 442376 | tf_op jit(solution)/shard_map/ppermute | solution.py:136
  150.1 3.3 %collective-permute-start.13 = (f32[3,14,8,128]{3,2,1,0:T(8,128)S(1)}, f32[3,14,8,128]{3,2,1,0:T(8,128)S(1)}, u32[]{:S(2)}, u32[]{:S(2)}) collective-permute-start(f32[3,14,8,128]{3,2,1,0:T(8,128)S(1)} %get-tuple-element.70), channel_id=1, source_target_pairs={{1,0},{2,1},{3,2},{5,4},{6,5},{7,6},{9,8},{10,9},{11,10},{13,12},{... | collective-permute-start | bytes 516104 | tf_op jit(solution)/shard_map/ppermute | solution.py:137
  153.4 3.5 %collective-permute-start.12 = (f32[3,14,8,128]{3,2,1,0:T(8,128)S(1)}, f32[3,14,8,128]{3,2,1,0:T(8,128)S(1)}, u32[]{:S(2)}, u32[]{:S(2)}) collective-permute-start(f32[3,14,8,128]{3,2,1,0:T(8,128)S(1)} %get-tuple-element.69), channel_id=1, source_target_pairs={{0,1},{1,2},{2,3},{4,5},{5,6},{6,7},{8,9},{9,10},{10,11},{12,13},{... | collective-permute-start | bytes 516104 | tf_op jit(solution)/shard_map/ppermute | solution.py:136
  206.2 17.6 %all_to_all.10 = f32[32,1,1536]{2,1,0:T(1,128)S(1)} all-to-all(f32[32,1,1536]{2,1,0:T(1,128)S(1)} %reshape.94), channel_id=1, replica_groups=mesh['slab'=32,'gy'=4] {'slab'}, dimensions={0} | all-to-all | bytes 393216 | tf_op jit(solution)/shard_map/all_to_all | solution.py:171
  227.1 3.3 %multiply_bitcast_fusion = f32[8,64,1024]{2,1,0:T(8,128)} fusion(f32[8,32,1024]{2,1,0:T(8,128)S(1)} %convolution_bitcast_fusion, f32[32,64]{1,0:T(8,128)S(1)} %copy-done.24), kind=kOutput, calls=%fused_computation.114 | convolution fusion | flops 201850880 | bytes 3153920 | tf_op jit(solution)/shard_map/hc,qhk->qck/dot_general | solution.py:177
  (186 shorter events, 79.1 us)
Async XLA Ops:
  0.6 111.2 %copy-start = (f32[256,1024]{1,0:T(8,128)S(1)}, f32[256,1024]{1,0:T(8,128)}, u32[]{:S(2)}) copy-start(f32[256,1024]{1,0:T(8,128)} %param.23) | copy-start | bytes 3145732
  7.8 40.5 %collective-permute-start.3 = (f32[2,8,1,1024]{3,2,1,0:T(1,128)S(1)}, f32[2,8,1,1024]{3,2,1,0:T(1,128)S(1)}, u32[]{:S(2)}, u32[]{:S(2)}) collective-permute-start(f32[2,8,1,1024]{3,2,1,0:T(1,128)S(1)} %get-tuple-element.44), channel_id=1, source_target_pairs={{0,1},{1,2},{2,3},{4,5},{5,6},{6,7},{8,9},{9,10},{10,11},{12,13},{... | collective-permute-start | bytes 196616 | tf_op jit(solution)/shard_map/ppermute | solution.py:18
  12.3 36.0 %collective-permute-start.2 = (f32[2,8,1,1024]{3,2,1,0:T(1,128)S(1)}, f32[2,8,1,1024]{3,2,1,0:T(1,128)S(1)}, u32[]{:S(2)}, u32[]{:S(2)}) collective-permute-start(f32[2,8,1,1024]{3,2,1,0:T(1,128)S(1)} %get-tuple-element.43), channel_id=1, source_target_pairs={{1,0},{2,1},{3,2},{5,4},{6,5},{7,6},{9,8},{10,9},{11,10},{13,12},{... | collective-permute-start | bytes 196616 | tf_op jit(solution)/shard_map/ppermute | solution.py:19
  15.3 17.0 %collective-permute-start.1 = (f32[2,1,64,1024]{3,2,1,0:T(8,128)}, f32[2,1,64,1024]{3,2,1,0:T(8,128)}, u32[]{:S(2)}, u32[]{:S(2)}) collective-permute-start(f32[2,1,64,1024]{3,2,1,0:T(8,128)} %get-tuple-element.40), channel_id=1, source_target_pairs={{0,4},{4,8},{8,12},{12,16},{16,20},{20,24},{24,28},{28,32},{32,36}... | collective-permute-start | bytes 1572872 | tf_op jit(solution)/shard_map/ppermute | solution.py:18
  20.5 23.0 %collective-permute-start = (f32[2,1,64,1024]{3,2,1,0:T(8,128)}, f32[2,1,64,1024]{3,2,1,0:T(8,128)}, u32[]{:S(2)}, u32[]{:S(2)}) collective-permute-start(f32[2,1,64,1024]{3,2,1,0:T(8,128)} %get-tuple-element.39), channel_id=1, source_target_pairs={{4,0},{8,4},{12,8},{16,12},{20,16},{24,20},{28,24},{32,28},{36,32}... | collective-permute-start | bytes 1572872 | tf_op jit(solution)/shard_map/ppermute | solution.py:19
  28.3 84.8 %copy-start.25 = (f32[6,10]{1,0:T(8,128)}, f32[6,10]{1,0:T(8,128)S(1)}, u32[]{:S(2)}) copy-start(f32[6,10]{1,0:T(8,128)S(1)} %pad_dynamic-slice_fusion) | copy-start | bytes 724
  31.2 12.3 %copy-start.5 = (f32[2,7,64,1024]{3,2,1,0:T(8,128)S(1)}, f32[2,7,64,1024]{3,2,1,0:T(8,128)}, u32[]{:S(2)}) copy-start(f32[2,7,64,1024]{3,2,1,0:T(8,128)} %get-tuple-element.37) | copy-start | bytes 11010052
  31.2 12.3 %copy-start.6 = (f32[2,7,64,1024]{3,2,1,0:T(8,128)S(1)}, f32[2,7,64,1024]{3,2,1,0:T(8,128)}, u32[]{:S(2)}) copy-start(f32[2,7,64,1024]{3,2,1,0:T(8,128)} %get-tuple-element.38) | copy-start | bytes 11010052
  61.3 15.8 %collective-permute-start.4 = (f32[1,64,1024]{2,1,0:T(8,128)S(1)}, f32[1,64,1024]{2,1,0:T(8,128)S(1)}, u32[]{:S(2)}, u32[]{:S(2)}) collective-permute-start(f32[1,64,1024]{2,1,0:T(8,128)S(1)} %get-tuple-element.62), channel_id=1, source_target_pairs={{4,0},{8,4},{12,8},{16,12},{20,16},{24,20},{28,24},{32,28},{36,32}... | collective-permute-start | bytes 786440 | tf_op jit(solution)/shard_map/ppermute | solution.py:19
  62.6 14.5 %collective-permute-start.5 = (f32[1,64,1024]{2,1,0:T(8,128)S(1)}, f32[1,64,1024]{2,1,0:T(8,128)S(1)}, u32[]{:S(2)}, u32[]{:S(2)}) collective-permute-start(f32[1,64,1024]{2,1,0:T(8,128)S(1)} %get-tuple-element.61), channel_id=1, source_target_pairs={{0,4},{4,8},{8,12},{12,16},{16,20},{20,24},{24,28},{28,32},{32,36}... | collective-permute-start | bytes 786440 | tf_op jit(solution)/shard_map/ppermute | solution.py:18
  68.1 9.0 %collective-permute-start.6 = (f32[8,1,1024]{2,1,0:T(1,128)S(1)}, f32[8,1,1024]{2,1,0:T(1,128)S(1)}, u32[]{:S(2)}, u32[]{:S(2)}) collective-permute-start(f32[8,1,1024]{2,1,0:T(1,128)S(1)} %get-tuple-element.58), channel_id=1, source_target_pairs={{1,0},{2,1},{3,2},{5,4},{6,5},{7,6},{9,8},{10,9},{11,10},{13,12},{... | collective-permute-start | bytes 98312 | tf_op jit(solution)/shard_map/ppermute | solution.py:19
  70.0 7.0 %collective-permute-start.7 = (f32[8,1,1024]{2,1,0:T(1,128)S(1)}, f32[8,1,1024]{2,1,0:T(1,128)S(1)}, u32[]{:S(2)}, u32[]{:S(2)}) collective-permute-start(f32[8,1,1024]{2,1,0:T(1,128)S(1)} %get-tuple-element.57), channel_id=1, source_target_pairs={{0,1},{1,2},{2,3},{4,5},{5,6},{6,7},{8,9},{9,10},{10,11},{12,13},{... | collective-permute-start | bytes 98312 | tf_op jit(solution)/shard_map/ppermute | solution.py:18
  88.5 10.6 %copy-start.1 = (f32[8,64,1024]{2,1,0:T(8,128)}, f32[8,64,1024]{2,1,0:T(8,128)S(1)}, u32[]{:S(2)}) copy-start(f32[8,64,1024]{2,1,0:T(8,128)S(1)} %fusion.56) | copy-start | bytes 6291460
  92.3 6.7 %collective-permute-start.8 = (f32[8,1,1024]{2,1,0:T(1,128)S(1)}, f32[8,1,1024]{2,1,0:T(1,128)S(1)}, u32[]{:S(2)}, u32[]{:S(2)}) collective-permute-start(f32[8,1,1024]{2,1,0:T(1,128)S(1)} %get-tuple-element.52), channel_id=1, source_target_pairs={{1,0},{2,1},{3,2},{5,4},{6,5},{7,6},{9,8},{10,9},{11,10},{13,12},{... | collective-permute-start | bytes 98312 | tf_op jit(solution)/shard_map/ppermute | solution.py:19
  94.2 4.8 %collective-permute-start.9 = (f32[8,1,1024]{2,1,0:T(1,128)S(1)}, f32[8,1,1024]{2,1,0:T(1,128)S(1)}, u32[]{:S(2)}, u32[]{:S(2)}) collective-permute-start(f32[8,1,1024]{2,1,0:T(1,128)S(1)} %get-tuple-element.51), channel_id=1, source_target_pairs={{0,1},{1,2},{2,3},{4,5},{5,6},{6,7},{8,9},{9,10},{10,11},{12,13},{... | collective-permute-start | bytes 98312 | tf_op jit(solution)/shard_map/ppermute | solution.py:18
  99.1 11.2 %copy-start.23 = (f32[32,64]{1,0:T(8,128)S(1)}, f32[32,64]{1,0:T(8,128)}, u32[]{:S(2)}) copy-start(f32[32,64]{1,0:T(8,128)} %param.22) | copy-start | bytes 24580
  113.8 14.2 %copy-start.13 = (f32[8,32,128]{2,1,0:T(8,128)S(1)}, f32[8,32,128]{2,1,0:T(8,128)}, u32[]{:S(2)}) copy-start(f32[8,32,128]{2,1,0:T(8,128)} %param.24) | copy-start | bytes 393220
  115.2 22.6 %all-to-all-start = ((f32[32,1,1536]{2,1,0:T(1,128)}), f32[32,1,1536]{2,1,0:T(1,128)S(1)}, u32[]{:S(2)}, u32[]{:S(2)}) async-start(f32[32,1,1536]{2,1,0:T(1,128)} %reshape.92), calls=%async_computation | async-start | bytes 393216 | tf_op jit(solution)/shard_map/all_to_all | solution.py:120
  140.6 8.6 %collective-permute-start.11 = (f32[3,3,32,128]{3,2,1,0:T(8,128)S(1)}, f32[3,3,32,128]{3,2,1,0:T(8,128)S(1)}, u32[]{:S(2)}, u32[]{:S(2)}) collective-permute-start(f32[3,3,32,128]{3,2,1,0:T(8,128)S(1)} %get-tuple-element.72), channel_id=1, source_target_pairs={{4,0},{8,4},{12,8},{16,12},{20,16},{24,20},{28,24},{32,28},{36,32}... | collective-permute-start | bytes 442376 | tf_op jit(solution)/shard_map/ppermute | solution.py:137
  141.9 8.1 %collective-permute-start.10 = (f32[3,3,32,128]{3,2,1,0:T(8,128)S(1)}, f32[3,3,32,128]{3,2,1,0:T(8,128)S(1)}, u32[]{:S(2)}, u32[]{:S(2)}) collective-permute-start(f32[3,3,32,128]{3,2,1,0:T(8,128)S(1)} %get-tuple-element.71), channel_id=1, source_target_pairs={{0,4},{4,8},{8,12},{12,16},{16,20},{20,24},{24,28},{28,32},{32,36}... | collective-permute-start | bytes 442376 | tf_op jit(solution)/shard_map/ppermute | solution.py:136
  150.1 7.9 %collective-permute-start.13 = (f32[3,14,8,128]{3,2,1,0:T(8,128)S(1)}, f32[3,14,8,128]{3,2,1,0:T(8,128)S(1)}, u32[]{:S(2)}, u32[]{:S(2)}) collective-permute-start(f32[3,14,8,128]{3,2,1,0:T(8,128)S(1)} %get-tuple-element.70), channel_id=1, source_target_pairs={{1,0},{2,1},{3,2},{5,4},{6,5},{7,6},{9,8},{10,9},{11,10},{13,12},{... | collective-permute-start | bytes 516104 | tf_op jit(solution)/shard_map/ppermute | solution.py:137
  153.4 5.8 %collective-permute-start.12 = (f32[3,14,8,128]{3,2,1,0:T(8,128)S(1)}, f32[3,14,8,128]{3,2,1,0:T(8,128)S(1)}, u32[]{:S(2)}, u32[]{:S(2)}) collective-permute-start(f32[3,14,8,128]{3,2,1,0:T(8,128)S(1)} %get-tuple-element.69), channel_id=1, source_target_pairs={{0,1},{1,2},{2,3},{4,5},{5,6},{6,7},{8,9},{9,10},{10,11},{12,13},{... | collective-permute-start | bytes 516104 | tf_op jit(solution)/shard_map/ppermute | solution.py:136
  163.7 30.8 %copy-start.11 = (f32[1,8,32,6]{3,2,1,0:T(8,128)S(1)}, f32[1,8,32,6]{3,2,1,0:T(8,128)}, u32[]{:S(2)}) copy-start(f32[1,8,32,6]{3,2,1,0:T(8,128)} %get-tuple-element.84) | copy-start | bytes 18436
  196.0 9.7 %copy-start.14 = (f32[1,8,32,6]{2,1,3,0:T(8,128)S(1)}, f32[1,8,32,6]{2,1,3,0:T(8,128)}, u32[]{:S(2)}) copy-start(f32[1,8,32,6]{2,1,3,0:T(8,128)} %copy.73) | copy-start | bytes 18436
  (18 other events, 110.9 us)
where the time goes:
time: 234 us; the launch traced here: 230 us
  local copies, waits for them, and re-layouts  59.4 us (25%)
  other arithmetic  59.4 us (25%)
  starting transfers between devices  58.3 us (25%)
  waiting for transfers between devices  25.8 us (11%)
  blocking collectives  17.6 us (8%)
  matrix products  8.31 us (4%)
    another operation x36, local copies, waits for them, and re-layouts, per_device(): jnp.stack([padded_warm[..., ratio * s:ratio * s + BAND] for s in range(sl...  36.2 us
    ppermute x5, starting transfers between devices, face_halos(): lax.ppermute(lax.slice_in_dim(block, size - 1, size, axis=dim), axis, for...  23.6 us
    div x2, other arithmetic, sweep(): return fraction_top_quantity / denominator_quantity  21.7 us
    all_to_all x1, blocking collectives, per_device(): got_warm = lax.all_to_all(windows, 'slab', 0, 0, tiled=False)  17.6 us
    all_to_all x1, starting transfers between devices, per_device(): got = lax.all_to_all(piece, 'slab', 0, 0, tiled=False)  12.8 us
    another operation x6, other arithmetic, per_device(): both = jnp.stack([effective, initial_electrons])  11.6 us
    unnamed x91, local copies, waits for them, and re-layouts  11.5 us
    mul x1, other arithmetic, per_device(): joule_power_input = 0.5 * joule_power_input  11.2 us
  transfers between devices with their start and end apart: 15, of which 6 were waited for; matrix products, arithmetic and copies ran while one was open for 9% of the time, Pallas kernels for 0%

commit v1 on v0

--- a/solution.py
+++ b/solution.py
@@ -164,16 +164,18 @@
         warm = jnp.where(inside, total / scale_ext, 0.0)
     warming_distribution = warm[depths[0] : depths[0] + tc, depths[1] : depths[1] + tb]
 
-    padded_warm = jnp.pad(warming_distribution, ((0, 0), (0, 0), (1, 1)))
-    windows = jnp.stack(
-        [padded_warm[..., ratio * s : ratio * s + BAND] for s in range(slabs)]
-    )
+    a_count = warming_distribution.shape[2]
+    pick = (
+        lax.broadcasted_iota(jnp.int32, (slabs, BAND, a_count), 2)
+        == lax.broadcasted_iota(jnp.int32, (slabs, BAND, a_count), 0) * ratio
+        + lax.broadcasted_iota(jnp.int32, (slabs, BAND, a_count), 1)
+        - 1
+    ).astype(jnp.float32)
+    windows = jnp.einsum("ska,cba->skcb", pick, warming_distribution, precision=upper_limit)
     got_warm = lax.all_to_all(windows, "slab", 0, 0, tiled=False)
-    got_warm = got_warm.reshape(slabs * chunk_c, got_warm.shape[2], BAND)
-    spread = jnp.einsum("cta,ax->ctx", got_warm, columns, precision=upper_limit)
-    raised_field = jnp.einsum(
-        "ctx,cz->xtz", spread, restrict_matrix_third, precision=upper_limit
-    )
+    spread = jnp.einsum("skcb,kx->scbx", got_warm, columns, precision=upper_limit)
+    third = restrict_matrix_third.reshape(slabs, chunk_c, restrict_matrix_third.shape[1])
+    raised_field = jnp.einsum("scbx,scz->xbz", spread, third, precision=upper_limit)
     fine_mesh_warming = 16.0 * jnp.einsum(
         "hc,qhk->qck", restrict_matrix_second, raised_field, precision=upper_limit
     )

time: 234 us -> 189 us (0.81)
  local copies, waits for them, and re-layouts: 59.4 us -> 14.3 us
    another operation x36 -> x0, local copies, waits for them, and re-layouts: 36.2 us -> none  [per_device(): jnp.stack([padded_warm[..., ratio * s:ratio * s + BAND] for s in range(sl...]
    unnamed x91 -> x34, local copies, waits for them, and re-layouts: 11.5 us -> 2.5 us
  transfers between devices with their start and end apart: 15 -> 15, of which waited for: 6 -> 6; matrix products, arithmetic and copies ran while one was open for 9% -> 11% of each run, Pallas kernels for 0% -> 0%
where the time goes in v1:
time: 189 us; the launch traced here: 187 us
  other arithmetic  59.5 us (31%)
  starting transfers between devices  58.2 us (31%)
  waiting for transfers between devices  25.8 us (14%)
  blocking collectives  17.6 us (9%)
  local copies, waits for them, and re-layouts  14.3 us (8%)
  matrix products  10.6 us (6%)
    ppermute x5, starting transfers between devices, face_halos(): lax.ppermute(lax.slice_in_dim(block, size - 1, size, axis=dim), axis, for...  23.6 us
    div x2, other arithmetic, sweep(): return fraction_top_quantity / denominator_quantity  21.7 us
    all_to_all x1, blocking collectives, per_device(): got_warm = lax.all_to_all(windows, 'slab', 0, 0, tiled=False)  17.6 us
    all_to_all x1, starting transfers between devices, per_device(): got = lax.all_to_all(piece, 'slab', 0, 0, tiled=False)  12.8 us
    another operation x6, other arithmetic, per_device(): both = jnp.stack([effective, initial_electrons])  11.5 us
    ppermute x5, waiting for transfers between devices, face_halos(): high = lax.ppermute(lax.slice_in_dim(block, 0, 1, axis=dim), axis, backward)  11.3 us
    mul x1, other arithmetic, per_device(): joule_power_input = 0.5 * joule_power_input  11.2 us
    all_to_all x1, waiting for transfers between devices, per_device(): got = lax.all_to_all(piece, 'slab', 0, 0, tiled=False)  9.74 us
  transfers between devices with their start and end apart: 15, of which 6 were waited for; matrix products, arithmetic and copies ran while one was open for 11% of the time, Pallas kernels for 0%

profile of v1, /device:TPU:1, one launch (start us, length us, event | category | flops | bytes accessed | tf_op | source)
XLA Modules:
  0.0 187.2 jit_solution(5008010718317810093)
XLA Ops:
  2.0 5.7 %select_add_fusion = f32[8,64,1024]{2,1,0:T(8,128)S(1)} fusion(f32[8,64,1024]{2,1,0:T(8,128)} %param.15, s32[8,64,1024]{2,1,0:T(8,128)} %param.19, f32[]{:T(128)} %bitcast.3, f32[]{:T(128)} %bitcast.2, f32[]{:T(128)} %bitcast.1, f32[]{:T(128)} %bitcast), kind=kLoop, calls=%fused_computation.124 | loop fusion | flops 6291456 | bytes 6291472 | tf_op jit(solution)/shard_map/add | solution.py:64
  7.8 4.5 %collective-permute-start.3 = (f32[2,8,1,1024]{3,2,1,0:T(1,128)S(1)}, f32[2,8,1,1024]{3,2,1,0:T(1,128)S(1)}, u32[]{:S(2)}, u32[]{:S(2)}) collective-permute-start(f32[2,8,1,1024]{3,2,1,0:T(1,128)S(1)} %get-tuple-element.41), channel_id=1, source_target_pairs={{0,1},{1,2},{2,3},{4,5},{5,6},{6,7},{8,9},{9,10},{10,11},{12,13},{... | collective-permute-start | bytes 196616 | tf_op jit(solution)/shard_map/ppermute | solution.py:18
  15.3 5.1 %collective-permute-start.1 = (f32[2,1,64,1024]{3,2,1,0:T(8,128)}, f32[2,1,64,1024]{3,2,1,0:T(8,128)}, u32[]{:S(2)}, u32[]{:S(2)}) collective-permute-start(f32[2,1,64,1024]{3,2,1,0:T(8,128)} %get-tuple-element.37), channel_id=1, source_target_pairs={{0,4},{4,8},{8,12},{12,16},{16,20},{20,24},{24,28},{28,32},{32,36}... | collective-permute-start | bytes 1572872 | tf_op jit(solution)/shard_map/ppermute | solution.py:18
  21.7 3.1 %fusion = f32[2,8,64,1023]{3,2,1,0:T(8,128)} fusion(f32[1,8,64,1024]{3,2,1,0:T(8,128)S(1)} %bitcast.213, f32[1,8,64,1024]{3,2,1,0:T(8,128)S(1)} %bitcast.220), kind=kLoop, calls=%fused_computation.18 | loop fusion | flops 1047552 | bytes 8384512 | tf_op jit(solution)/shard_map/stack | solution.py:68
  24.9 3.2 %fusion.3 = (f32[2,7,64,1024]{3,2,1,0:T(8,128)}, f32[2,7,64,1024]{3,2,1,0:T(8,128)}) fusion(f32[1,8,64,1024]{3,2,1,0:T(8,128)S(1)} %bitcast.214, f32[1,8,64,1024]{3,2,1,0:T(8,128)S(1)} %bitcast.221), kind=kLoop, calls=%fused_computation.33 | loop fusion | flops 1835008 | bytes 11534336 | tf_op jit(solution)/shard_map/stack | solution.py:68
  28.2 2.9 %select_maximum_fusion = f32[2,8,64,1024]{3,2,1,0:T(8,128)S(1)} fusion(f32[1,8,64,1024]{3,2,1,0:T(8,128)} %bitcast.217, f32[1,8,64,1024]{3,2,1,0:T(8,128)S(1)} %bitcast.215), kind=kLoop, calls=%fused_computation.21 | loop fusion | flops 4194304 | bytes 8388608 | tf_op jit(solution)/shard_map/stack | solution.py:68
  32.2 11.3 %collective-permute-done = f32[2,1,64,1024]{3,2,1,0:T(8,128)} collective-permute-done((f32[2,1,64,1024]{3,2,1,0:T(8,128)}, f32[2,1,64,1024]{3,2,1,0:T(8,128)}, u32[]{:S(2)}, u32[]{:S(2)}) %collective-permute-start) | collective-permute-done | bytes 524320 | tf_op jit(solution)/shard_map/ppermute | solution.py:19
  43.5 4.8 %fusion.11 = (f32[8,64,1024]{2,1,0:T(8,128)}, f32[8,64,1024]{2,1,0:T(8,128)S(1)}, f32[8,64,1024]{2,1,0:T(8,128)}, f32[8,64,1024]{2,1,0:T(8,128)S(1)}) fusion(f32[8,64,1024]{2,1,0:T(8,128)S(1)} %select_add_fusion, f32[2,1,64,1024]{3,2,1,0:T(8,128)} %collective-permute-done, f32[2,7,64,1024]{3,2,1,0:T(8,128)S(1)} %copy-done.5, ...), kind=kLoop, calls=%fused_computation.47 | loop fusion | flops 9437184 | bytes 18874368 | tf_op jit(solution)/shard_map/jit(_where)/select_n | solution.py:42
  48.4 10.2 %fusion.23 = f32[8,64,1024]{2,1,0:T(8,128)S(1)} fusion(f32[2,8,64,1023]{3,2,1,0:T(8,128)S(1)} %copy-done.4, f32[2,8,64,1024]{3,2,1,0:T(8,128)S(1)} %select_maximum_fusion, f32[2,8,63,1024]{3,2,1,0:T(8,128)S(1)} %get-tuple-element.39, f32[2,8,1,1024]{3,2,1,0:T(1,128)S(1)} %collective-permute-done.3, f32[2,8,1,1024]{3,2,1,0:T(1,128)S(1)} %collective-permute-done.2, ...), kind=kLoop, calls=%fused_computation.59 | loop fusion | flops 40370176 | bytes 37744640 | tf_op jit(solution)/shard_map/div | solution.py:82
  62.5 5.5 %collective-permute-start.5 = (f32[1,64,1024]{2,1,0:T(8,128)S(1)}, f32[1,64,1024]{2,1,0:T(8,128)S(1)}, u32[]{:S(2)}, u32[]{:S(2)}) collective-permute-start(f32[1,64,1024]{2,1,0:T(8,128)S(1)} %get-tuple-element.58), channel_id=1, source_target_pairs={{0,4},{4,8},{8,12},{12,16},{16,20},{20,24},{24,28},{28,32},{32,36}... | collective-permute-start | bytes 786440 | tf_op jit(solution)/shard_map/ppermute | solution.py:18
  70.0 4.8 %collective-permute-start.7 = (f32[8,1,1024]{2,1,0:T(1,128)S(1)}, f32[8,1,1024]{2,1,0:T(1,128)S(1)}, u32[]{:S(2)}, u32[]{:S(2)}) collective-permute-start(f32[8,1,1024]{2,1,0:T(1,128)S(1)} %get-tuple-element.54), channel_id=1, source_target_pairs={{0,1},{1,2},{2,3},{4,5},{5,6},{6,7},{8,9},{9,10},{10,11},{12,13},{... | collective-permute-start | bytes 98312 | tf_op jit(solution)/shard_map/ppermute | solution.py:18
  74.8 2.2 %fusion.137 = (f32[7,64,1024]{2,1,0:T(8,128)}, f32[7,64,1024]{2,1,0:T(8,128)}) fusion(f32[8,64,1024]{2,1,0:T(8,128)S(1)} %fusion.23), kind=kLoop, calls=%fused_computation.243 | loop fusion | bytes 7340032 | tf_op jit(solution)/shard_map/slice | solution.py:30
  77.0 11.4 %fusion.56 = f32[8,64,1024]{2,1,0:T(8,128)S(1)} fusion(f32[8,64,1024]{2,1,0:T(8,128)S(1)} %copy-done.7, f32[1,64,1024]{2,1,0:T(8,128)S(1)} %collective-permute-done.4, f32[7,64,1024]{2,1,0:T(8,128)} %get-tuple-element.61, f32[7,64,1024]{2,1,0:T(8,128)} %get-tuple-element.60, f32[1,64,1024]{2,1,0:T(8,128)S(1)} %collective-permute-done.5, ...), kind=kLoop, calls=%fused_computation.99 | loop fusion | flops 40370176 | bytes 39837696 | tf_op jit(solution)/shard_map/div | solution.py:82
  90.0 2.3 %fusion.129 = (f32[7,64,1024]{2,1,0:T(8,128)}, f32[7,64,1024]{2,1,0:T(8,128)}) fusion(f32[8,64,1024]{2,1,0:T(8,128)S(1)} %fusion.56), kind=kLoop, calls=%fused_computation.235 | loop fusion | bytes 7340032 | tf_op jit(solution)/shard_map/slice | solution.py:29
  94.2 3.6 %collective-permute-start.9 = (f32[8,1,1024]{2,1,0:T(1,128)S(1)}, f32[8,1,1024]{2,1,0:T(1,128)S(1)}, u32[]{:S(2)}, u32[]{:S(2)}) collective-permute-start(f32[8,1,1024]{2,1,0:T(1,128)S(1)} %get-tuple-element.48), channel_id=1, source_target_pairs={{0,1},{1,2},{2,3},{4,5},{5,6},{6,7},{8,9},{9,10},{10,11},{12,13},{... | collective-permute-start | bytes 98312 | tf_op jit(solution)/shard_map/ppermute | solution.py:18
  99.1 11.2 %fusion.63 = f32[8,64,1024]{2,1,0:T(8,128)S(1)} fusion(f32[8,1,1024]{2,1,0:T(1,128)S(1)} %collective-permute-done.8, f32[8,63,1024]{2,1,0:T(8,128)S(1)} %get-tuple-element.51, f32[8,63,1024]{2,1,0:T(8,128)S(1)} %get-tuple-element.50, f32[8,1,1024]{2,1,0:T(1,128)S(1)} %collective-permute-done.9, f32[8,64,1024]{2,1,0:T(8,128)S(1)} %fusion.56, ...), kind=kLoop, calls=%fused_computation.110 | loop fusion | flops 45088768 | bytes 37216256 | tf_op jit(solution)/shard_map/mul | solution.py:100
  115.1 12.8 %all-to-all-start = ((f32[32,1,1536]{2,1,0:T(1,128)}), f32[32,1,1536]{2,1,0:T(1,128)S(1)}, u32[]{:S(2)}, u32[]{:S(2)}) async-start(f32[32,1,1536]{2,1,0:T(1,128)} %reshape.96), calls=%async_computation | async-start | bytes 393216 | tf_op jit(solution)/shard_map/all_to_all | solution.py:120
  128.0 9.7 %all-to-all-done = f32[32,1,1536]{2,1,0:T(1,128)S(1)} async-done(((f32[32,1,1536]{2,1,0:T(1,128)}), f32[32,1,1536]{2,1,0:T(1,128)S(1)}, u32[]{:S(2)}, u32[]{:S(2)}) %all-to-all-start) | async-done | bytes 196640 | tf_op jit(solution)/shard_map/all_to_all | solution.py:120
  141.9 5.5 %collective-permute-start.10 = (f32[3,3,32,128]{3,2,1,0:T(8,128)S(1)}, f32[3,3,32,128]{3,2,1,0:T(8,128)S(1)}, u32[]{:S(2)}, u32[]{:S(2)}) collective-permute-start(f32[3,3,32,128]{3,2,1,0:T(8,128)S(1)} %get-tuple-element.70), channel_id=1, source_target_pairs={{0,4},{4,8},{8,12},{12,16},{16,20},{20,24},{24,28},{28,32},{32,36}... | collective-permute-start | bytes 442376 | tf_op jit(solution)/shard_map/ppermute | solution.py:136
  150.0 3.3 %collective-permute-start.13 = (f32[3,14,8,128]{3,2,1,0:T(8,128)S(1)}, f32[3,14,8,128]{3,2,1,0:T(8,128)S(1)}, u32[]{:S(2)}, u32[]{:S(2)}) collective-permute-start(f32[3,14,8,128]{3,2,1,0:T(8,128)S(1)} %get-tuple-element.69), channel_id=1, source_target_pairs={{1,0},{2,1},{3,2},{5,4},{6,5},{7,6},{9,8},{10,9},{11,10},{13,12},{... | collective-permute-start | bytes 516104 | tf_op jit(solution)/shard_map/ppermute | solution.py:137
  153.3 3.4 %collective-permute-start.12 = (f32[3,14,8,128]{3,2,1,0:T(8,128)S(1)}, f32[3,14,8,128]{3,2,1,0:T(8,128)S(1)}, u32[]{:S(2)}, u32[]{:S(2)}) collective-permute-start(f32[3,14,8,128]{3,2,1,0:T(8,128)S(1)} %get-tuple-element.68), channel_id=1, source_target_pairs={{0,1},{1,2},{2,3},{4,5},{5,6},{6,7},{8,9},{9,10},{10,11},{12,13},{... | collective-permute-start | bytes 516104 | tf_op jit(solution)/shard_map/ppermute | solution.py:136
  161.6 17.6 %all_to_all.10 = f32[32,1,1536]{2,1,0:T(1,128)S(1)} all-to-all(f32[32,1,1536]{2,1,0:T(1,128)S(1)} %reshape.98), channel_id=1, replica_groups=mesh['slab'=32,'gy'=4] {'slab'}, dimensions={0} | all-to-all | bytes 393216 | tf_op jit(solution)/shard_map/all_to_all | solution.py:175
  181.7 2.1 %convolution_bitcast_fusion = f32[8,32,1024]{2,1,0:T(8,128)S(1)} fusion(f32[256,1024]{1,0:T(8,128)S(1)} %copy-done, f32[32,8,32,8]{2,3,1,0:T(8,128)S(1)} %fusion.72), kind=kOutput, calls=%fused_computation.144 | convolution fusion | flops 805306368 | bytes 2359296 | tf_op jit(solution)/shard_map/scbx,scz->xbz/dot_general | solution.py:178
  183.8 3.3 %multiply_bitcast_fusion = f32[8,64,1024]{2,1,0:T(8,128)} fusion(f32[8,32,1024]{2,1,0:T(8,128)S(1)} %convolution_bitcast_fusion, f32[32,64]{1,0:T(8,128)S(1)} %copy-done.13), kind=kOutput, calls=%fused_computation.114 | convolution fusion | flops 201850880 | bytes 3153920 | tf_op jit(solution)/shard_map/hc,qhk->qck/dot_general | solution.py:179
  (95 shorter events, 36.1 us)
Async XLA Ops:
  0.6 111.2 %copy-start = (f32[256,1024]{1,0:T(8,128)S(1)}, f32[256,1024]{1,0:T(8,128)}, u32[]{:S(2)}) copy-start(f32[256,1024]{1,0:T(8,128)} %param.23) | copy-start | bytes 3145732
  2.0 5.7 %copy-start.2 = (f32[8,64,1024]{2,1,0:T(8,128)S(1)}, f32[8,64,1024]{2,1,0:T(8,128)}, u32[]{:S(2)}) copy-start(f32[8,64,1024]{2,1,0:T(8,128)} %param.16) | copy-start | bytes 6291460
  7.8 40.5 %collective-permute-start.3 = (f32[2,8,1,1024]{3,2,1,0:T(1,128)S(1)}, f32[2,8,1,1024]{3,2,1,0:T(1,128)S(1)}, u32[]{:S(2)}, u32[]{:S(2)}) collective-permute-start(f32[2,8,1,1024]{3,2,1,0:T(1,128)S(1)} %get-tuple-element.41), channel_id=1, source_target_pairs={{0,1},{1,2},{2,3},{4,5},{5,6},{6,7},{8,9},{9,10},{10,11},{12,13},{... | collective-permute-start | bytes 196616 | tf_op jit(solution)/shard_map/ppermute | solution.py:18
  12.3 36.0 %collective-permute-start.2 = (f32[2,8,1,1024]{3,2,1,0:T(1,128)S(1)}, f32[2,8,1,1024]{3,2,1,0:T(1,128)S(1)}, u32[]{:S(2)}, u32[]{:S(2)}) collective-permute-start(f32[2,8,1,1024]{3,2,1,0:T(1,128)S(1)} %get-tuple-element.40), channel_id=1, source_target_pairs={{1,0},{2,1},{3,2},{5,4},{6,5},{7,6},{9,8},{10,9},{11,10},{13,12},{... | collective-permute-start | bytes 196616 | tf_op jit(solution)/shard_map/ppermute | solution.py:19
  15.3 16.9 %collective-permute-start.1 = (f32[2,1,64,1024]{3,2,1,0:T(8,128)}, f32[2,1,64,1024]{3,2,1,0:T(8,128)}, u32[]{:S(2)}, u32[]{:S(2)}) collective-permute-start(f32[2,1,64,1024]{3,2,1,0:T(8,128)} %get-tuple-element.37), channel_id=1, source_target_pairs={{0,4},{4,8},{8,12},{12,16},{16,20},{20,24},{24,28},{28,32},{32,36}... | collective-permute-start | bytes 1572872 | tf_op jit(solution)/shard_map/ppermute | solution.py:18
  20.5 23.0 %collective-permute-start = (f32[2,1,64,1024]{3,2,1,0:T(8,128)}, f32[2,1,64,1024]{3,2,1,0:T(8,128)}, u32[]{:S(2)}, u32[]{:S(2)}) collective-permute-start(f32[2,1,64,1024]{3,2,1,0:T(8,128)} %get-tuple-element.36), channel_id=1, source_target_pairs={{4,0},{8,4},{12,8},{16,12},{20,16},{24,20},{28,24},{32,28},{36,32}... | collective-permute-start | bytes 1572872 | tf_op jit(solution)/shard_map/ppermute | solution.py:19
  31.1 12.4 %copy-start.5 = (f32[2,7,64,1024]{3,2,1,0:T(8,128)S(1)}, f32[2,7,64,1024]{3,2,1,0:T(8,128)}, u32[]{:S(2)}) copy-start(f32[2,7,64,1024]{3,2,1,0:T(8,128)} %get-tuple-element.34) | copy-start | bytes 11010052
  31.1 12.4 %copy-start.6 = (f32[2,7,64,1024]{3,2,1,0:T(8,128)S(1)}, f32[2,7,64,1024]{3,2,1,0:T(8,128)}, u32[]{:S(2)}) copy-start(f32[2,7,64,1024]{3,2,1,0:T(8,128)} %get-tuple-element.35) | copy-start | bytes 11010052
  43.5 4.9 %copy-start.8 = (f32[8,64,1024]{2,1,0:T(8,128)S(1)}, f32[8,64,1024]{2,1,0:T(8,128)}, u32[]{:S(2)}) copy-start(f32[8,64,1024]{2,1,0:T(8,128)} %param.18) | copy-start | bytes 6291460
  61.3 15.8 %collective-permute-start.4 = (f32[1,64,1024]{2,1,0:T(8,128)S(1)}, f32[1,64,1024]{2,1,0:T(8,128)S(1)}, u32[]{:S(2)}, u32[]{:S(2)}) collective-permute-start(f32[1,64,1024]{2,1,0:T(8,128)S(1)} %get-tuple-element.59), channel_id=1, source_target_pairs={{4,0},{8,4},{12,8},{16,12},{20,16},{24,20},{28,24},{32,28},{36,32}... | collective-permute-start | bytes 786440 | tf_op jit(solution)/shard_map/ppermute | solution.py:19
  62.5 14.5 %collective-permute-start.5 = (f32[1,64,1024]{2,1,0:T(8,128)S(1)}, f32[1,64,1024]{2,1,0:T(8,128)S(1)}, u32[]{:S(2)}, u32[]{:S(2)}) collective-permute-start(f32[1,64,1024]{2,1,0:T(8,128)S(1)} %get-tuple-element.58), channel_id=1, source_target_pairs={{0,4},{4,8},{8,12},{12,16},{16,20},{20,24},{24,28},{28,32},{32,36}... | collective-permute-start | bytes 786440 | tf_op jit(solution)/shard_map/ppermute | solution.py:18
  68.1 9.0 %collective-permute-start.6 = (f32[8,1,1024]{2,1,0:T(1,128)S(1)}, f32[8,1,1024]{2,1,0:T(1,128)S(1)}, u32[]{:S(2)}, u32[]{:S(2)}) collective-permute-start(f32[8,1,1024]{2,1,0:T(1,128)S(1)} %get-tuple-element.55), channel_id=1, source_target_pairs={{1,0},{2,1},{3,2},{5,4},{6,5},{7,6},{9,8},{10,9},{11,10},{13,12},{... | collective-permute-start | bytes 98312 | tf_op jit(solution)/shard_map/ppermute | solution.py:19
  70.0 7.0 %collective-permute-start.7 = (f32[8,1,1024]{2,1,0:T(1,128)S(1)}, f32[8,1,1024]{2,1,0:T(1,128)S(1)}, u32[]{:S(2)}, u32[]{:S(2)}) collective-permute-start(f32[8,1,1024]{2,1,0:T(1,128)S(1)} %get-tuple-element.54), channel_id=1, source_target_pairs={{0,1},{1,2},{2,3},{4,5},{5,6},{6,7},{8,9},{9,10},{10,11},{12,13},{... | collective-permute-start | bytes 98312 | tf_op jit(solution)/shard_map/ppermute | solution.py:18
  88.5 10.6 %copy-start.1 = (f32[8,64,1024]{2,1,0:T(8,128)}, f32[8,64,1024]{2,1,0:T(8,128)S(1)}, u32[]{:S(2)}) copy-start(f32[8,64,1024]{2,1,0:T(8,128)S(1)} %fusion.56) | copy-start | bytes 6291460
  92.3 6.7 %collective-permute-start.8 = (f32[8,1,1024]{2,1,0:T(1,128)S(1)}, f32[8,1,1024]{2,1,0:T(1,128)S(1)}, u32[]{:S(2)}, u32[]{:S(2)}) collective-permute-start(f32[8,1,1024]{2,1,0:T(1,128)S(1)} %get-tuple-element.49), channel_id=1, source_target_pairs={{1,0},{2,1},{3,2},{5,4},{6,5},{7,6},{9,8},{10,9},{11,10},{13,12},{... | collective-permute-start | bytes 98312 | tf_op jit(solution)/shard_map/ppermute | solution.py:19
  94.2 4.8 %collective-permute-start.9 = (f32[8,1,1024]{2,1,0:T(1,128)S(1)}, f32[8,1,1024]{2,1,0:T(1,128)S(1)}, u32[]{:S(2)}, u32[]{:S(2)}) collective-permute-start(f32[8,1,1024]{2,1,0:T(1,128)S(1)} %get-tuple-element.48), channel_id=1, source_target_pairs={{0,1},{1,2},{2,3},{4,5},{5,6},{6,7},{8,9},{9,10},{10,11},{12,13},{... | collective-permute-start | bytes 98312 | tf_op jit(solution)/shard_map/ppermute | solution.py:18
  99.1 11.2 %copy-start.13 = (f32[32,64]{1,0:T(8,128)S(1)}, f32[32,64]{1,0:T(8,128)}, u32[]{:S(2)}) copy-start(f32[32,64]{1,0:T(8,128)} %param.22) | copy-start | bytes 24580
  113.7 14.2 %copy-start.12 = (f32[8,32,128]{2,1,0:T(8,128)S(1)}, f32[8,32,128]{2,1,0:T(8,128)}, u32[]{:S(2)}) copy-start(f32[8,32,128]{2,1,0:T(8,128)} %param.24) | copy-start | bytes 393220
  115.1 22.6 %all-to-all-start = ((f32[32,1,1536]{2,1,0:T(1,128)}), f32[32,1,1536]{2,1,0:T(1,128)S(1)}, u32[]{:S(2)}, u32[]{:S(2)}) async-start(f32[32,1,1536]{2,1,0:T(1,128)} %reshape.96), calls=%async_computation | async-start | bytes 393216 | tf_op jit(solution)/shard_map/all_to_all | solution.py:120
  140.6 8.6 %collective-permute-start.11 = (f32[3,3,32,128]{3,2,1,0:T(8,128)S(1)}, f32[3,3,32,128]{3,2,1,0:T(8,128)S(1)}, u32[]{:S(2)}, u32[]{:S(2)}) collective-permute-start(f32[3,3,32,128]{3,2,1,0:T(8,128)S(1)} %get-tuple-element.71), channel_id=1, source_target_pairs={{4,0},{8,4},{12,8},{16,12},{20,16},{24,20},{28,24},{32,28},{36,32}... | collective-permute-start | bytes 442376 | tf_op jit(solution)/shard_map/ppermute | solution.py:137
  141.9 8.1 %collective-permute-start.10 = (f32[3,3,32,128]{3,2,1,0:T(8,128)S(1)}, f32[3,3,32,128]{3,2,1,0:T(8,128)S(1)}, u32[]{:S(2)}, u32[]{:S(2)}) collective-permute-start(f32[3,3,32,128]{3,2,1,0:T(8,128)S(1)} %get-tuple-element.70), channel_id=1, source_target_pairs={{0,4},{4,8},{8,12},{12,16},{16,20},{20,24},{24,28},{28,32},{32,36}... | collective-permute-start | bytes 442376 | tf_op jit(solution)/shard_map/ppermute | solution.py:136
  150.0 7.9 %collective-permute-start.13 = (f32[3,14,8,128]{3,2,1,0:T(8,128)S(1)}, f32[3,14,8,128]{3,2,1,0:T(8,128)S(1)}, u32[]{:S(2)}, u32[]{:S(2)}) collective-permute-start(f32[3,14,8,128]{3,2,1,0:T(8,128)S(1)} %get-tuple-element.69), channel_id=1, source_target_pairs={{1,0},{2,1},{3,2},{5,4},{6,5},{7,6},{9,8},{10,9},{11,10},{13,12},{... | collective-permute-start | bytes 516104 | tf_op jit(solution)/shard_map/ppermute | solution.py:137
  153.3 5.8 %collective-permute-start.12 = (f32[3,14,8,128]{3,2,1,0:T(8,128)S(1)}, f32[3,14,8,128]{3,2,1,0:T(8,128)S(1)}, u32[]{:S(2)}, u32[]{:S(2)}) collective-permute-start(f32[3,14,8,128]{3,2,1,0:T(8,128)S(1)} %get-tuple-element.68), channel_id=1, source_target_pairs={{0,1},{1,2},{2,3},{4,5},{5,6},{6,7},{8,9},{9,10},{10,11},{12,13},{... | collective-permute-start | bytes 516104 | tf_op jit(solution)/shard_map/ppermute | solution.py:136
  160.2 20.0 %copy-start.10 = (f32[8,32,128]{2,1,0:T(8,128)}, f32[8,32,128]{2,1,0:T(8,128)S(1)}, u32[]{:S(2)}) copy-start(f32[8,32,128]{2,1,0:T(8,128)S(1)} %fusion.100) | copy-start | bytes 393220
  (5 other events, 16.7 us)

commit v2 on v1

--- a/solution.py
+++ b/solution.py
@@ -18,6 +18,26 @@
         low = lax.ppermute(lax.slice_in_dim(block, size - 1, size, axis=dim), axis, forward)
         high = lax.ppermute(lax.slice_in_dim(block, 0, 1, axis=dim), axis, backward)
         halos.append((low, high))
+    return halos
+
+
+def face_halos_of(blocks, sides):
+    halos = [[] for _ in blocks]
+    for axis, dim in sides:
+        count = lax.axis_size(axis)
+        forward = [(i, i + 1) for i in range(count - 1)]
+        backward = [(i + 1, i) for i in range(count - 1)]
+        size = blocks[0].shape[dim]
+        low = lax.ppermute(
+            jnp.stack([lax.slice_in_dim(b, size - 1, size, axis=dim) for b in blocks]),
+            axis,
+            forward,
+        )
+        high = lax.ppermute(
+            jnp.stack([lax.slice_in_dim(b, 0, 1, axis=dim) for b in blocks]), axis, backward
+        )
+        for k in range(len(blocks)):
+            halos[k].append((low[k], high[k]))
     return halos
 
 
@@ -65,12 +85,12 @@
             crystal_orientation_class == grain, crystal_barrier_shift[grain], jnp.float32(0.0)
         )
     device_sides = (("slab", 0), ("gy", 1))
-    both = jnp.stack([effective, initial_electrons])
-    both_halos = face_halos(both, (("slab", 1), ("gy", 2)))
-    beside_both = neighbours_of(both, both_halos, lead=1)
-    beside_all = [b[0] for b in beside_both]
+    eff_halos, start_halos = face_halos_of([effective, initial_electrons], device_sides)
+    beside_all = neighbours_of(effective, eff_halos)
     voltage_gradients = [leftover_portion - effective for leftover_portion in beside_all]
-    bernoulli_coefficients = [bernoulli(voltage_gradient) for voltage_gradient in voltage_gradients]
+    bernoulli_coefficients = list(
+        lax.optimization_barrier(tuple(bernoulli(vg) for vg in voltage_gradients[:4]))
+    ) + [bernoulli(vg) for vg in voltage_gradients[4:]]
     denominator_quantity = annihilation_coefficient
     for bernoulli_coefficient, voltage_gradient in zip(bernoulli_coefficients, voltage_gradients):
         denominator_quantity = denominator_quantity + (bernoulli_coefficient + voltage_gradient)
@@ -81,7 +101,7 @@
             fraction_top_quantity = fraction_top_quantity + bernoulli_coefficient * leftover_portion
         return fraction_top_quantity / denominator_quantity
 
-    electron_concentration = sweep([b[1] for b in beside_both])
+    electron_concentration = sweep(neighbours_of(initial_electrons, start_halos))
     electron_concentration = sweep(
         neighbours_of(electron_concentration, face_halos(electron_concentration, device_sides))
     )

time: 189 us -> 227 us (1.20)
  local copies, waits for them, and re-layouts: 14.3 us -> 45.1 us
  other arithmetic: 59.5 us -> 71.1 us
  waiting for transfers between devices: 25.8 us -> 19.5 us
    slice x3 -> x7, local copies, waits for them, and re-layouts: 3.29 us -> 19.9 us  [neighbours_of(): lax.slice_in_dim(block, 0, size - 1, axis=dim)]
    ppermute x0 -> x4, starting transfers between devices: none -> 12.8 us  [the longest x2 9.66 us: face_halos_of(): lax.ppermute(jnp.stack([lax.slice_in_dim(b, size - 1, size, axis=dim) for...]
    ppermute x5 -> x3, waiting for transfers between devices: 11.3 us -> 0.01 us  [face_halos(): high = lax.ppermute(lax.slice_in_dim(block, 0, 1, axis=dim), axis, backward)]
    div x2, other arithmetic: 21.7 us -> 32.1 us  [sweep(): return fraction_top_quantity / denominator_quantity]
    ppermute x5 -> x3, starting transfers between devices: 23.6 us -> 14.2 us  [face_halos(): lax.ppermute(lax.slice_in_dim(block, size - 1, size, axis=dim), axis, for...]
    another operation x6 -> x4, other arithmetic: 11.5 us -> 2.46 us  [the longest x2 1.53 us: face_halos_of(): jnp.stack([lax.slice_in_dim(b, 0, 1, axis=dim) for b in blocks])]
    mul x1, other arithmetic: 11.2 us -> 16.6 us  [per_device(): joule_power_input = 0.5 * joule_power_input]
    ppermute x0 -> x4, waiting for transfers between devices: none -> 4.77 us  [the longest x2 4.77 us: face_halos_of(): lax.ppermute(jnp.stack([lax.slice_in_dim(b, 0, 1, axis=dim) for b in bloc...]
  transfers between devices with their start and end apart: 15 -> 15, of which waited for: 6 -> 6; matrix products, arithmetic and copies ran while one was open for 11% -> 10% of each run, Pallas kernels for 0% -> 0%
where the time goes in v2:
time: 227 us; the launch traced here: 225 us
  other arithmetic  71.1 us (31%)
  starting transfers between devices  58.3 us (26%)
  local copies, waits for them, and re-layouts  45.1 us (20%)
  waiting for transfers between devices  19.5 us (9%)
  blocking collectives  17.6 us (8%)
  matrix products  12.1 us (5%)
    div x2, other arithmetic, sweep(): return fraction_top_quantity / denominator_quantity  32.1 us
    slice x7, local copies, waits for them, and re-layouts, neighbours_of(): lax.slice_in_dim(block, 0, size - 1, axis=dim)  19.9 us
    all_to_all x1, blocking collectives, per_device(): got_warm = lax.all_to_all(windows, 'slab', 0, 0, tiled=False)  17.6 us
    mul x1, other arithmetic, per_device(): joule_power_input = 0.5 * joule_power_input  16.6 us
    ppermute x3, starting transfers between devices, face_halos(): lax.ppermute(lax.slice_in_dim(block, size - 1, size, axis=dim), axis, for...  14.2 us
    all_to_all x1, starting transfers between devices, per_device(): got = lax.all_to_all(piece, 'slab', 0, 0, tiled=False)  12.6 us
    all_to_all x1, waiting for transfers between devices, per_device(): got = lax.all_to_all(piece, 'slab', 0, 0, tiled=False)  9.97 us
    ppermute x2, starting transfers between devices, face_halos_of(): lax.ppermute(jnp.stack([lax.slice_in_dim(b, size - 1, size, axis=dim) for...  9.66 us
  transfers between devices with their start and end apart: 15, of which 6 were waited for; matrix products, arithmetic and copies ran while one was open for 10% of the time, Pallas kernels for 0%

profile of v2, /device:TPU:1, one launch (start us, length us, event | category | flops | bytes accessed | tf_op | source)
XLA Modules:
  0.0 224.8 jit_solution(12688381802619644983)
XLA Ops:
  3.2 5.7 %select_add_fusion = f32[8,64,1024]{2,1,0:T(8,128)S(1)} fusion(f32[8,64,1024]{2,1,0:T(8,128)} %param.15, s32[8,64,1024]{2,1,0:T(8,128)} %param.19, f32[]{:T(128)} %bitcast.3, f32[]{:T(128)} %bitcast.2, f32[]{:T(128)} %bitcast.1, f32[]{:T(128)} %bitcast), kind=kLoop, calls=%fused_computation.66 | loop fusion | flops 6291456 | bytes 6291472 | tf_op jit(solution)/shard_map/add | solution.py:84
  9.0 4.5 %collective-permute-start.3 = (f32[2,8,1,1024]{3,2,1,0:T(1,128)S(1)}, f32[2,8,1,1024]{3,2,1,0:T(1,128)S(1)}, u32[]{:S(2)}, u32[]{:S(2)}) collective-permute-start(f32[2,8,1,1024]{3,2,1,0:T(1,128)S(1)} %pad_maximum_fusion.12), channel_id=1, source_target_pairs={{0,1},{1,2},{2,3},{4,5},{5,6},{6,7},{8,9},{9,10},{10,11},{12,13},{... | collective-permute-start | bytes 196616 | tf_op jit(solution)/shard_map/ppermute | solution.py:31
  17.1 5.1 %collective-permute-start.1 = (f32[2,1,64,1024]{3,2,1,0:T(8,128)}, f32[2,1,64,1024]{3,2,1,0:T(8,128)}, u32[]{:S(2)}, u32[]{:S(2)}) collective-permute-start(f32[2,1,64,1024]{3,2,1,0:T(8,128)} %pad_maximum_fusion.2), channel_id=1, source_target_pairs={{0,4},{4,8},{8,12},{12,16},{16,20},{20,24},{24,28},{28,32},{32,36}... | collective-permute-start | bytes 1572872 | tf_op jit(solution)/shard_map/ppermute | solution.py:31
  33.9 4.6 %fusion.97 = (f32[8,64,1023]{2,1,0:T(8,128)}, f32[8,64,1023]{2,1,0:T(8,128)}, f32[8,64,1023]{2,1,0:T(8,128)}, f32[8,64,1023]{2,1,0:T(8,128)}) fusion(f32[8,64,1024]{2,1,0:T(8,128)S(1)} %select_add_fusion, f32[8,64,1024]{2,1,0:T(8,128)S(1)} %copy-done.3), kind=kLoop, calls=%fused_computation.196 | loop fusion | bytes 16760832 | tf_op jit(solution)/shard_map/slice | solution.py:55
  40.5 4.8 %collective-permute-done = f32[2,1,64,1024]{3,2,1,0:T(8,128)} collective-permute-done((f32[2,1,64,1024]{3,2,1,0:T(8,128)}, f32[2,1,64,1024]{3,2,1,0:T(8,128)}, u32[]{:S(2)}, u32[]{:S(2)}) %collective-permute-start) | collective-permute-done | bytes 524320 | tf_op jit(solution)/shard_map/ppermute | solution.py:36
  47.1 9.6 %fusion.9 = (f32[8,64,1024]{2,1,0:T(8,128)}, f32[8,64,1024]{2,1,0:T(8,128)}, f32[8,64,1024]{2,1,0:T(8,128)}, f32[8,64,1024]{2,1,0:T(8,128)}, f32[8,64,1024]{2,1,...) fusion(f32[8,64,1024]{2,1,0:T(8,128)S(1)} %select_add_fusion, ...), kind=kLoop, calls=%fused_computation.15 | loop fusion | flops 18874368 | bytes 27262976 | tf_op jit(solution)/shard_map/jit(_where)/select_n | solution.py:62
  56.6 18.7 %fusion.18 = (f32[8,64,1024]{2,1,0:T(8,128)}, f32[8,64,1024]{2,1,0:T(8,128)}, f32[8,64,1024]{2,1,0:T(8,128)}, f32[8,64,1024]{2,1,0:T(8,128)}, f32[8,64,1024]{2,1,0:T(8,128)}) fusion(f32[8,64,1024]{2,1,0:T(8,128)} %param.17, f32[8,64,1024]{2,1,0:T(8,128)} %get-tuple-element.31, f32[1,64,1024]{2,1,0:T(8,128)} %get-tuple-element.105, ...), kind=kLoop, calls=%fused_computation.29 | loop fusion | flops 23592960 | bytes 50323456 | tf_op jit(solution)/shard_map/div | solution.py:102
  77.5 5.2 %fusion.94 = (f32[8,63,1024]{2,1,0:T(8,128)}, f32[8,63,1024]{2,1,0:T(8,128)}) fusion(f32[8,64,1024]{2,1,0:T(8,128)} %get-tuple-element.38), kind=kLoop, calls=%fused_computation.193 | loop fusion | bytes 8257536 | tf_op jit(solution)/shard_map/slice | solution.py:50
  82.7 2.8 %fusion.92 = (f32[8,64,1023]{2,1,0:T(8,128)}, f32[8,64,1023]{2,1,0:T(8,128)}) fusion(f32[8,64,1024]{2,1,0:T(8,128)S(1)} %copy-done.2), kind=kLoop, calls=%fused_computation.191 | loop fusion | bytes 8380416 | tf_op jit(solution)/shard_map/slice | solution.py:54
  86.9 5.7 %collective-permute-start.5 = (f32[1,64,1024]{2,1,0:T(8,128)S(1)}, f32[1,64,1024]{2,1,0:T(8,128)S(1)}, u32[]{:S(2)}, u32[]{:S(2)}) collective-permute-start(f32[1,64,1024]{2,1,0:T(8,128)S(1)} %get-tuple-element.67), channel_id=1, source_target_pairs={{0,4},{4,8},{8,12},{12,16},{16,20},{20,24},{24,28},{28,32},{32,36}... | collective-permute-start | bytes 786440 | tf_op jit(solution)/shard_map/ppermute | solution.py:18
  94.5 4.9 %collective-permute-start.7 = (f32[8,1,1024]{2,1,0:T(1,128)S(1)}, f32[8,1,1024]{2,1,0:T(1,128)S(1)}, u32[]{:S(2)}, u32[]{:S(2)}) collective-permute-start(f32[8,1,1024]{2,1,0:T(1,128)S(1)} %get-tuple-element.63), channel_id=1, source_target_pairs={{0,1},{1,2},{2,3},{4,5},{5,6},{6,7},{8,9},{9,10},{10,11},{12,13},{... | collective-permute-start | bytes 98312 | tf_op jit(solution)/shard_map/ppermute | solution.py:18
  101.8 13.4 %fusion.25 = f32[8,64,1024]{2,1,0:T(8,128)S(1)} fusion(f32[8,64,1024]{2,1,0:T(8,128)} %param.17, f32[8,64,1024]{2,1,0:T(8,128)S(1)} %copy-done.5, f32[1,64,1024]{2,1,0:T(8,128)S(1)} %collective-permute-done.4, f32[7,64,1024]{2,1,0:T(8,128)} %get-tuple-element.70, f32[8,64,1024]{2,1,0:T(8,128)S(1)} %copy-done.4, f32[7,64,1024]{2,1,0:T(8,128)} %get-tuple-element.69, ...), kind=kLoop, calls=%fused_computation.40 | loop fusion | flops 21495808 | bytes 41934848 | tf_op jit(solution)/shard_map/div | solution.py:102
  115.3 2.7 %fusion.91 = (f32[8,63,1024]{2,1,0:T(8,128)}, f32[8,63,1024]{2,1,0:T(8,128)}) fusion(f32[8,64,1024]{2,1,0:T(8,128)S(1)} %fusion.25), kind=kLoop, calls=%fused_computation.190 | loop fusion | bytes 8257536 | tf_op jit(solution)/shard_map/slice | solution.py:50
  118.0 2.7 %fusion.89 = (f32[8,64,1023]{2,1,0:T(8,128)}, f32[8,64,1023]{2,1,0:T(8,128)}) fusion(f32[8,64,1024]{2,1,0:T(8,128)S(1)} %fusion.25), kind=kLoop, calls=%fused_computation.188 | loop fusion | bytes 8380416 | tf_op jit(solution)/shard_map/slice | solution.py:54
  125.0 3.6 %collective-permute-start.9 = (f32[8,1,1024]{2,1,0:T(1,128)S(1)}, f32[8,1,1024]{2,1,0:T(1,128)S(1)}, u32[]{:S(2)}, u32[]{:S(2)}) collective-permute-start(f32[8,1,1024]{2,1,0:T(1,128)S(1)} %get-tuple-element.57), channel_id=1, source_target_pairs={{0,1},{1,2},{2,3},{4,5},{5,6},{6,7},{8,9},{9,10},{10,11},{12,13},{... | collective-permute-start | bytes 98312 | tf_op jit(solution)/shard_map/ppermute | solution.py:18
  129.8 16.6 %fusion.32 = f32[8,64,1024]{2,1,0:T(8,128)} fusion(f32[8,64,1024]{2,1,0:T(8,128)} %get-tuple-element.80, f32[8,64,1024]{2,1,0:T(8,128)} %get-tuple-element.33, f32[8,1,1024]{2,1,0:T(1,128)S(1)} %collective-permute-done.8, f32[8,63,1024]{2,1,0:T(8,128)} %get-tuple-element.60, f32[8,64,1024]{2,1,0:T(8,128)} %get-tuple-element.44, ...), kind=kLoop, calls=%fused_computation.51 | loop fusion | flops 26214400 | bytes 47702016 | tf_op jit(solution)/shard_map/mul | solution.py:120
  146.4 3.1 %fusion.35 = f32[10,32,1024]{2,1,0:T(8,128)S(1)} fusion(f32[1,64,1024]{2,1,0:T(8,128)S(1)} %get-tuple-element.52, f32[8,64,1024]{2,1,0:T(8,128)} %fusion.32, f32[1,64,1024]{2,1,0:T(8,128)S(1)} %get-tuple-element.51, f32[32,64]{1,0:T(8,128)S(1)} %copy-done.12), kind=kOutput, calls=%fused_computation.85 | convolution fusion | flops 252968960 | bytes 3940352 | tf_op jit(solution)/shard_map/ty,xyz->xtz/dot_general | solution.py:133
  152.9 12.6 %all-to-all-start = ((f32[32,1,1536]{2,1,0:T(1,128)}), f32[32,1,1536]{2,1,0:T(1,128)S(1)}, u32[]{:S(2)}, u32[]{:S(2)}) async-start(f32[32,1,1536]{2,1,0:T(1,128)} %reshape.96), calls=%async_computation | async-start | bytes 393216 | tf_op jit(solution)/shard_map/all_to_all | solution.py:140
  165.5 10.0 %all-to-all-done = f32[32,1,1536]{2,1,0:T(1,128)S(1)} async-done(((f32[32,1,1536]{2,1,0:T(1,128)}), f32[32,1,1536]{2,1,0:T(1,128)S(1)}, u32[]{:S(2)}, u32[]{:S(2)}) %all-to-all-start) | async-done | bytes 196640 | tf_op jit(solution)/shard_map/all_to_all | solution.py:140
  179.6 5.5 %collective-permute-start.10 = (f32[3,3,32,128]{3,2,1,0:T(8,128)S(1)}, f32[3,3,32,128]{3,2,1,0:T(8,128)S(1)}, u32[]{:S(2)}, u32[]{:S(2)}) collective-permute-start(f32[3,3,32,128]{3,2,1,0:T(8,128)S(1)} %get-tuple-element.107), channel_id=1, source_target_pairs={{0,4},{4,8},{8,12},{12,16},{16,20},{20,24},{24,28},{28,32},{32,36}... | collective-permute-start | bytes 442376 | tf_op jit(solution)/shard_map/ppermute | solution.py:156
  187.7 3.3 %collective-permute-start.13 = (f32[3,14,8,128]{3,2,1,0:T(8,128)S(1)}, f32[3,14,8,128]{3,2,1,0:T(8,128)S(1)}, u32[]{:S(2)}, u32[]{:S(2)}) collective-permute-start(f32[3,14,8,128]{3,2,1,0:T(8,128)S(1)} %get-tuple-element.102), channel_id=1, source_target_pairs={{1,0},{2,1},{3,2},{5,4},{6,5},{7,6},{9,8},{10,9},{11,10},{13,12},{... | collective-permute-start | bytes 516104 | tf_op jit(solution)/shard_map/ppermute | solution.py:157
  191.1 3.4 %collective-permute-start.12 = (f32[3,14,8,128]{3,2,1,0:T(8,128)S(1)}, f32[3,14,8,128]{3,2,1,0:T(8,128)S(1)}, u32[]{:S(2)}, u32[]{:S(2)}) collective-permute-start(f32[3,14,8,128]{3,2,1,0:T(8,128)S(1)} %get-tuple-element.101), channel_id=1, source_target_pairs={{0,1},{1,2},{2,3},{4,5},{5,6},{6,7},{8,9},{9,10},{10,11},{12,13},{... | collective-permute-start | bytes 516104 | tf_op jit(solution)/shard_map/ppermute | solution.py:156
  199.3 17.6 %all_to_all.10 = f32[32,1,1536]{2,1,0:T(1,128)S(1)} all-to-all(f32[32,1,1536]{2,1,0:T(1,128)S(1)} %reshape.98), channel_id=1, replica_groups=mesh['slab'=32,'gy'=4] {'slab'}, dimensions={0} | all-to-all | bytes 393216 | tf_op jit(solution)/shard_map/all_to_all | solution.py:195
  221.5 3.3 %multiply_bitcast_fusion = f32[8,64,1024]{2,1,0:T(8,128)} fusion(f32[8,32,1024]{2,1,0:T(8,128)S(1)} %convolution_bitcast_fusion, f32[32,64]{1,0:T(8,128)S(1)} %copy-done.12), kind=kOutput, calls=%fused_computation.55 | convolution fusion | flops 201850880 | bytes 3153920 | tf_op jit(solution)/shard_map/hc,qhk->qck/dot_general | solution.py:199
  (104 shorter events, 54.1 us)
Async XLA Ops:
  0.6 148.9 %copy-start = (f32[256,1024]{1,0:T(8,128)S(1)}, f32[256,1024]{1,0:T(8,128)}, u32[]{:S(2)}) copy-start(f32[256,1024]{1,0:T(8,128)} %param.23) | copy-start | bytes 3145732
  3.1 13.0 %copy-start.3 = (f32[8,64,1024]{2,1,0:T(8,128)S(1)}, f32[8,64,1024]{2,1,0:T(8,128)}, u32[]{:S(2)}) copy-start(f32[8,64,1024]{2,1,0:T(8,128)} %param.16) | copy-start | bytes 6291460
  9.0 29.5 %collective-permute-start.3 = (f32[2,8,1,1024]{3,2,1,0:T(1,128)S(1)}, f32[2,8,1,1024]{3,2,1,0:T(1,128)S(1)}, u32[]{:S(2)}, u32[]{:S(2)}) collective-permute-start(f32[2,8,1,1024]{3,2,1,0:T(1,128)S(1)} %pad_maximum_fusion.12), channel_id=1, source_target_pairs={{0,1},{1,2},{2,3},{4,5},{5,6},{6,7},{8,9},{9,10},{10,11},{12,13},{... | collective-permute-start | bytes 196616 | tf_op jit(solution)/shard_map/ppermute | solution.py:31
  14.2 24.3 %collective-permute-start.2 = (f32[2,8,1,1024]{3,2,1,0:T(1,128)}, f32[2,8,1,1024]{3,2,1,0:T(1,128)S(1)}, u32[]{:S(2)}, u32[]{:S(2)}) collective-permute-start(f32[2,8,1,1024]{3,2,1,0:T(1,128)} %pad_maximum_fusion.11), channel_id=1, source_target_pairs={{1,0},{2,1},{3,2},{5,4},{6,5},{7,6},{9,8},{10,9},{11,10},{13,12},{... | collective-permute-start | bytes 196616 | tf_op jit(solution)/shard_map/ppermute | solution.py:36
  17.1 21.5 %collective-permute-start.1 = (f32[2,1,64,1024]{3,2,1,0:T(8,128)}, f32[2,1,64,1024]{3,2,1,0:T(8,128)}, u32[]{:S(2)}, u32[]{:S(2)}) collective-permute-start(f32[2,1,64,1024]{3,2,1,0:T(8,128)} %pad_maximum_fusion.2), channel_id=1, source_target_pairs={{0,4},{4,8},{8,12},{12,16},{16,20},{20,24},{24,28},{28,32},{32,36}... | collective-permute-start | bytes 1572872 | tf_op jit(solution)/shard_map/ppermute | solution.py:31
  23.1 22.2 %collective-permute-start = (f32[2,1,64,1024]{3,2,1,0:T(8,128)}, f32[2,1,64,1024]{3,2,1,0:T(8,128)}, u32[]{:S(2)}, u32[]{:S(2)}) collective-permute-start(f32[2,1,64,1024]{3,2,1,0:T(8,128)} %pad_maximum_fusion.1), channel_id=1, source_target_pairs={{4,0},{8,4},{12,8},{16,12},{20,16},{24,20},{28,24},{32,28},{36,32}... | collective-permute-start | bytes 1572872 | tf_op jit(solution)/shard_map/ppermute | solution.py:36
  38.5 8.6 %copy-start.6 = (f32[8,63,1024]{2,1,0:T(8,128)S(1)}, f32[8,63,1024]{2,1,0:T(8,128)}, u32[]{:S(2)}) copy-start(f32[8,63,1024]{2,1,0:T(8,128)} %get-tuple-element.89) | copy-start | bytes 6193156
  47.1 9.6 %copy-start.7 = (f32[7,64,1024]{2,1,0:T(8,128)S(1)}, f32[7,64,1024]{2,1,0:T(8,128)}, u32[]{:S(2)}) copy-start(f32[7,64,1024]{2,1,0:T(8,128)} %get-tuple-element.77) | copy-start | bytes 5505028
  85.6 16.2 %collective-permute-start.4 = (f32[1,64,1024]{2,1,0:T(8,128)S(1)}, f32[1,64,1024]{2,1,0:T(8,128)S(1)}, u32[]{:S(2)}, u32[]{:S(2)}) collective-permute-start(f32[1,64,1024]{2,1,0:T(8,128)S(1)} %get-tuple-element.68), channel_id=1, source_target_pairs={{4,0},{8,4},{12,8},{16,12},{20,16},{24,20},{28,24},{32,28},{36,32}... | collective-permute-start | bytes 786440 | tf_op jit(solution)/shard_map/ppermute | solution.py:19
  86.9 14.9 %collective-permute-start.5 = (f32[1,64,1024]{2,1,0:T(8,128)S(1)}, f32[1,64,1024]{2,1,0:T(8,128)S(1)}, u32[]{:S(2)}, u32[]{:S(2)}) collective-permute-start(f32[1,64,1024]{2,1,0:T(8,128)S(1)} %get-tuple-element.67), channel_id=1, source_target_pairs={{0,4},{4,8},{8,12},{12,16},{16,20},{20,24},{24,28},{28,32},{32,36}... | collective-permute-start | bytes 786440 | tf_op jit(solution)/shard_map/ppermute | solution.py:18
  92.6 9.2 %collective-permute-start.6 = (f32[8,1,1024]{2,1,0:T(1,128)S(1)}, f32[8,1,1024]{2,1,0:T(1,128)S(1)}, u32[]{:S(2)}, u32[]{:S(2)}) collective-permute-start(f32[8,1,1024]{2,1,0:T(1,128)S(1)} %get-tuple-element.64), channel_id=1, source_target_pairs={{1,0},{2,1},{3,2},{5,4},{6,5},{7,6},{9,8},{10,9},{11,10},{13,12},{... | collective-permute-start | bytes 98312 | tf_op jit(solution)/shard_map/ppermute | solution.py:19
  94.5 7.3 %copy-start.4 = (f32[8,64,1024]{2,1,0:T(8,128)S(1)}, f32[8,64,1024]{2,1,0:T(8,128)}, u32[]{:S(2)}) copy-start(f32[8,64,1024]{2,1,0:T(8,128)} %get-tuple-element.32) | copy-start | bytes 6291460
  94.5 7.2 %collective-permute-start.7 = (f32[8,1,1024]{2,1,0:T(1,128)S(1)}, f32[8,1,1024]{2,1,0:T(1,128)S(1)}, u32[]{:S(2)}, u32[]{:S(2)}) collective-permute-start(f32[8,1,1024]{2,1,0:T(1,128)S(1)} %get-tuple-element.63), channel_id=1, source_target_pairs={{0,1},{1,2},{2,3},{4,5},{5,6},{6,7},{8,9},{9,10},{10,11},{12,13},{... | collective-permute-start | bytes 98312 | tf_op jit(solution)/shard_map/ppermute | solution.py:18
  115.2 14.6 %copy-start.1 = (f32[8,64,1024]{2,1,0:T(8,128)}, f32[8,64,1024]{2,1,0:T(8,128)S(1)}, u32[]{:S(2)}) copy-start(f32[8,64,1024]{2,1,0:T(8,128)S(1)} %fusion.25) | copy-start | bytes 6291460
  123.1 6.7 %collective-permute-start.8 = (f32[8,1,1024]{2,1,0:T(1,128)S(1)}, f32[8,1,1024]{2,1,0:T(1,128)S(1)}, u32[]{:S(2)}, u32[]{:S(2)}) collective-permute-start(f32[8,1,1024]{2,1,0:T(1,128)S(1)} %get-tuple-element.58), channel_id=1, source_target_pairs={{1,0},{2,1},{3,2},{5,4},{6,5},{7,6},{9,8},{10,9},{11,10},{13,12},{... | collective-permute-start | bytes 98312 | tf_op jit(solution)/shard_map/ppermute | solution.py:19
  125.0 4.8 %collective-permute-start.9 = (f32[8,1,1024]{2,1,0:T(1,128)S(1)}, f32[8,1,1024]{2,1,0:T(1,128)S(1)}, u32[]{:S(2)}, u32[]{:S(2)}) collective-permute-start(f32[8,1,1024]{2,1,0:T(1,128)S(1)} %get-tuple-element.57), channel_id=1, source_target_pairs={{0,1},{1,2},{2,3},{4,5},{5,6},{6,7},{8,9},{9,10},{10,11},{12,13},{... | collective-permute-start | bytes 98312 | tf_op jit(solution)/shard_map/ppermute | solution.py:18
  129.8 16.6 %copy-start.12 = (f32[32,64]{1,0:T(8,128)S(1)}, f32[32,64]{1,0:T(8,128)}, u32[]{:S(2)}) copy-start(f32[32,64]{1,0:T(8,128)} %param.22) | copy-start | bytes 24580
  151.5 14.0 %copy-start.11 = (f32[8,32,128]{2,1,0:T(8,128)S(1)}, f32[8,32,128]{2,1,0:T(8,128)}, u32[]{:S(2)}) copy-start(f32[8,32,128]{2,1,0:T(8,128)} %param.24) | copy-start | bytes 393220
  152.9 22.6 %all-to-all-start = ((f32[32,1,1536]{2,1,0:T(1,128)}), f32[32,1,1536]{2,1,0:T(1,128)S(1)}, u32[]{:S(2)}, u32[]{:S(2)}) async-start(f32[32,1,1536]{2,1,0:T(1,128)} %reshape.96), calls=%async_computation | async-start | bytes 393216 | tf_op jit(solution)/shard_map/all_to_all | solution.py:140
  178.3 8.6 %collective-permute-start.11 = (f32[3,3,32,128]{3,2,1,0:T(8,128)S(1)}, f32[3,3,32,128]{3,2,1,0:T(8,128)S(1)}, u32[]{:S(2)}, u32[]{:S(2)}) collective-permute-start(f32[3,3,32,128]{3,2,1,0:T(8,128)S(1)} %get-tuple-element.108), channel_id=1, source_target_pairs={{4,0},{8,4},{12,8},{16,12},{20,16},{24,20},{28,24},{32,28},{36,32}... | collective-permute-start | bytes 442376 | tf_op jit(solution)/shard_map/ppermute | solution.py:157
  179.6 8.1 %collective-permute-start.10 = (f32[3,3,32,128]{3,2,1,0:T(8,128)S(1)}, f32[3,3,32,128]{3,2,1,0:T(8,128)S(1)}, u32[]{:S(2)}, u32[]{:S(2)}) collective-permute-start(f32[3,3,32,128]{3,2,1,0:T(8,128)S(1)} %get-tuple-element.107), channel_id=1, source_target_pairs={{0,4},{4,8},{8,12},{12,16},{16,20},{20,24},{24,28},{28,32},{32,36}... | collective-permute-start | bytes 442376 | tf_op jit(solution)/shard_map/ppermute | solution.py:156
  187.7 7.9 %collective-permute-start.13 = (f32[3,14,8,128]{3,2,1,0:T(8,128)S(1)}, f32[3,14,8,128]{3,2,1,0:T(8,128)S(1)}, u32[]{:S(2)}, u32[]{:S(2)}) collective-permute-start(f32[3,14,8,128]{3,2,1,0:T(8,128)S(1)} %get-tuple-element.102), channel_id=1, source_target_pairs={{1,0},{2,1},{3,2},{5,4},{6,5},{7,6},{9,8},{10,9},{11,10},{13,12},{... | collective-permute-start | bytes 516104 | tf_op jit(solution)/shard_map/ppermute | solution.py:157
  191.1 5.8 %collective-permute-start.12 = (f32[3,14,8,128]{3,2,1,0:T(8,128)S(1)}, f32[3,14,8,128]{3,2,1,0:T(8,128)S(1)}, u32[]{:S(2)}, u32[]{:S(2)}) collective-permute-start(f32[3,14,8,128]{3,2,1,0:T(8,128)S(1)} %get-tuple-element.101), channel_id=1, source_target_pairs={{0,1},{1,2},{2,3},{4,5},{5,6},{6,7},{8,9},{9,10},{10,11},{12,13},{... | collective-permute-start | bytes 516104 | tf_op jit(solution)/shard_map/ppermute | solution.py:156
  197.9 20.0 %copy-start.9 = (f32[8,32,128]{2,1,0:T(8,128)}, f32[8,32,128]{2,1,0:T(8,128)S(1)}, u32[]{:S(2)}) copy-start(f32[8,32,128]{2,1,0:T(8,128)S(1)} %fusion.67) | copy-start | bytes 393220
  (4 other events, 18.0 us)

commit v3 on v1

--- a/solution.py
+++ b/solution.py
@@ -39,7 +39,7 @@
 def bernoulli(value):
     small = jnp.abs(value) < 0.0001
     safe = jnp.where(small, jnp.float32(1.0), value)
-    return jnp.where(small, 1.0 - 0.5 * value, safe / jnp.expm1(safe))
+    return jnp.where(small, 1.0 - 0.5 * value, safe / (jnp.exp(safe) - 1.0))
 
 
 def per_device(

time: 189 us -> 184 us (0.974)
  other arithmetic: 59.5 us -> 52.8 us
    div x2, other arithmetic: 21.7 us -> 17.7 us  [sweep(): return fraction_top_quantity / denominator_quantity]
    mul x1, other arithmetic: 11.2 us -> 9.14 us  [per_device(): joule_power_input = 0.5 * joule_power_input]
where the time goes in v3:
time: 184 us; the launch traced here: 181 us
  starting transfers between devices  57.8 us (31%)
  other arithmetic  52.8 us (29%)
  waiting for transfers between devices  26 us (14%)
  blocking collectives  17.6 us (10%)
  local copies, waits for them, and re-layouts  15.3 us (8%)
  matrix products  10.5 us (6%)
    ppermute x5, starting transfers between devices, face_halos(): lax.ppermute(lax.slice_in_dim(block, size - 1, size, axis=dim), axis, for...  23.6 us
    div x2, other arithmetic, sweep(): return fraction_top_quantity / denominator_quantity  17.7 us
    all_to_all x1, blocking collectives, per_device(): got_warm = lax.all_to_all(windows, 'slab', 0, 0, tiled=False)  17.6 us
    all_to_all x1, starting transfers between devices, per_device(): got = lax.all_to_all(piece, 'slab', 0, 0, tiled=False)  12.6 us
    another operation x6, other arithmetic, per_device(): both = jnp.stack([effective, initial_electrons])  11.5 us
    ppermute x5, waiting for transfers between devices, face_halos(): high = lax.ppermute(lax.slice_in_dim(block, 0, 1, axis=dim), axis, backward)  11.3 us
    all_to_all x1, waiting for transfers between devices, per_device(): got = lax.all_to_all(piece, 'slab', 0, 0, tiled=False)  9.96 us
    mul x1, other arithmetic, per_device(): joule_power_input = 0.5 * joule_power_input  9.14 us
  transfers between devices with their start and end apart: 15, of which 6 were waited for; matrix products, arithmetic and copies ran while one was open for 11% of the time, Pallas kernels for 0%

profile of v3, /device:TPU:1, one launch (start us, length us, event | category | flops | bytes accessed | tf_op | source)
XLA Modules:
  0.0 181.3 jit_solution(14573053466276788645)
XLA Ops:
  2.0 5.7 %select_add_fusion = f32[8,64,1024]{2,1,0:T(8,128)S(1)} fusion(f32[8,64,1024]{2,1,0:T(8,128)} %param.15, s32[8,64,1024]{2,1,0:T(8,128)} %param.19, f32[]{:T(128)} %bitcast.3, f32[]{:T(128)} %bitcast.2, f32[]{:T(128)} %bitcast.1, f32[]{:T(128)} %bitcast), kind=kLoop, calls=%fused_computation.118 | loop fusion | flops 6291456 | bytes 6291472 | tf_op jit(solution)/shard_map/add | solution.py:64
  7.8 4.5 %collective-permute-start.3 = (f32[2,8,1,1024]{3,2,1,0:T(1,128)S(1)}, f32[2,8,1,1024]{3,2,1,0:T(1,128)S(1)}, u32[]{:S(2)}, u32[]{:S(2)}) collective-permute-start(f32[2,8,1,1024]{3,2,1,0:T(1,128)S(1)} %get-tuple-element.41), channel_id=1, source_target_pairs={{0,1},{1,2},{2,3},{4,5},{5,6},{6,7},{8,9},{9,10},{10,11},{12,13},{... | collective-permute-start | bytes 196616 | tf_op jit(solution)/shard_map/ppermute | solution.py:18
  15.3 5.1 %collective-permute-start.1 = (f32[2,1,64,1024]{3,2,1,0:T(8,128)}, f32[2,1,64,1024]{3,2,1,0:T(8,128)}, u32[]{:S(2)}, u32[]{:S(2)}) collective-permute-start(f32[2,1,64,1024]{3,2,1,0:T(8,128)} %get-tuple-element.37), channel_id=1, source_target_pairs={{0,4},{4,8},{8,12},{12,16},{16,20},{20,24},{24,28},{28,32},{32,36}... | collective-permute-start | bytes 1572872 | tf_op jit(solution)/shard_map/ppermute | solution.py:18
  21.7 3.1 %fusion = f32[2,8,64,1023]{3,2,1,0:T(8,128)} fusion(f32[1,8,64,1024]{3,2,1,0:T(8,128)S(1)} %bitcast.213, f32[1,8,64,1024]{3,2,1,0:T(8,128)S(1)} %bitcast.220), kind=kLoop, calls=%fused_computation.18 | loop fusion | flops 1047552 | bytes 8384512 | tf_op jit(solution)/shard_map/stack | solution.py:68
  24.9 3.2 %fusion.3 = (f32[2,7,64,1024]{3,2,1,0:T(8,128)}, f32[2,7,64,1024]{3,2,1,0:T(8,128)}) fusion(f32[1,8,64,1024]{3,2,1,0:T(8,128)S(1)} %bitcast.214, f32[1,8,64,1024]{3,2,1,0:T(8,128)S(1)} %bitcast.221), kind=kLoop, calls=%fused_computation.33 | loop fusion | flops 1835008 | bytes 11534336 | tf_op jit(solution)/shard_map/stack | solution.py:68
  28.2 2.9 %select_maximum_fusion = f32[2,8,64,1024]{3,2,1,0:T(8,128)S(1)} fusion(f32[1,8,64,1024]{3,2,1,0:T(8,128)} %bitcast.217, f32[1,8,64,1024]{3,2,1,0:T(8,128)S(1)} %bitcast.215), kind=kLoop, calls=%fused_computation.21 | loop fusion | flops 4194304 | bytes 8388608 | tf_op jit(solution)/shard_map/stack | solution.py:68
  32.2 11.3 %collective-permute-done = f32[2,1,64,1024]{3,2,1,0:T(8,128)} collective-permute-done((f32[2,1,64,1024]{3,2,1,0:T(8,128)}, f32[2,1,64,1024]{3,2,1,0:T(8,128)}, u32[]{:S(2)}, u32[]{:S(2)}) %collective-permute-start) | collective-permute-done | bytes 524320 | tf_op jit(solution)/shard_map/ppermute | solution.py:19
  43.5 4.2 %divide_select_fusion.4 = (f32[8,64,1024]{2,1,0:T(8,128)}, f32[8,64,1024]{2,1,0:T(8,128)S(1)}, f32[8,64,1024]{2,1,0:T(8,128)}, f32[8,64,1024]{2,1,0:T(8,128)S(1)}) fusion(f32[8,64,1024]{2,1,0:T(8,128)S(1)} %select_add_fusion, f32[2,7,64,1024]{3,2,1,0:T(8,128)S(1)} %copy-done.6, f32[2,1,64,1024]{3,2,1,0:T(8,128)} %collective-permute-done.1, ...), kind=kLoop, calls=%fused_computation.114 | loop fusion | flops 10485760 | bytes 18874368 | tf_op jit(solution)/shard_map/jit(_where)/select_n | solution.py:42
  48.7 8.3 %fusion.17 = f32[8,64,1024]{2,1,0:T(8,128)S(1)} fusion(f32[2,8,64,1023]{3,2,1,0:T(8,128)S(1)} %copy-done.4, f32[2,8,64,1024]{3,2,1,0:T(8,128)S(1)} %select_maximum_fusion, f32[2,8,63,1024]{3,2,1,0:T(8,128)S(1)} %get-tuple-element.39, f32[2,8,1,1024]{3,2,1,0:T(1,128)S(1)} %collective-permute-done.3, f32[2,8,1,1024]{3,2,1,0:T(1,128)S(1)} %collective-permute-done.2, ...), kind=kLoop, calls=%fused_computation.47 | loop fusion | flops 43515904 | bytes 37744640 | tf_op jit(solution)/shard_map/div | solution.py:82
  61.0 5.5 %collective-permute-start.5 = (f32[1,64,1024]{2,1,0:T(8,128)S(1)}, f32[1,64,1024]{2,1,0:T(8,128)S(1)}, u32[]{:S(2)}, u32[]{:S(2)}) collective-permute-start(f32[1,64,1024]{2,1,0:T(8,128)S(1)} %get-tuple-element.58), channel_id=1, source_target_pairs={{0,4},{4,8},{8,12},{12,16},{16,20},{20,24},{24,28},{28,32},{32,36}... | collective-permute-start | bytes 786440 | tf_op jit(solution)/shard_map/ppermute | solution.py:18
  68.4 4.6 %collective-permute-start.7 = (f32[8,1,1024]{2,1,0:T(1,128)S(1)}, f32[8,1,1024]{2,1,0:T(1,128)S(1)}, u32[]{:S(2)}, u32[]{:S(2)}) collective-permute-start(f32[8,1,1024]{2,1,0:T(1,128)S(1)} %get-tuple-element.54), channel_id=1, source_target_pairs={{0,1},{1,2},{2,3},{4,5},{5,6},{6,7},{8,9},{9,10},{10,11},{12,13},{... | collective-permute-start | bytes 98312 | tf_op jit(solution)/shard_map/ppermute | solution.py:18
  73.0 2.2 %fusion.131 = (f32[7,64,1024]{2,1,0:T(8,128)}, f32[7,64,1024]{2,1,0:T(8,128)}) fusion(f32[8,64,1024]{2,1,0:T(8,128)S(1)} %fusion.17), kind=kLoop, calls=%fused_computation.237 | loop fusion | bytes 7340032 | tf_op jit(solution)/shard_map/slice | solution.py:30
  75.3 9.4 %fusion.50 = f32[8,64,1024]{2,1,0:T(8,128)S(1)} fusion(f32[8,64,1024]{2,1,0:T(8,128)S(1)} %copy-done.7, f32[1,64,1024]{2,1,0:T(8,128)S(1)} %collective-permute-done.4, f32[7,64,1024]{2,1,0:T(8,128)} %get-tuple-element.61, f32[7,64,1024]{2,1,0:T(8,128)} %get-tuple-element.60, f32[1,64,1024]{2,1,0:T(8,128)S(1)} %collective-permute-done.5, ...), kind=kLoop, calls=%fused_computation.87 | loop fusion | flops 43515904 | bytes 39837696 | tf_op jit(solution)/shard_map/div | solution.py:82
  86.2 2.3 %fusion.123 = (f32[7,64,1024]{2,1,0:T(8,128)}, f32[7,64,1024]{2,1,0:T(8,128)}) fusion(f32[8,64,1024]{2,1,0:T(8,128)S(1)} %fusion.50), kind=kLoop, calls=%fused_computation.229 | loop fusion | bytes 7340032 | tf_op jit(solution)/shard_map/slice | solution.py:29
  90.4 3.8 %collective-permute-start.9 = (f32[8,1,1024]{2,1,0:T(1,128)S(1)}, f32[8,1,1024]{2,1,0:T(1,128)S(1)}, u32[]{:S(2)}, u32[]{:S(2)}) collective-permute-start(f32[8,1,1024]{2,1,0:T(1,128)S(1)} %get-tuple-element.48), channel_id=1, source_target_pairs={{0,1},{1,2},{2,3},{4,5},{5,6},{6,7},{8,9},{9,10},{10,11},{12,13},{... | collective-permute-start | bytes 98312 | tf_op jit(solution)/shard_map/ppermute | solution.py:18
  95.4 9.1 %fusion.57 = f32[8,64,1024]{2,1,0:T(8,128)S(1)} fusion(f32[8,1,1024]{2,1,0:T(1,128)S(1)} %collective-permute-done.8, f32[8,63,1024]{2,1,0:T(8,128)S(1)} %get-tuple-element.51, f32[8,63,1024]{2,1,0:T(8,128)S(1)} %get-tuple-element.50, f32[8,1,1024]{2,1,0:T(1,128)S(1)} %collective-permute-done.9, f32[8,64,1024]{2,1,0:T(8,128)S(1)} %fusion.50, ...), kind=kLoop, calls=%fused_computation.98 | loop fusion | flops 48234496 | bytes 37216256 | tf_op jit(solution)/shard_map/mul | solution.py:100
  109.5 12.6 %all-to-all-start = ((f32[32,1,1536]{2,1,0:T(1,128)}), f32[32,1,1536]{2,1,0:T(1,128)S(1)}, u32[]{:S(2)}, u32[]{:S(2)}) async-start(f32[32,1,1536]{2,1,0:T(1,128)} %reshape.96), calls=%async_computation | async-start | bytes 393216 | tf_op jit(solution)/shard_map/all_to_all | solution.py:120
  122.1 10.0 %all-to-all-done = f32[32,1,1536]{2,1,0:T(1,128)S(1)} async-done(((f32[32,1,1536]{2,1,0:T(1,128)}), f32[32,1,1536]{2,1,0:T(1,128)S(1)}, u32[]{:S(2)}, u32[]{:S(2)}) %all-to-all-start) | async-done | bytes 196640 | tf_op jit(solution)/shard_map/all_to_all | solution.py:120
  136.2 5.5 %collective-permute-start.10 = (f32[3,3,32,128]{3,2,1,0:T(8,128)S(1)}, f32[3,3,32,128]{3,2,1,0:T(8,128)S(1)}, u32[]{:S(2)}, u32[]{:S(2)}) collective-permute-start(f32[3,3,32,128]{3,2,1,0:T(8,128)S(1)} %get-tuple-element.70), channel_id=1, source_target_pairs={{0,4},{4,8},{8,12},{12,16},{16,20},{20,24},{24,28},{28,32},{32,36}... | collective-permute-start | bytes 442376 | tf_op jit(solution)/shard_map/ppermute | solution.py:136
  144.3 3.3 %collective-permute-start.13 = (f32[3,14,8,128]{3,2,1,0:T(8,128)S(1)}, f32[3,14,8,128]{3,2,1,0:T(8,128)S(1)}, u32[]{:S(2)}, u32[]{:S(2)}) collective-permute-start(f32[3,14,8,128]{3,2,1,0:T(8,128)S(1)} %get-tuple-element.69), channel_id=1, source_target_pairs={{1,0},{2,1},{3,2},{5,4},{6,5},{7,6},{9,8},{10,9},{11,10},{13,12},{... | collective-permute-start | bytes 516104 | tf_op jit(solution)/shard_map/ppermute | solution.py:137
  147.7 3.3 %collective-permute-start.12 = (f32[3,14,8,128]{3,2,1,0:T(8,128)S(1)}, f32[3,14,8,128]{3,2,1,0:T(8,128)S(1)}, u32[]{:S(2)}, u32[]{:S(2)}) collective-permute-start(f32[3,14,8,128]{3,2,1,0:T(8,128)S(1)} %get-tuple-element.68), channel_id=1, source_target_pairs={{0,1},{1,2},{2,3},{4,5},{5,6},{6,7},{8,9},{9,10},{10,11},{12,13},{... | collective-permute-start | bytes 516104 | tf_op jit(solution)/shard_map/ppermute | solution.py:136
  155.7 17.6 %all_to_all.10 = f32[32,1,1536]{2,1,0:T(1,128)S(1)} all-to-all(f32[32,1,1536]{2,1,0:T(1,128)S(1)} %reshape.98), channel_id=1, replica_groups=mesh['slab'=32,'gy'=4] {'slab'}, dimensions={0} | all-to-all | bytes 393216 | tf_op jit(solution)/shard_map/all_to_all | solution.py:175
  175.9 2.1 %convolution_bitcast_fusion = f32[8,32,1024]{2,1,0:T(8,128)S(1)} fusion(f32[256,1024]{1,0:T(8,128)S(1)} %copy-done, f32[32,8,32,8]{2,3,1,0:T(8,128)S(1)} %fusion.66), kind=kOutput, calls=%fused_computation.138 | convolution fusion | flops 805306368 | bytes 2359296 | tf_op jit(solution)/shard_map/scbx,scz->xbz/dot_general | solution.py:178
  178.0 3.3 %multiply_bitcast_fusion = f32[8,64,1024]{2,1,0:T(8,128)} fusion(f32[8,32,1024]{2,1,0:T(8,128)S(1)} %convolution_bitcast_fusion, f32[32,64]{1,0:T(8,128)S(1)} %copy-done.13), kind=kOutput, calls=%fused_computation.102 | convolution fusion | flops 201850880 | bytes 3153920 | tf_op jit(solution)/shard_map/hc,qhk->qck/dot_general | solution.py:179
  (95 shorter events, 37.1 us)
Async XLA Ops:
  0.6 105.5 %copy-start = (f32[256,1024]{1,0:T(8,128)S(1)}, f32[256,1024]{1,0:T(8,128)}, u32[]{:S(2)}) copy-start(f32[256,1024]{1,0:T(8,128)} %param.23) | copy-start | bytes 3145732
  2.0 5.7 %copy-start.2 = (f32[8,64,1024]{2,1,0:T(8,128)S(1)}, f32[8,64,1024]{2,1,0:T(8,128)}, u32[]{:S(2)}) copy-start(f32[8,64,1024]{2,1,0:T(8,128)} %param.16) | copy-start | bytes 6291460
  7.8 39.9 %collective-permute-start.3 = (f32[2,8,1,1024]{3,2,1,0:T(1,128)S(1)}, f32[2,8,1,1024]{3,2,1,0:T(1,128)S(1)}, u32[]{:S(2)}, u32[]{:S(2)}) collective-permute-start(f32[2,8,1,1024]{3,2,1,0:T(1,128)S(1)} %get-tuple-element.41), channel_id=1, source_target_pairs={{0,1},{1,2},{2,3},{4,5},{5,6},{6,7},{8,9},{9,10},{10,11},{12,13},{... | collective-permute-start | bytes 196616 | tf_op jit(solution)/shard_map/ppermute | solution.py:18
  12.3 35.3 %collective-permute-start.2 = (f32[2,8,1,1024]{3,2,1,0:T(1,128)S(1)}, f32[2,8,1,1024]{3,2,1,0:T(1,128)S(1)}, u32[]{:S(2)}, u32[]{:S(2)}) collective-permute-start(f32[2,8,1,1024]{3,2,1,0:T(1,128)S(1)} %get-tuple-element.40), channel_id=1, source_target_pairs={{1,0},{2,1},{3,2},{5,4},{6,5},{7,6},{9,8},{10,9},{11,10},{13,12},{... | collective-permute-start | bytes 196616 | tf_op jit(solution)/shard_map/ppermute | solution.py:19
  15.3 16.9 %collective-permute-start.1 = (f32[2,1,64,1024]{3,2,1,0:T(8,128)}, f32[2,1,64,1024]{3,2,1,0:T(8,128)}, u32[]{:S(2)}, u32[]{:S(2)}) collective-permute-start(f32[2,1,64,1024]{3,2,1,0:T(8,128)} %get-tuple-element.37), channel_id=1, source_target_pairs={{0,4},{4,8},{8,12},{12,16},{16,20},{20,24},{24,28},{28,32},{32,36}... | collective-permute-start | bytes 1572872 | tf_op jit(solution)/shard_map/ppermute | solution.py:18
  20.5 23.0 %collective-permute-start = (f32[2,1,64,1024]{3,2,1,0:T(8,128)}, f32[2,1,64,1024]{3,2,1,0:T(8,128)}, u32[]{:S(2)}, u32[]{:S(2)}) collective-permute-start(f32[2,1,64,1024]{3,2,1,0:T(8,128)} %get-tuple-element.36), channel_id=1, source_target_pairs={{4,0},{8,4},{12,8},{16,12},{20,16},{24,20},{28,24},{32,28},{36,32}... | collective-permute-start | bytes 1572872 | tf_op jit(solution)/shard_map/ppermute | solution.py:19
  31.1 12.4 %copy-start.5 = (f32[2,7,64,1024]{3,2,1,0:T(8,128)S(1)}, f32[2,7,64,1024]{3,2,1,0:T(8,128)}, u32[]{:S(2)}) copy-start(f32[2,7,64,1024]{3,2,1,0:T(8,128)} %get-tuple-element.34) | copy-start | bytes 11010052
  31.1 12.4 %copy-start.6 = (f32[2,7,64,1024]{3,2,1,0:T(8,128)S(1)}, f32[2,7,64,1024]{3,2,1,0:T(8,128)}, u32[]{:S(2)}) copy-start(f32[2,7,64,1024]{3,2,1,0:T(8,128)} %get-tuple-element.35) | copy-start | bytes 11010052
  43.5 5.2 %copy-start.8 = (f32[8,64,1024]{2,1,0:T(8,128)S(1)}, f32[8,64,1024]{2,1,0:T(8,128)}, u32[]{:S(2)}) copy-start(f32[8,64,1024]{2,1,0:T(8,128)} %param.18) | copy-start | bytes 6291460
  59.7 15.6 %collective-permute-start.4 = (f32[1,64,1024]{2,1,0:T(8,128)S(1)}, f32[1,64,1024]{2,1,0:T(8,128)S(1)}, u32[]{:S(2)}, u32[]{:S(2)}) collective-permute-start(f32[1,64,1024]{2,1,0:T(8,128)S(1)} %get-tuple-element.59), channel_id=1, source_target_pairs={{4,0},{8,4},{12,8},{16,12},{20,16},{24,20},{28,24},{32,28},{36,32}... | collective-permute-start | bytes 786440 | tf_op jit(solution)/shard_map/ppermute | solution.py:19
  61.0 14.3 %collective-permute-start.5 = (f32[1,64,1024]{2,1,0:T(8,128)S(1)}, f32[1,64,1024]{2,1,0:T(8,128)S(1)}, u32[]{:S(2)}, u32[]{:S(2)}) collective-permute-start(f32[1,64,1024]{2,1,0:T(8,128)S(1)} %get-tuple-element.58), channel_id=1, source_target_pairs={{0,4},{4,8},{8,12},{12,16},{16,20},{20,24},{24,28},{28,32},{32,36}... | collective-permute-start | bytes 786440 | tf_op jit(solution)/shard_map/ppermute | solution.py:18
  66.5 8.8 %collective-permute-start.6 = (f32[8,1,1024]{2,1,0:T(1,128)S(1)}, f32[8,1,1024]{2,1,0:T(1,128)S(1)}, u32[]{:S(2)}, u32[]{:S(2)}) collective-permute-start(f32[8,1,1024]{2,1,0:T(1,128)S(1)} %get-tuple-element.55), channel_id=1, source_target_pairs={{1,0},{2,1},{3,2},{5,4},{6,5},{7,6},{9,8},{10,9},{11,10},{13,12},{... | collective-permute-start | bytes 98312 | tf_op jit(solution)/shard_map/ppermute | solution.py:19
  68.4 6.9 %collective-permute-start.7 = (f32[8,1,1024]{2,1,0:T(1,128)S(1)}, f32[8,1,1024]{2,1,0:T(1,128)S(1)}, u32[]{:S(2)}, u32[]{:S(2)}) collective-permute-start(f32[8,1,1024]{2,1,0:T(1,128)S(1)} %get-tuple-element.54), channel_id=1, source_target_pairs={{0,1},{1,2},{2,3},{4,5},{5,6},{6,7},{8,9},{9,10},{10,11},{12,13},{... | collective-permute-start | bytes 98312 | tf_op jit(solution)/shard_map/ppermute | solution.py:18
  84.7 10.7 %copy-start.1 = (f32[8,64,1024]{2,1,0:T(8,128)}, f32[8,64,1024]{2,1,0:T(8,128)S(1)}, u32[]{:S(2)}) copy-start(f32[8,64,1024]{2,1,0:T(8,128)S(1)} %fusion.50) | copy-start | bytes 6291460
  88.5 6.9 %collective-permute-start.8 = (f32[8,1,1024]{2,1,0:T(1,128)S(1)}, f32[8,1,1024]{2,1,0:T(1,128)S(1)}, u32[]{:S(2)}, u32[]{:S(2)}) collective-permute-start(f32[8,1,1024]{2,1,0:T(1,128)S(1)} %get-tuple-element.49), channel_id=1, source_target_pairs={{1,0},{2,1},{3,2},{5,4},{6,5},{7,6},{9,8},{10,9},{11,10},{13,12},{... | collective-permute-start | bytes 98312 | tf_op jit(solution)/shard_map/ppermute | solution.py:19
  90.4 5.0 %collective-permute-start.9 = (f32[8,1,1024]{2,1,0:T(1,128)S(1)}, f32[8,1,1024]{2,1,0:T(1,128)S(1)}, u32[]{:S(2)}, u32[]{:S(2)}) collective-permute-start(f32[8,1,1024]{2,1,0:T(1,128)S(1)} %get-tuple-element.48), channel_id=1, source_target_pairs={{0,1},{1,2},{2,3},{4,5},{5,6},{6,7},{8,9},{9,10},{10,11},{12,13},{... | collective-permute-start | bytes 98312 | tf_op jit(solution)/shard_map/ppermute | solution.py:18
  95.4 9.2 %copy-start.13 = (f32[32,64]{1,0:T(8,128)S(1)}, f32[32,64]{1,0:T(8,128)}, u32[]{:S(2)}) copy-start(f32[32,64]{1,0:T(8,128)} %param.22) | copy-start | bytes 24580
  108.1 14.0 %copy-start.12 = (f32[8,32,128]{2,1,0:T(8,128)S(1)}, f32[8,32,128]{2,1,0:T(8,128)}, u32[]{:S(2)}) copy-start(f32[8,32,128]{2,1,0:T(8,128)} %param.24) | copy-start | bytes 393220
  109.5 22.6 %all-to-all-start = ((f32[32,1,1536]{2,1,0:T(1,128)}), f32[32,1,1536]{2,1,0:T(1,128)S(1)}, u32[]{:S(2)}, u32[]{:S(2)}) async-start(f32[32,1,1536]{2,1,0:T(1,128)} %reshape.96), calls=%async_computation | async-start | bytes 393216 | tf_op jit(solution)/shard_map/all_to_all | solution.py:120
  134.9 8.6 %collective-permute-start.11 = (f32[3,3,32,128]{3,2,1,0:T(8,128)S(1)}, f32[3,3,32,128]{3,2,1,0:T(8,128)S(1)}, u32[]{:S(2)}, u32[]{:S(2)}) collective-permute-start(f32[3,3,32,128]{3,2,1,0:T(8,128)S(1)} %get-tuple-element.71), channel_id=1, source_target_pairs={{4,0},{8,4},{12,8},{16,12},{20,16},{24,20},{28,24},{32,28},{36,32}... | collective-permute-start | bytes 442376 | tf_op jit(solution)/shard_map/ppermute | solution.py:137
  136.2 8.1 %collective-permute-start.10 = (f32[3,3,32,128]{3,2,1,0:T(8,128)S(1)}, f32[3,3,32,128]{3,2,1,0:T(8,128)S(1)}, u32[]{:S(2)}, u32[]{:S(2)}) collective-permute-start(f32[3,3,32,128]{3,2,1,0:T(8,128)S(1)} %get-tuple-element.70), channel_id=1, source_target_pairs={{0,4},{4,8},{8,12},{12,16},{16,20},{20,24},{24,28},{28,32},{32,36}... | collective-permute-start | bytes 442376 | tf_op jit(solution)/shard_map/ppermute | solution.py:136
  144.3 7.7 %collective-permute-start.13 = (f32[3,14,8,128]{3,2,1,0:T(8,128)S(1)}, f32[3,14,8,128]{3,2,1,0:T(8,128)S(1)}, u32[]{:S(2)}, u32[]{:S(2)}) collective-permute-start(f32[3,14,8,128]{3,2,1,0:T(8,128)S(1)} %get-tuple-element.69), channel_id=1, source_target_pairs={{1,0},{2,1},{3,2},{5,4},{6,5},{7,6},{9,8},{10,9},{11,10},{13,12},{... | collective-permute-start | bytes 516104 | tf_op jit(solution)/shard_map/ppermute | solution.py:137
  147.7 5.6 %collective-permute-start.12 = (f32[3,14,8,128]{3,2,1,0:T(8,128)S(1)}, f32[3,14,8,128]{3,2,1,0:T(8,128)S(1)}, u32[]{:S(2)}, u32[]{:S(2)}) collective-permute-start(f32[3,14,8,128]{3,2,1,0:T(8,128)S(1)} %get-tuple-element.68), channel_id=1, source_target_pairs={{0,1},{1,2},{2,3},{4,5},{5,6},{6,7},{8,9},{9,10},{10,11},{12,13},{... | collective-permute-start | bytes 516104 | tf_op jit(solution)/shard_map/ppermute | solution.py:136
  154.4 20.0 %copy-start.10 = (f32[8,32,128]{2,1,0:T(8,128)}, f32[8,32,128]{2,1,0:T(8,128)S(1)}, u32[]{:S(2)}) copy-start(f32[8,32,128]{2,1,0:T(8,128)S(1)} %fusion.94) | copy-start | bytes 393220
  (5 other events, 15.5 us)

commit v4 on v3

--- a/solution.py
+++ b/solution.py
@@ -98,10 +98,10 @@
             - (bernoulli_coefficient + voltage_gradient) * n_final
         )
     joule_power_input = 0.5 * joule_power_input
-    up_x, down_x = voltage_gradients[0], voltage_gradients[1]
-    bup_x, bdown_x = bernoulli_coefficients[0], bernoulli_coefficients[1]
-    heat_left = -0.5 * (down_x[:1] * ((bdown_x[:1] + down_x[:1]) * n_final[:1]))
-    heat_right = -0.5 * (up_x[-1:] * ((bup_x[-1:] + up_x[-1:]) * n_final[-1:]))
+    down_x = voltage_gradients[1][:1]
+    up_x = voltage_gradients[0][-1:]
+    heat_left = -0.5 * (down_x * ((bernoulli(down_x) + down_x) * n_final[:1]))
+    heat_right = -0.5 * (up_x * ((bernoulli(up_x) + up_x) * n_final[-1:]))
     heat_ext = jnp.concatenate([heat_left, joule_power_input, heat_right], axis=0)
 
     padded_first = jnp.pad(restrict_matrix_first, ((1, 1), (1, 1)))

time: 184 us -> 181 us (0.984)
  waiting for transfers between devices: 26 us -> 23.6 us
    select_n x1 -> x0, other arithmetic: 4.17 us -> none  [bernoulli(): return jnp.where(small, 1.0 - 0.5 * value, safe / (jnp.exp(safe) - 1.0))]
    another operation x6, other arithmetic: 11.5 us -> 14.6 us  [per_device(): both = jnp.stack([effective, initial_electrons])]
    ppermute x5, waiting for transfers between devices: 11.3 us -> 8.26 us  [face_halos(): high = lax.ppermute(lax.slice_in_dim(block, 0, 1, axis=dim), axis, backward)]
  transfers between devices with their start and end apart: 15 -> 15, of which waited for: 6 -> 7; matrix products, arithmetic and copies ran while one was open for 11% -> 10% of each run, Pallas kernels for 0% -> 0%
where the time goes in v4:
time: 181 us; the launch traced here: 179 us
  starting transfers between devices  58.5 us (32%)
  other arithmetic  52.2 us (29%)
  waiting for transfers between devices  23.6 us (13%)
  blocking collectives  17.6 us (10%)
  local copies, waits for them, and re-layouts  15.2 us (8%)
  matrix products  10.5 us (6%)
    ppermute x5, starting transfers between devices, face_halos(): lax.ppermute(lax.slice_in_dim(block, size - 1, size, axis=dim), axis, for...  23.9 us
    div x2, other arithmetic, sweep(): return fraction_top_quantity / denominator_quantity  18.4 us
    all_to_all x1, blocking collectives, per_device(): got_warm = lax.all_to_all(windows, 'slab', 0, 0, tiled=False)  17.6 us
    another operation x6, other arithmetic, per_device(): both = jnp.stack([effective, initial_electrons])  14.6 us
    all_to_all x1, starting transfers between devices, per_device(): got = lax.all_to_all(piece, 'slab', 0, 0, tiled=False)  12.6 us
    all_to_all x1, waiting for transfers between devices, per_device(): got = lax.all_to_all(piece, 'slab', 0, 0, tiled=False)  9.8 us
    ppermute x2, starting transfers between devices, per_device(): lax.ppermute(lax.slice_in_dim(stacked, size - depth, size, axis=dim), axi...  9.33 us
    mul x1, other arithmetic, per_device(): joule_power_input = 0.5 * joule_power_input  9.15 us
  transfers between devices with their start and end apart: 15, of which 7 were waited for; matrix products, arithmetic and copies ran while one was open for 10% of the time, Pallas kernels for 0%

profile of v4, /device:TPU:1, one launch (start us, length us, event | category | flops | bytes accessed | tf_op | source)
XLA Modules:
  0.0 178.7 jit_solution(16448191132198819967)
XLA Ops:
  2.1 5.8 %select_add_fusion = f32[8,64,1024]{2,1,0:T(8,128)S(1)} fusion(f32[8,64,1024]{2,1,0:T(8,128)} %param.15, s32[8,64,1024]{2,1,0:T(8,128)} %param.19, f32[]{:T(128)} %bitcast.3, f32[]{:T(128)} %bitcast.2, f32[]{:T(128)} %bitcast.1, f32[]{:T(128)} %bitcast), kind=kLoop, calls=%fused_computation.118 | loop fusion | flops 6291456 | bytes 6291472 | tf_op jit(solution)/shard_map/add | solution.py:64
  8.6 4.5 %collective-permute-start.3 = (f32[2,8,1,1024]{3,2,1,0:T(1,128)}, f32[2,8,1,1024]{3,2,1,0:T(1,128)S(1)}, u32[]{:S(2)}, u32[]{:S(2)}) collective-permute-start(f32[2,8,1,1024]{3,2,1,0:T(1,128)} %get-tuple-element.40), channel_id=1, source_target_pairs={{0,1},{1,2},{2,3},{4,5},{5,6},{6,7},{8,9},{9,10},{10,11},{12,13},{... | collective-permute-start | bytes 196616 | tf_op jit(solution)/shard_map/ppermute | solution.py:18
  16.1 5.2 %collective-permute-start.1 = (f32[2,1,64,1024]{3,2,1,0:T(8,128)}, f32[2,1,64,1024]{3,2,1,0:T(8,128)}, u32[]{:S(2)}, u32[]{:S(2)}) collective-permute-start(f32[2,1,64,1024]{3,2,1,0:T(8,128)} %get-tuple-element.36), channel_id=1, source_target_pairs={{0,4},{4,8},{8,12},{12,16},{16,20},{20,24},{24,28},{28,32},{32,36}... | collective-permute-start | bytes 1572872 | tf_op jit(solution)/shard_map/ppermute | solution.py:18
  22.5 3.1 %fusion = f32[2,8,64,1023]{3,2,1,0:T(8,128)} fusion(f32[1,8,64,1024]{3,2,1,0:T(8,128)S(1)} %bitcast.213, f32[1,8,64,1024]{3,2,1,0:T(8,128)S(1)} %bitcast.220), kind=kLoop, calls=%fused_computation.18 | loop fusion | flops 1047552 | bytes 8384512 | tf_op jit(solution)/shard_map/stack | solution.py:68
  25.6 3.2 %select_maximum_fusion = f32[2,8,64,1024]{3,2,1,0:T(8,128)} fusion(f32[1,8,64,1024]{3,2,1,0:T(8,128)S(1)} %bitcast.221, f32[1,8,64,1024]{3,2,1,0:T(8,128)S(1)} %bitcast.214), kind=kLoop, calls=%fused_computation.21 | loop fusion | flops 4194304 | bytes 8388608 | tf_op jit(solution)/shard_map/stack | solution.py:68
  28.8 3.4 %fusion.3 = (f32[2,7,64,1024]{3,2,1,0:T(8,128)}, f32[2,7,64,1024]{3,2,1,0:T(8,128)}) fusion(f32[1,8,64,1024]{3,2,1,0:T(8,128)S(1)} %bitcast.215, f32[1,8,64,1024]{3,2,1,0:T(8,128)S(1)} %bitcast.222), kind=kLoop, calls=%fused_computation.33 | loop fusion | flops 1835008 | bytes 11534336 | tf_op jit(solution)/shard_map/stack | solution.py:68
  32.3 3.1 %fusion.1 = (f32[2,8,63,1024]{3,2,1,0:T(8,128)S(1)}, f32[2,8,63,1024]{3,2,1,0:T(8,128)S(1)}) fusion(f32[1,8,64,1024]{3,2,1,0:T(8,128)S(1)} %bitcast.216, f32[1,8,64,1024]{3,2,1,0:T(8,128)} %bitcast.217), kind=kLoop, calls=%fused_computation.19 | loop fusion | flops 2064384 | bytes 12451840 | tf_op jit(solution)/shard_map/stack | solution.py:68
  36.0 8.3 %collective-permute-done = f32[2,1,64,1024]{3,2,1,0:T(8,128)} collective-permute-done((f32[2,1,64,1024]{3,2,1,0:T(8,128)}, f32[2,1,64,1024]{3,2,1,0:T(8,128)}, u32[]{:S(2)}, u32[]{:S(2)}) %collective-permute-start) | collective-permute-done | bytes 524320 | tf_op jit(solution)/shard_map/ppermute | solution.py:19
  44.3 9.1 %fusion.17 = (f32[8,64,1024]{2,1,0:T(8,128)S(1)}, f32[8,64,1024]{2,1,0:T(8,128)S(1)}, f32[8,64,1024]{2,1,0:T(8,128)S(1)}) fusion(f32[2,8,64,1023]{3,2,1,0:T(8,128)S(1)} %copy-done.3, f32[2,8,64,1024]{3,2,1,0:T(8,128)S(1)} %copy-done.4, f32[2,8,63,1024]{3,2,1,0:T(8,128)S(1)} %get-tuple-element.38, f32[2,8,1,1024]{3,2,1,0:T(1,128)S(1)} %collective-permute-done.3, ...), kind=kLoop, calls=%fused_computation.47 | loop fusion | flops 45613056 | bytes 37744640 | tf_op jit(solution)/shard_map/div | solution.py:82
  54.1 2.1 %fusion.127 = (f32[8,64,1023]{2,1,0:T(8,128)S(1)}, f32[8,64,1023]{2,1,0:T(8,128)}) fusion(f32[8,64,1024]{2,1,0:T(8,128)S(1)} %get-tuple-element.30), kind=kLoop, calls=%fused_computation.233 | loop fusion | bytes 8380416 | tf_op jit(solution)/shard_map/slice | solution.py:34
  57.5 5.5 %collective-permute-start.5 = (f32[1,64,1024]{2,1,0:T(8,128)S(1)}, f32[1,64,1024]{2,1,0:T(8,128)S(1)}, u32[]{:S(2)}, u32[]{:S(2)}) collective-permute-start(f32[1,64,1024]{2,1,0:T(8,128)S(1)} %get-tuple-element.57), channel_id=1, source_target_pairs={{0,4},{4,8},{8,12},{12,16},{16,20},{20,24},{24,28},{28,32},{32,36}... | collective-permute-start | bytes 786440 | tf_op jit(solution)/shard_map/ppermute | solution.py:18
  64.9 4.9 %collective-permute-start.7 = (f32[8,1,1024]{2,1,0:T(1,128)S(1)}, f32[8,1,1024]{2,1,0:T(1,128)S(1)}, u32[]{:S(2)}, u32[]{:S(2)}) collective-permute-start(f32[8,1,1024]{2,1,0:T(1,128)S(1)} %get-tuple-element.53), channel_id=1, source_target_pairs={{0,1},{1,2},{2,3},{4,5},{5,6},{6,7},{8,9},{9,10},{10,11},{12,13},{... | collective-permute-start | bytes 98312 | tf_op jit(solution)/shard_map/ppermute | solution.py:18
  69.8 2.3 %fusion.131 = (f32[7,64,1024]{2,1,0:T(8,128)}, f32[7,64,1024]{2,1,0:T(8,128)}) fusion(f32[8,64,1024]{2,1,0:T(8,128)S(1)} %get-tuple-element.30), kind=kLoop, calls=%fused_computation.237 | loop fusion | bytes 7340032 | tf_op jit(solution)/shard_map/slice | solution.py:30
  73.0 9.3 %fusion.50 = f32[8,64,1024]{2,1,0:T(8,128)S(1)} fusion(f32[8,64,1024]{2,1,0:T(8,128)S(1)} %copy-done.6, f32[1,64,1024]{2,1,0:T(8,128)} %copy-done.10, f32[7,64,1024]{2,1,0:T(8,128)} %get-tuple-element.60, f32[7,64,1024]{2,1,0:T(8,128)} %get-tuple-element.59, f32[1,64,1024]{2,1,0:T(8,128)} %copy-done.11, f32[8,1,1024]{2,1,0:T(1,128)S(1)} %collective-permute-done.6, ...), kind=kLoop, calls=%fused_computation.87 | loop fusion | flops 43515904 | bytes 39837696 | tf_op jit(solution)/shard_map/div | solution.py:82
  83.5 2.4 %fusion.123 = (f32[7,64,1024]{2,1,0:T(8,128)}, f32[7,64,1024]{2,1,0:T(8,128)}) fusion(f32[8,64,1024]{2,1,0:T(8,128)S(1)} %fusion.50), kind=kLoop, calls=%fused_computation.229 | loop fusion | bytes 7340032 | tf_op jit(solution)/shard_map/slice | solution.py:29
  87.8 3.8 %collective-permute-start.9 = (f32[8,1,1024]{2,1,0:T(1,128)S(1)}, f32[8,1,1024]{2,1,0:T(1,128)S(1)}, u32[]{:S(2)}, u32[]{:S(2)}) collective-permute-start(f32[8,1,1024]{2,1,0:T(1,128)S(1)} %get-tuple-element.47), channel_id=1, source_target_pairs={{0,1},{1,2},{2,3},{4,5},{5,6},{6,7},{8,9},{9,10},{10,11},{12,13},{... | collective-permute-start | bytes 98312 | tf_op jit(solution)/shard_map/ppermute | solution.py:18
  92.5 9.2 %fusion.57 = f32[8,64,1024]{2,1,0:T(8,128)S(1)} fusion(f32[8,1,1024]{2,1,0:T(1,128)S(1)} %collective-permute-done.8, f32[8,63,1024]{2,1,0:T(8,128)S(1)} %get-tuple-element.50, f32[8,63,1024]{2,1,0:T(8,128)S(1)} %get-tuple-element.49, f32[8,1,1024]{2,1,0:T(1,128)S(1)} %collective-permute-done.9, f32[8,64,1024]{2,1,0:T(8,128)S(1)} %fusion.50, ...), kind=kLoop, calls=%fused_computation.98 | loop fusion | flops 48234496 | bytes 37216256 | tf_op jit(solution)/shard_map/mul | solution.py:100
  106.5 12.6 %all-to-all-start = ((f32[32,1,1536]{2,1,0:T(1,128)}), f32[32,1,1536]{2,1,0:T(1,128)S(1)}, u32[]{:S(2)}, u32[]{:S(2)}) async-start(f32[32,1,1536]{2,1,0:T(1,128)} %reshape.96), calls=%async_computation | async-start | bytes 393216 | tf_op jit(solution)/shard_map/all_to_all | solution.py:120
  119.1 9.8 %all-to-all-done = f32[32,1,1536]{2,1,0:T(1,128)S(1)} async-done(((f32[32,1,1536]{2,1,0:T(1,128)}), f32[32,1,1536]{2,1,0:T(1,128)S(1)}, u32[]{:S(2)}, u32[]{:S(2)}) %all-to-all-start) | async-done | bytes 196640 | tf_op jit(solution)/shard_map/all_to_all | solution.py:120
  133.1 5.5 %collective-permute-start.10 = (f32[3,3,32,128]{3,2,1,0:T(8,128)S(1)}, f32[3,3,32,128]{3,2,1,0:T(8,128)S(1)}, u32[]{:S(2)}, u32[]{:S(2)}) collective-permute-start(f32[3,3,32,128]{3,2,1,0:T(8,128)S(1)} %get-tuple-element.67), channel_id=1, source_target_pairs={{0,4},{4,8},{8,12},{12,16},{16,20},{20,24},{24,28},{28,32},{32,36}... | collective-permute-start | bytes 442376 | tf_op jit(solution)/shard_map/ppermute | solution.py:136
  141.5 3.1 %collective-permute-start.13 = (f32[3,14,8,128]{3,2,1,0:T(8,128)S(1)}, f32[3,14,8,128]{3,2,1,0:T(8,128)S(1)}, u32[]{:S(2)}, u32[]{:S(2)}) collective-permute-start(f32[3,14,8,128]{3,2,1,0:T(8,128)S(1)} %get-tuple-element.66), channel_id=1, source_target_pairs={{1,0},{2,1},{3,2},{5,4},{6,5},{7,6},{9,8},{10,9},{11,10},{13,12},{... | collective-permute-start | bytes 516104 | tf_op jit(solution)/shard_map/ppermute | solution.py:137
  144.6 3.8 %collective-permute-start.12 = (f32[3,14,8,128]{3,2,1,0:T(8,128)S(1)}, f32[3,14,8,128]{3,2,1,0:T(8,128)S(1)}, u32[]{:S(2)}, u32[]{:S(2)}) collective-permute-start(f32[3,14,8,128]{3,2,1,0:T(8,128)S(1)} %get-tuple-element.65), channel_id=1, source_target_pairs={{0,1},{1,2},{2,3},{4,5},{5,6},{6,7},{8,9},{9,10},{10,11},{12,13},{... | collective-permute-start | bytes 516104 | tf_op jit(solution)/shard_map/ppermute | solution.py:136
  153.2 17.6 %all_to_all.10 = f32[32,1,1536]{2,1,0:T(1,128)S(1)} all-to-all(f32[32,1,1536]{2,1,0:T(1,128)S(1)} %reshape.98), channel_id=1, replica_groups=mesh['slab'=32,'gy'=4] {'slab'}, dimensions={0} | all-to-all | bytes 393216 | tf_op jit(solution)/shard_map/all_to_all | solution.py:175
  175.4 3.3 %multiply_bitcast_fusion = f32[8,64,1024]{2,1,0:T(8,128)} fusion(f32[8,32,1024]{2,1,0:T(8,128)S(1)} %convolution_bitcast_fusion, f32[32,64]{1,0:T(8,128)S(1)} %copy-done.14), kind=kOutput, calls=%fused_computation.102 | convolution fusion | flops 201850880 | bytes 3153920 | tf_op jit(solution)/shard_map/hc,qhk->qck/dot_general | solution.py:179
  (100 shorter events, 36.8 us)
Async XLA Ops:
  0.6 102.6 %copy-start = (f32[256,1024]{1,0:T(8,128)S(1)}, f32[256,1024]{1,0:T(8,128)}, u32[]{:S(2)}) copy-start(f32[256,1024]{1,0:T(8,128)} %param.23) | copy-start | bytes 3145732
  8.6 27.4 %collective-permute-start.3 = (f32[2,8,1,1024]{3,2,1,0:T(1,128)}, f32[2,8,1,1024]{3,2,1,0:T(1,128)S(1)}, u32[]{:S(2)}, u32[]{:S(2)}) collective-permute-start(f32[2,8,1,1024]{3,2,1,0:T(1,128)} %get-tuple-element.40), channel_id=1, source_target_pairs={{0,1},{1,2},{2,3},{4,5},{5,6},{6,7},{8,9},{9,10},{10,11},{12,13},{... | collective-permute-start | bytes 196616 | tf_op jit(solution)/shard_map/ppermute | solution.py:18
  13.1 22.9 %collective-permute-start.2 = (f32[2,8,1,1024]{3,2,1,0:T(1,128)S(1)}, f32[2,8,1,1024]{3,2,1,0:T(1,128)S(1)}, u32[]{:S(2)}, u32[]{:S(2)}) collective-permute-start(f32[2,8,1,1024]{3,2,1,0:T(1,128)S(1)} %get-tuple-element.39), channel_id=1, source_target_pairs={{1,0},{2,1},{3,2},{5,4},{6,5},{7,6},{9,8},{10,9},{11,10},{13,12},{... | collective-permute-start | bytes 196616 | tf_op jit(solution)/shard_map/ppermute | solution.py:19
  16.1 19.9 %collective-permute-start.1 = (f32[2,1,64,1024]{3,2,1,0:T(8,128)}, f32[2,1,64,1024]{3,2,1,0:T(8,128)}, u32[]{:S(2)}, u32[]{:S(2)}) collective-permute-start(f32[2,1,64,1024]{3,2,1,0:T(8,128)} %get-tuple-element.36), channel_id=1, source_target_pairs={{0,4},{4,8},{8,12},{12,16},{16,20},{20,24},{24,28},{28,32},{32,36}... | collective-permute-start | bytes 1572872 | tf_op jit(solution)/shard_map/ppermute | solution.py:18
  21.2 23.0 %collective-permute-start = (f32[2,1,64,1024]{3,2,1,0:T(8,128)}, f32[2,1,64,1024]{3,2,1,0:T(8,128)}, u32[]{:S(2)}, u32[]{:S(2)}) collective-permute-start(f32[2,1,64,1024]{3,2,1,0:T(8,128)} %get-tuple-element.35), channel_id=1, source_target_pairs={{4,0},{8,4},{12,8},{16,12},{20,16},{24,20},{28,24},{32,28},{36,32}... | collective-permute-start | bytes 1572872 | tf_op jit(solution)/shard_map/ppermute | solution.py:19
  32.3 12.0 %copy-start.3 = (f32[2,8,64,1023]{3,2,1,0:T(8,128)S(1)}, f32[2,8,64,1023]{3,2,1,0:T(8,128)}, u32[]{:S(2)}) copy-start(f32[2,8,64,1023]{3,2,1,0:T(8,128)} %fusion) | copy-start | bytes 12570628
  32.3 12.0 %copy-start.4 = (f32[2,8,64,1024]{3,2,1,0:T(8,128)S(1)}, f32[2,8,64,1024]{3,2,1,0:T(8,128)}, u32[]{:S(2)}) copy-start(f32[2,8,64,1024]{3,2,1,0:T(8,128)} %select_maximum_fusion) | copy-start | bytes 12582916
  32.3 12.0 %copy-start.5 = (f32[2,7,64,1024]{3,2,1,0:T(8,128)S(1)}, f32[2,7,64,1024]{3,2,1,0:T(8,128)}, u32[]{:S(2)}) copy-start(f32[2,7,64,1024]{3,2,1,0:T(8,128)} %get-tuple-element.33) | copy-start | bytes 11010052
  56.2 16.0 %collective-permute-start.4 = (f32[1,64,1024]{2,1,0:T(8,128)S(1)}, f32[1,64,1024]{2,1,0:T(8,128)S(1)}, u32[]{:S(2)}, u32[]{:S(2)}) collective-permute-start(f32[1,64,1024]{2,1,0:T(8,128)S(1)} %get-tuple-element.58), channel_id=1, source_target_pairs={{4,0},{8,4},{12,8},{16,12},{20,16},{24,20},{28,24},{32,28},{36,32}... | collective-permute-start | bytes 786440 | tf_op jit(solution)/shard_map/ppermute | solution.py:19
  57.5 14.7 %collective-permute-start.5 = (f32[1,64,1024]{2,1,0:T(8,128)S(1)}, f32[1,64,1024]{2,1,0:T(8,128)S(1)}, u32[]{:S(2)}, u32[]{:S(2)}) collective-permute-start(f32[1,64,1024]{2,1,0:T(8,128)S(1)} %get-tuple-element.57), channel_id=1, source_target_pairs={{0,4},{4,8},{8,12},{12,16},{16,20},{20,24},{24,28},{28,32},{32,36}... | collective-permute-start | bytes 786440 | tf_op jit(solution)/shard_map/ppermute | solution.py:18
  63.0 9.2 %collective-permute-start.6 = (f32[8,1,1024]{2,1,0:T(1,128)S(1)}, f32[8,1,1024]{2,1,0:T(1,128)S(1)}, u32[]{:S(2)}, u32[]{:S(2)}) collective-permute-start(f32[8,1,1024]{2,1,0:T(1,128)S(1)} %get-tuple-element.54), channel_id=1, source_target_pairs={{1,0},{2,1},{3,2},{5,4},{6,5},{7,6},{9,8},{10,9},{11,10},{13,12},{... | collective-permute-start | bytes 98312 | tf_op jit(solution)/shard_map/ppermute | solution.py:19
  64.9 8.1 %copy-start.6 = (f32[8,64,1024]{2,1,0:T(8,128)S(1)}, f32[8,64,1024]{2,1,0:T(8,128)}, u32[]{:S(2)}) copy-start(f32[8,64,1024]{2,1,0:T(8,128)} %param.17) | copy-start | bytes 6291460
  64.9 7.2 %collective-permute-start.7 = (f32[8,1,1024]{2,1,0:T(1,128)S(1)}, f32[8,1,1024]{2,1,0:T(1,128)S(1)}, u32[]{:S(2)}, u32[]{:S(2)}) collective-permute-start(f32[8,1,1024]{2,1,0:T(1,128)S(1)} %get-tuple-element.53), channel_id=1, source_target_pairs={{0,1},{1,2},{2,3},{4,5},{5,6},{6,7},{8,9},{9,10},{10,11},{12,13},{... | collective-permute-start | bytes 98312 | tf_op jit(solution)/shard_map/ppermute | solution.py:18
  82.2 10.3 %copy-start.1 = (f32[8,64,1024]{2,1,0:T(8,128)}, f32[8,64,1024]{2,1,0:T(8,128)S(1)}, u32[]{:S(2)}) copy-start(f32[8,64,1024]{2,1,0:T(8,128)S(1)} %fusion.50) | copy-start | bytes 6291460
  85.9 6.0 %collective-permute-start.8 = (f32[8,1,1024]{2,1,0:T(1,128)S(1)}, f32[8,1,1024]{2,1,0:T(1,128)S(1)}, u32[]{:S(2)}, u32[]{:S(2)}) collective-permute-start(f32[8,1,1024]{2,1,0:T(1,128)S(1)} %get-tuple-element.48), channel_id=1, source_target_pairs={{1,0},{2,1},{3,2},{5,4},{6,5},{7,6},{9,8},{10,9},{11,10},{13,12},{... | collective-permute-start | bytes 98312 | tf_op jit(solution)/shard_map/ppermute | solution.py:19
  87.8 4.7 %collective-permute-start.9 = (f32[8,1,1024]{2,1,0:T(1,128)S(1)}, f32[8,1,1024]{2,1,0:T(1,128)S(1)}, u32[]{:S(2)}, u32[]{:S(2)}) collective-permute-start(f32[8,1,1024]{2,1,0:T(1,128)S(1)} %get-tuple-element.47), channel_id=1, source_target_pairs={{0,1},{1,2},{2,3},{4,5},{5,6},{6,7},{8,9},{9,10},{10,11},{12,13},{... | collective-permute-start | bytes 98312 | tf_op jit(solution)/shard_map/ppermute | solution.py:18
  92.5 9.2 %copy-start.14 = (f32[32,64]{1,0:T(8,128)S(1)}, f32[32,64]{1,0:T(8,128)}, u32[]{:S(2)}) copy-start(f32[32,64]{1,0:T(8,128)} %param.22) | copy-start | bytes 24580
  105.1 14.0 %copy-start.13 = (f32[8,32,128]{2,1,0:T(8,128)S(1)}, f32[8,32,128]{2,1,0:T(8,128)}, u32[]{:S(2)}) copy-start(f32[8,32,128]{2,1,0:T(8,128)} %param.24) | copy-start | bytes 393220
  106.5 22.4 %all-to-all-start = ((f32[32,1,1536]{2,1,0:T(1,128)}), f32[32,1,1536]{2,1,0:T(1,128)S(1)}, u32[]{:S(2)}, u32[]{:S(2)}) async-start(f32[32,1,1536]{2,1,0:T(1,128)} %reshape.96), calls=%async_computation | async-start | bytes 393216 | tf_op jit(solution)/shard_map/all_to_all | solution.py:120
  131.8 8.8 %collective-permute-start.11 = (f32[3,3,32,128]{3,2,1,0:T(8,128)S(1)}, f32[3,3,32,128]{3,2,1,0:T(8,128)S(1)}, u32[]{:S(2)}, u32[]{:S(2)}) collective-permute-start(f32[3,3,32,128]{3,2,1,0:T(8,128)S(1)} %get-tuple-element.68), channel_id=1, source_target_pairs={{4,0},{8,4},{12,8},{16,12},{20,16},{24,20},{28,24},{32,28},{36,32}... | collective-permute-start | bytes 442376 | tf_op jit(solution)/shard_map/ppermute | solution.py:137
  133.1 8.4 %collective-permute-start.10 = (f32[3,3,32,128]{3,2,1,0:T(8,128)S(1)}, f32[3,3,32,128]{3,2,1,0:T(8,128)S(1)}, u32[]{:S(2)}, u32[]{:S(2)}) collective-permute-start(f32[3,3,32,128]{3,2,1,0:T(8,128)S(1)} %get-tuple-element.67), channel_id=1, source_target_pairs={{0,4},{4,8},{8,12},{12,16},{16,20},{20,24},{24,28},{28,32},{32,36}... | collective-permute-start | bytes 442376 | tf_op jit(solution)/shard_map/ppermute | solution.py:136
  141.5 8.1 %collective-permute-start.13 = (f32[3,14,8,128]{3,2,1,0:T(8,128)S(1)}, f32[3,14,8,128]{3,2,1,0:T(8,128)S(1)}, u32[]{:S(2)}, u32[]{:S(2)}) collective-permute-start(f32[3,14,8,128]{3,2,1,0:T(8,128)S(1)} %get-tuple-element.66), channel_id=1, source_target_pairs={{1,0},{2,1},{3,2},{5,4},{6,5},{7,6},{9,8},{10,9},{11,10},{13,12},{... | collective-permute-start | bytes 516104 | tf_op jit(solution)/shard_map/ppermute | solution.py:137
  144.6 6.2 %collective-permute-start.12 = (f32[3,14,8,128]{3,2,1,0:T(8,128)S(1)}, f32[3,14,8,128]{3,2,1,0:T(8,128)S(1)}, u32[]{:S(2)}, u32[]{:S(2)}) collective-permute-start(f32[3,14,8,128]{3,2,1,0:T(8,128)S(1)} %get-tuple-element.65), channel_id=1, source_target_pairs={{0,1},{1,2},{2,3},{4,5},{5,6},{6,7},{8,9},{9,10},{10,11},{12,13},{... | collective-permute-start | bytes 516104 | tf_op jit(solution)/shard_map/ppermute | solution.py:136
  151.8 20.0 %copy-start.9 = (f32[8,32,128]{2,1,0:T(8,128)}, f32[8,32,128]{2,1,0:T(8,128)S(1)}, u32[]{:S(2)}) copy-start(f32[8,32,128]{2,1,0:T(8,128)S(1)} %fusion.94) | copy-start | bytes 393220
  (8 other events, 20.9 us)

commit v5 on v4

--- a/solution.py
+++ b/solution.py
@@ -175,9 +175,9 @@
     got_warm = lax.all_to_all(windows, "slab", 0, 0, tiled=False)
     spread = jnp.einsum("skcb,kx->scbx", got_warm, columns, precision=upper_limit)
     third = restrict_matrix_third.reshape(slabs, chunk_c, restrict_matrix_third.shape[1])
-    raised_field = jnp.einsum("scbx,scz->xbz", spread, third, precision=upper_limit)
+    spread_y = jnp.einsum("scbx,by->scxy", spread, restrict_matrix_second, precision=upper_limit)
     fine_mesh_warming = 16.0 * jnp.einsum(
-        "hc,qhk->qck", restrict_matrix_second, raised_field, precision=upper_limit
+        "scxy,scz->xyz", spread_y, third, precision=upper_limit
     )
     return (electron_concentration, warming_distribution, fine_mesh_warming)
 

time: 181 us -> 178 us (0.983)
  no operation moved by 1% of the time
where the time goes in v5:
time: 178 us; the launch traced here: 176 us
  starting transfers between devices  57.7 us (32%)
  other arithmetic  50.8 us (29%)
  waiting for transfers between devices  24.7 us (14%)
  blocking collectives  17.6 us (10%)
  local copies, waits for them, and re-layouts  13.6 us (8%)
  matrix products  10.5 us (6%)
    ppermute x5, starting transfers between devices, face_halos(): lax.ppermute(lax.slice_in_dim(block, size - 1, size, axis=dim), axis, for...  23.1 us
    div x2, other arithmetic, sweep(): return fraction_top_quantity / denominator_quantity  18.4 us
    all_to_all x1, blocking collectives, per_device(): got_warm = lax.all_to_all(windows, 'slab', 0, 0, tiled=False)  17.6 us
    another operation x6, other arithmetic, per_device(): both = jnp.stack([effective, initial_electrons])  14.6 us
    all_to_all x1, starting transfers between devices, per_device(): got = lax.all_to_all(piece, 'slab', 0, 0, tiled=False)  12.6 us
    all_to_all x1, waiting for transfers between devices, per_device(): got = lax.all_to_all(piece, 'slab', 0, 0, tiled=False)  9.8 us
    ppermute x5, waiting for transfers between devices, face_halos(): high = lax.ppermute(lax.slice_in_dim(block, 0, 1, axis=dim), axis, backward)  9.4 us
    ppermute x2, starting transfers between devices, per_device(): lax.ppermute(lax.slice_in_dim(stacked, size - depth, size, axis=dim), axi...  9.33 us
  transfers between devices with their start and end apart: 15, of which 7 were waited for; matrix products, arithmetic and copies ran while one was open for 10% of the time, Pallas kernels for 0%

profile of v5, /device:TPU:1, one launch (start us, length us, event | category | flops | bytes accessed | tf_op | source)
XLA Modules:
  0.0 176.0 jit_solution(13066990152881664576)
XLA Ops:
  2.1 5.8 %select_add_fusion = f32[8,64,1024]{2,1,0:T(8,128)S(1)} fusion(f32[8,64,1024]{2,1,0:T(8,128)} %param.15, s32[8,64,1024]{2,1,0:T(8,128)} %param.19, f32[]{:T(128)} %bitcast.3, f32[]{:T(128)} %bitcast.2, f32[]{:T(128)} %bitcast.1, f32[]{:T(128)} %bitcast), kind=kLoop, calls=%fused_computation.118 | loop fusion | flops 6291456 | bytes 6291472 | tf_op jit(solution)/shard_map/add | solution.py:64
  8.6 4.5 %collective-permute-start.3 = (f32[2,8,1,1024]{3,2,1,0:T(1,128)}, f32[2,8,1,1024]{3,2,1,0:T(1,128)S(1)}, u32[]{:S(2)}, u32[]{:S(2)}) collective-permute-start(f32[2,8,1,1024]{3,2,1,0:T(1,128)} %get-tuple-element.40), channel_id=1, source_target_pairs={{0,1},{1,2},{2,3},{4,5},{5,6},{6,7},{8,9},{9,10},{10,11},{12,13},{... | collective-permute-start | bytes 196616 | tf_op jit(solution)/shard_map/ppermute | solution.py:18
  16.1 4.4 %collective-permute-start.1 = (f32[2,1,64,1024]{3,2,1,0:T(8,128)}, f32[2,1,64,1024]{3,2,1,0:T(8,128)S(1)}, u32[]{:S(2)}, u32[]{:S(2)}) collective-permute-start(f32[2,1,64,1024]{3,2,1,0:T(8,128)} %get-tuple-element.36), channel_id=1, source_target_pairs={{0,4},{4,8},{8,12},{12,16},{16,20},{20,24},{24,28},{28,32},{32,36}... | collective-permute-start | bytes 1572872 | tf_op jit(solution)/shard_map/ppermute | solution.py:18
  21.8 3.1 %fusion = f32[2,8,64,1023]{3,2,1,0:T(8,128)} fusion(f32[1,8,64,1024]{3,2,1,0:T(8,128)S(1)} %bitcast.209, f32[1,8,64,1024]{3,2,1,0:T(8,128)S(1)} %bitcast.216), kind=kLoop, calls=%fused_computation.18 | loop fusion | flops 1047552 | bytes 8384512 | tf_op jit(solution)/shard_map/stack | solution.py:68
  24.9 3.2 %select_maximum_fusion = f32[2,8,64,1024]{3,2,1,0:T(8,128)} fusion(f32[1,8,64,1024]{3,2,1,0:T(8,128)S(1)} %bitcast.217, f32[1,8,64,1024]{3,2,1,0:T(8,128)S(1)} %bitcast.210), kind=kLoop, calls=%fused_computation.21 | loop fusion | flops 4194304 | bytes 8388608 | tf_op jit(solution)/shard_map/stack | solution.py:68
  28.1 3.4 %fusion.3 = (f32[2,7,64,1024]{3,2,1,0:T(8,128)}, f32[2,7,64,1024]{3,2,1,0:T(8,128)}) fusion(f32[1,8,64,1024]{3,2,1,0:T(8,128)S(1)} %bitcast.211, f32[1,8,64,1024]{3,2,1,0:T(8,128)S(1)} %bitcast.218), kind=kLoop, calls=%fused_computation.33 | loop fusion | flops 1835008 | bytes 11534336 | tf_op jit(solution)/shard_map/stack | solution.py:68
  31.6 3.1 %fusion.1 = (f32[2,8,63,1024]{3,2,1,0:T(8,128)S(1)}, f32[2,8,63,1024]{3,2,1,0:T(8,128)S(1)}) fusion(f32[1,8,64,1024]{3,2,1,0:T(8,128)S(1)} %bitcast.212, f32[1,8,64,1024]{3,2,1,0:T(8,128)} %bitcast.213), kind=kLoop, calls=%fused_computation.19 | loop fusion | flops 2064384 | bytes 12451840 | tf_op jit(solution)/shard_map/stack | solution.py:68
  34.8 9.4 %collective-permute-done = f32[2,1,64,1024]{3,2,1,0:T(8,128)S(1)} collective-permute-done((f32[2,1,64,1024]{3,2,1,0:T(8,128)}, f32[2,1,64,1024]{3,2,1,0:T(8,128)S(1)}, u32[]{:S(2)}, u32[]{:S(2)}) %collective-permute-start) | collective-permute-done | bytes 524320 | tf_op jit(solution)/shard_map/ppermute | solution.py:19
  44.2 9.0 %fusion.17 = (f32[8,64,1024]{2,1,0:T(8,128)S(1)}, f32[8,64,1024]{2,1,0:T(8,128)S(1)}, f32[8,64,1024]{2,1,0:T(8,128)S(1)}) fusion(f32[2,8,64,1023]{3,2,1,0:T(8,128)S(1)} %copy-done.3, f32[2,8,64,1024]{3,2,1,0:T(8,128)S(1)} %copy-done.4, f32[2,8,63,1024]{3,2,1,0:T(8,128)S(1)} %get-tuple-element.38, f32[2,8,1,1024]{3,2,1,0:T(1,128)S(1)} %collective-permute-done.3, ...), kind=kLoop, calls=%fused_computation.47 | loop fusion | flops 45613056 | bytes 37744640 | tf_op jit(solution)/shard_map/div | solution.py:82
  53.9 2.1 %fusion.129 = (f32[8,64,1023]{2,1,0:T(8,128)S(1)}, f32[8,64,1023]{2,1,0:T(8,128)}) fusion(f32[8,64,1024]{2,1,0:T(8,128)S(1)} %get-tuple-element.30), kind=kLoop, calls=%fused_computation.234 | loop fusion | bytes 8380416 | tf_op jit(solution)/shard_map/slice | solution.py:34
  57.3 5.5 %collective-permute-start.5 = (f32[1,64,1024]{2,1,0:T(8,128)S(1)}, f32[1,64,1024]{2,1,0:T(8,128)S(1)}, u32[]{:S(2)}, u32[]{:S(2)}) collective-permute-start(f32[1,64,1024]{2,1,0:T(8,128)S(1)} %get-tuple-element.57), channel_id=1, source_target_pairs={{0,4},{4,8},{8,12},{12,16},{16,20},{20,24},{24,28},{28,32},{32,36}... | collective-permute-start | bytes 786440 | tf_op jit(solution)/shard_map/ppermute | solution.py:18
  64.8 4.9 %collective-permute-start.7 = (f32[8,1,1024]{2,1,0:T(1,128)S(1)}, f32[8,1,1024]{2,1,0:T(1,128)S(1)}, u32[]{:S(2)}, u32[]{:S(2)}) collective-permute-start(f32[8,1,1024]{2,1,0:T(1,128)S(1)} %get-tuple-element.53), channel_id=1, source_target_pairs={{0,1},{1,2},{2,3},{4,5},{5,6},{6,7},{8,9},{9,10},{10,11},{12,13},{... | collective-permute-start | bytes 98312 | tf_op jit(solution)/shard_map/ppermute | solution.py:18
  69.6 2.3 %fusion.133 = (f32[7,64,1024]{2,1,0:T(8,128)}, f32[7,64,1024]{2,1,0:T(8,128)}) fusion(f32[8,64,1024]{2,1,0:T(8,128)S(1)} %get-tuple-element.30), kind=kLoop, calls=%fused_computation.238 | loop fusion | bytes 7340032 | tf_op jit(solution)/shard_map/slice | solution.py:30
  72.0 9.4 %fusion.50 = f32[8,64,1024]{2,1,0:T(8,128)S(1)} fusion(f32[8,64,1024]{2,1,0:T(8,128)S(1)} %copy-done.6, f32[1,64,1024]{2,1,0:T(8,128)S(1)} %collective-permute-done.4, f32[7,64,1024]{2,1,0:T(8,128)} %get-tuple-element.60, f32[7,64,1024]{2,1,0:T(8,128)} %get-tuple-element.59, f32[1,64,1024]{2,1,0:T(8,128)S(1)} %collective-permute-done.5, ...), kind=kLoop, calls=%fused_computation.87 | loop fusion | flops 43515904 | bytes 39837696 | tf_op jit(solution)/shard_map/div | solution.py:82
  86.2 3.8 %collective-permute-start.9 = (f32[8,1,1024]{2,1,0:T(1,128)S(1)}, f32[8,1,1024]{2,1,0:T(1,128)S(1)}, u32[]{:S(2)}, u32[]{:S(2)}) collective-permute-start(f32[8,1,1024]{2,1,0:T(1,128)S(1)} %get-tuple-element.47), channel_id=1, source_target_pairs={{0,1},{1,2},{2,3},{4,5},{5,6},{6,7},{8,9},{9,10},{10,11},{12,13},{... | collective-permute-start | bytes 98312 | tf_op jit(solution)/shard_map/ppermute | solution.py:18
  90.8 8.2 %fusion.57 = f32[8,64,1024]{2,1,0:T(8,128)S(1)} fusion(f32[8,1,1024]{2,1,0:T(1,128)S(1)} %collective-permute-done.8, f32[8,63,1024]{2,1,0:T(8,128)S(1)} %get-tuple-element.50, f32[8,63,1024]{2,1,0:T(8,128)S(1)} %get-tuple-element.49, f32[8,1,1024]{2,1,0:T(1,128)S(1)} %collective-permute-done.9, f32[8,64,1024]{2,1,0:T(8,128)S(1)} %fusion.50, ...), kind=kLoop, calls=%fused_computation.98 | loop fusion | flops 48234496 | bytes 37216256 | tf_op jit(solution)/shard_map/mul | solution.py:100
  103.9 12.6 %all-to-all-start = ((f32[32,1,1536]{2,1,0:T(1,128)}), f32[32,1,1536]{2,1,0:T(1,128)S(1)}, u32[]{:S(2)}, u32[]{:S(2)}) async-start(f32[32,1,1536]{2,1,0:T(1,128)} %reshape.97), calls=%async_computation | async-start | bytes 393216 | tf_op jit(solution)/shard_map/all_to_all | solution.py:120
  116.5 9.8 %all-to-all-done = f32[32,1,1536]{2,1,0:T(1,128)S(1)} async-done(((f32[32,1,1536]{2,1,0:T(1,128)}), f32[32,1,1536]{2,1,0:T(1,128)S(1)}, u32[]{:S(2)}, u32[]{:S(2)}) %all-to-all-start) | async-done | bytes 196640 | tf_op jit(solution)/shard_map/all_to_all | solution.py:120
  130.5 5.5 %collective-permute-start.10 = (f32[3,3,32,128]{3,2,1,0:T(8,128)S(1)}, f32[3,3,32,128]{3,2,1,0:T(8,128)S(1)}, u32[]{:S(2)}, u32[]{:S(2)}) collective-permute-start(f32[3,3,32,128]{3,2,1,0:T(8,128)S(1)} %get-tuple-element.67), channel_id=1, source_target_pairs={{0,4},{4,8},{8,12},{12,16},{16,20},{20,24},{24,28},{28,32},{32,36}... | collective-permute-start | bytes 442376 | tf_op jit(solution)/shard_map/ppermute | solution.py:136
  136.0 2.0 %collective-permute-done.11 = f32[3,3,32,128]{3,2,1,0:T(8,128)S(1)} collective-permute-done((f32[3,3,32,128]{3,2,1,0:T(8,128)S(1)}, f32[3,3,32,128]{3,2,1,0:T(8,128)S(1)}, u32[]{:S(2)}, u32[]{:S(2)}) %collective-permute-start.11) | collective-permute-done | bytes 147488 | tf_op jit(solution)/shard_map/ppermute | solution.py:137
  138.9 3.1 %collective-permute-start.13 = (f32[3,14,8,128]{3,2,1,0:T(8,128)S(1)}, f32[3,14,8,128]{3,2,1,0:T(8,128)S(1)}, u32[]{:S(2)}, u32[]{:S(2)}) collective-permute-start(f32[3,14,8,128]{3,2,1,0:T(8,128)S(1)} %get-tuple-element.66), channel_id=1, source_target_pairs={{1,0},{2,1},{3,2},{5,4},{6,5},{7,6},{9,8},{10,9},{11,10},{13,12},{... | collective-permute-start | bytes 516104 | tf_op jit(solution)/shard_map/ppermute | solution.py:137
  142.0 3.8 %collective-permute-start.12 = (f32[3,14,8,128]{3,2,1,0:T(8,128)S(1)}, f32[3,14,8,128]{3,2,1,0:T(8,128)S(1)}, u32[]{:S(2)}, u32[]{:S(2)}) collective-permute-start(f32[3,14,8,128]{3,2,1,0:T(8,128)S(1)} %get-tuple-element.65), channel_id=1, source_target_pairs={{0,1},{1,2},{2,3},{4,5},{5,6},{6,7},{8,9},{9,10},{10,11},{12,13},{... | collective-permute-start | bytes 516104 | tf_op jit(solution)/shard_map/ppermute | solution.py:136
  150.6 17.6 %all_to_all.10 = f32[32,1,1536]{2,1,0:T(1,128)S(1)} all-to-all(f32[32,1,1536]{2,1,0:T(1,128)S(1)} %reshape.99), channel_id=1, replica_groups=mesh['slab'=32,'gy'=4] {'slab'}, dimensions={0} | all-to-all | bytes 393216 | tf_op jit(solution)/shard_map/all_to_all | solution.py:175
  172.3 3.8 %bitcast_multiply_fusion = f32[8,64,1024]{2,1,0:T(8,128)} fusion(f32[32,8,8,64]{3,0,1,2:T(8,128)S(1)} %fusion.66, f32[32,8,1024]{2,1,0:T(8,128)S(1)} %bitcast.219), kind=kOutput, calls=%fused_computation.102 | convolution fusion | flops 1611137024 | bytes 3670016 | tf_op jit(solution)/shard_map/scxy,scz->xyz/dot_general | solution.py:179
  (92 shorter events, 34.6 us)
Async XLA Ops:
  0.6 98.4 %copy-start = (f32[32,64]{1,0:T(8,128)S(1)}, f32[32,64]{1,0:T(8,128)}, u32[]{:S(2)}) copy-start(f32[32,64]{1,0:T(8,128)} %param.22) | copy-start | bytes 24580
  8.6 26.2 %collective-permute-start.3 = (f32[2,8,1,1024]{3,2,1,0:T(1,128)}, f32[2,8,1,1024]{3,2,1,0:T(1,128)S(1)}, u32[]{:S(2)}, u32[]{:S(2)}) collective-permute-start(f32[2,8,1,1024]{3,2,1,0:T(1,128)} %get-tuple-element.40), channel_id=1, source_target_pairs={{0,1},{1,2},{2,3},{4,5},{5,6},{6,7},{8,9},{9,10},{10,11},{12,13},{... | collective-permute-start | bytes 196616 | tf_op jit(solution)/shard_map/ppermute | solution.py:18
  13.1 21.7 %collective-permute-start.2 = (f32[2,8,1,1024]{3,2,1,0:T(1,128)S(1)}, f32[2,8,1,1024]{3,2,1,0:T(1,128)S(1)}, u32[]{:S(2)}, u32[]{:S(2)}) collective-permute-start(f32[2,8,1,1024]{3,2,1,0:T(1,128)S(1)} %get-tuple-element.39), channel_id=1, source_target_pairs={{1,0},{2,1},{3,2},{5,4},{6,5},{7,6},{9,8},{10,9},{11,10},{13,12},{... | collective-permute-start | bytes 196616 | tf_op jit(solution)/shard_map/ppermute | solution.py:19
  16.1 18.7 %collective-permute-start.1 = (f32[2,1,64,1024]{3,2,1,0:T(8,128)}, f32[2,1,64,1024]{3,2,1,0:T(8,128)S(1)}, u32[]{:S(2)}, u32[]{:S(2)}) collective-permute-start(f32[2,1,64,1024]{3,2,1,0:T(8,128)} %get-tuple-element.36), channel_id=1, source_target_pairs={{0,4},{4,8},{8,12},{12,16},{16,20},{20,24},{24,28},{28,32},{32,36}... | collective-permute-start | bytes 1572872 | tf_op jit(solution)/shard_map/ppermute | solution.py:18
  20.5 23.7 %collective-permute-start = (f32[2,1,64,1024]{3,2,1,0:T(8,128)}, f32[2,1,64,1024]{3,2,1,0:T(8,128)S(1)}, u32[]{:S(2)}, u32[]{:S(2)}) collective-permute-start(f32[2,1,64,1024]{3,2,1,0:T(8,128)} %get-tuple-element.35), channel_id=1, source_target_pairs={{4,0},{8,4},{12,8},{16,12},{20,16},{24,20},{28,24},{32,28},{36,32}... | collective-permute-start | bytes 1572872 | tf_op jit(solution)/shard_map/ppermute | solution.py:19
  31.6 12.6 %copy-start.3 = (f32[2,8,64,1023]{3,2,1,0:T(8,128)S(1)}, f32[2,8,64,1023]{3,2,1,0:T(8,128)}, u32[]{:S(2)}) copy-start(f32[2,8,64,1023]{3,2,1,0:T(8,128)} %fusion) | copy-start | bytes 12570628
  31.6 12.6 %copy-start.4 = (f32[2,8,64,1024]{3,2,1,0:T(8,128)S(1)}, f32[2,8,64,1024]{3,2,1,0:T(8,128)}, u32[]{:S(2)}) copy-start(f32[2,8,64,1024]{3,2,1,0:T(8,128)} %select_maximum_fusion) | copy-start | bytes 12582916
  31.6 12.6 %copy-start.5 = (f32[2,7,64,1024]{3,2,1,0:T(8,128)S(1)}, f32[2,7,64,1024]{3,2,1,0:T(8,128)}, u32[]{:S(2)}) copy-start(f32[2,7,64,1024]{3,2,1,0:T(8,128)} %get-tuple-element.33) | copy-start | bytes 11010052
  56.0 15.9 %collective-permute-start.4 = (f32[1,64,1024]{2,1,0:T(8,128)S(1)}, f32[1,64,1024]{2,1,0:T(8,128)S(1)}, u32[]{:S(2)}, u32[]{:S(2)}) collective-permute-start(f32[1,64,1024]{2,1,0:T(8,128)S(1)} %get-tuple-element.58), channel_id=1, source_target_pairs={{4,0},{8,4},{12,8},{16,12},{20,16},{24,20},{28,24},{32,28},{36,32}... | collective-permute-start | bytes 786440 | tf_op jit(solution)/shard_map/ppermute | solution.py:19
  57.3 14.7 %collective-permute-start.5 = (f32[1,64,1024]{2,1,0:T(8,128)S(1)}, f32[1,64,1024]{2,1,0:T(8,128)S(1)}, u32[]{:S(2)}, u32[]{:S(2)}) collective-permute-start(f32[1,64,1024]{2,1,0:T(8,128)S(1)} %get-tuple-element.57), channel_id=1, source_target_pairs={{0,4},{4,8},{8,12},{12,16},{16,20},{20,24},{24,28},{28,32},{32,36}... | collective-permute-start | bytes 786440 | tf_op jit(solution)/shard_map/ppermute | solution.py:18
  62.8 9.1 %collective-permute-start.6 = (f32[8,1,1024]{2,1,0:T(1,128)S(1)}, f32[8,1,1024]{2,1,0:T(1,128)S(1)}, u32[]{:S(2)}, u32[]{:S(2)}) collective-permute-start(f32[8,1,1024]{2,1,0:T(1,128)S(1)} %get-tuple-element.54), channel_id=1, source_target_pairs={{1,0},{2,1},{3,2},{5,4},{6,5},{7,6},{9,8},{10,9},{11,10},{13,12},{... | collective-permute-start | bytes 98312 | tf_op jit(solution)/shard_map/ppermute | solution.py:19
  64.8 7.2 %copy-start.6 = (f32[8,64,1024]{2,1,0:T(8,128)S(1)}, f32[8,64,1024]{2,1,0:T(8,128)}, u32[]{:S(2)}) copy-start(f32[8,64,1024]{2,1,0:T(8,128)} %param.17) | copy-start | bytes 6291460
  64.8 7.2 %copy-start.7 = (f32[8,64,1024]{2,1,0:T(8,128)S(1)}, f32[8,64,1024]{2,1,0:T(8,128)}, u32[]{:S(2)}) copy-start(f32[8,64,1024]{2,1,0:T(8,128)} %param.18) | copy-start | bytes 6291460
  64.8 7.2 %collective-permute-start.7 = (f32[8,1,1024]{2,1,0:T(1,128)S(1)}, f32[8,1,1024]{2,1,0:T(1,128)S(1)}, u32[]{:S(2)}, u32[]{:S(2)}) collective-permute-start(f32[8,1,1024]{2,1,0:T(1,128)S(1)} %get-tuple-element.53), channel_id=1, source_target_pairs={{0,1},{1,2},{2,3},{4,5},{5,6},{6,7},{8,9},{9,10},{10,11},{12,13},{... | collective-permute-start | bytes 98312 | tf_op jit(solution)/shard_map/ppermute | solution.py:18
  81.4 9.4 %copy-start.1 = (f32[8,64,1024]{2,1,0:T(8,128)}, f32[8,64,1024]{2,1,0:T(8,128)S(1)}, u32[]{:S(2)}) copy-start(f32[8,64,1024]{2,1,0:T(8,128)S(1)} %fusion.50) | copy-start | bytes 6291460
  84.3 6.0 %collective-permute-start.8 = (f32[8,1,1024]{2,1,0:T(1,128)S(1)}, f32[8,1,1024]{2,1,0:T(1,128)S(1)}, u32[]{:S(2)}, u32[]{:S(2)}) collective-permute-start(f32[8,1,1024]{2,1,0:T(1,128)S(1)} %get-tuple-element.48), channel_id=1, source_target_pairs={{1,0},{2,1},{3,2},{5,4},{6,5},{7,6},{9,8},{10,9},{11,10},{13,12},{... | collective-permute-start | bytes 98312 | tf_op jit(solution)/shard_map/ppermute | solution.py:19
  86.2 4.7 %collective-permute-start.9 = (f32[8,1,1024]{2,1,0:T(1,128)S(1)}, f32[8,1,1024]{2,1,0:T(1,128)S(1)}, u32[]{:S(2)}, u32[]{:S(2)}) collective-permute-start(f32[8,1,1024]{2,1,0:T(1,128)S(1)} %get-tuple-element.47), channel_id=1, source_target_pairs={{0,1},{1,2},{2,3},{4,5},{5,6},{6,7},{8,9},{9,10},{10,11},{12,13},{... | collective-permute-start | bytes 98312 | tf_op jit(solution)/shard_map/ppermute | solution.py:18
  102.5 14.0 %copy-start.12 = (f32[8,32,128]{2,1,0:T(8,128)S(1)}, f32[8,32,128]{2,1,0:T(8,128)}, u32[]{:S(2)}) copy-start(f32[8,32,128]{2,1,0:T(8,128)} %param.24) | copy-start | bytes 393220
  103.9 22.4 %all-to-all-start = ((f32[32,1,1536]{2,1,0:T(1,128)}), f32[32,1,1536]{2,1,0:T(1,128)S(1)}, u32[]{:S(2)}, u32[]{:S(2)}) async-start(f32[32,1,1536]{2,1,0:T(1,128)} %reshape.97), calls=%async_computation | async-start | bytes 393216 | tf_op jit(solution)/shard_map/all_to_all | solution.py:120
  129.2 8.8 %collective-permute-start.11 = (f32[3,3,32,128]{3,2,1,0:T(8,128)S(1)}, f32[3,3,32,128]{3,2,1,0:T(8,128)S(1)}, u32[]{:S(2)}, u32[]{:S(2)}) collective-permute-start(f32[3,3,32,128]{3,2,1,0:T(8,128)S(1)} %get-tuple-element.68), channel_id=1, source_target_pairs={{4,0},{8,4},{12,8},{16,12},{20,16},{24,20},{28,24},{32,28},{36,32}... | collective-permute-start | bytes 442376 | tf_op jit(solution)/shard_map/ppermute | solution.py:137
  130.5 8.4 %collective-permute-start.10 = (f32[3,3,32,128]{3,2,1,0:T(8,128)S(1)}, f32[3,3,32,128]{3,2,1,0:T(8,128)S(1)}, u32[]{:S(2)}, u32[]{:S(2)}) collective-permute-start(f32[3,3,32,128]{3,2,1,0:T(8,128)S(1)} %get-tuple-element.67), channel_id=1, source_target_pairs={{0,4},{4,8},{8,12},{12,16},{16,20},{20,24},{24,28},{28,32},{32,36}... | collective-permute-start | bytes 442376 | tf_op jit(solution)/shard_map/ppermute | solution.py:136
  138.9 8.1 %collective-permute-start.13 = (f32[3,14,8,128]{3,2,1,0:T(8,128)S(1)}, f32[3,14,8,128]{3,2,1,0:T(8,128)S(1)}, u32[]{:S(2)}, u32[]{:S(2)}) collective-permute-start(f32[3,14,8,128]{3,2,1,0:T(8,128)S(1)} %get-tuple-element.66), channel_id=1, source_target_pairs={{1,0},{2,1},{3,2},{5,4},{6,5},{7,6},{9,8},{10,9},{11,10},{13,12},{... | collective-permute-start | bytes 516104 | tf_op jit(solution)/shard_map/ppermute | solution.py:137
  142.0 6.2 %collective-permute-start.12 = (f32[3,14,8,128]{3,2,1,0:T(8,128)S(1)}, f32[3,14,8,128]{3,2,1,0:T(8,128)S(1)}, u32[]{:S(2)}, u32[]{:S(2)}) collective-permute-start(f32[3,14,8,128]{3,2,1,0:T(8,128)S(1)} %get-tuple-element.65), channel_id=1, source_target_pairs={{0,1},{1,2},{2,3},{4,5},{5,6},{6,7},{8,9},{9,10},{10,11},{12,13},{... | collective-permute-start | bytes 516104 | tf_op jit(solution)/shard_map/ppermute | solution.py:136
  149.2 20.0 %copy-start.10 = (f32[8,32,128]{2,1,0:T(8,128)}, f32[8,32,128]{2,1,0:T(8,128)S(1)}, u32[]{:S(2)}) copy-start(f32[8,32,128]{2,1,0:T(8,128)S(1)} %fusion.96) | copy-start | bytes 393220
  (4 other events, 11.7 us)

commit v6 on v5

--- a/solution.py
+++ b/solution.py
@@ -71,9 +71,23 @@
     beside_all = [b[0] for b in beside_both]
     voltage_gradients = [leftover_portion - effective for leftover_portion in beside_all]
     bernoulli_coefficients = [bernoulli(voltage_gradient) for voltage_gradient in voltage_gradients]
-    denominator_quantity = annihilation_coefficient
-    for bernoulli_coefficient, voltage_gradient in zip(bernoulli_coefficients, voltage_gradients):
-        denominator_quantity = denominator_quantity + (bernoulli_coefficient + voltage_gradient)
+    start_beside = [b[1] for b in beside_both]
+    partial_denominator = annihilation_coefficient
+    partial_top = creation_amounts
+    for d in (2, 3, 4, 5):
+        partial_denominator = partial_denominator + (
+            bernoulli_coefficients[d] + voltage_gradients[d]
+        )
+        partial_top = partial_top + bernoulli_coefficients[d] * start_beside[d]
+    partial_denominator, partial_top = lax.optimization_barrier(
+        (partial_denominator, partial_top)
+    )
+    denominator_quantity = partial_denominator
+    for d in (0, 1):
+        denominator_quantity = denominator_quantity + (
+            bernoulli_coefficients[d] + voltage_gradients[d]
+        )
+        partial_top = partial_top + bernoulli_coefficients[d] * start_beside[d]
 
     def sweep(beside):
         fraction_top_quantity = creation_amounts
@@ -81,7 +95,7 @@
             fraction_top_quantity = fraction_top_quantity + bernoulli_coefficient * leftover_portion
         return fraction_top_quantity / denominator_quantity
 
-    electron_concentration = sweep([b[1] for b in beside_both])
+    electron_concentration = partial_top / denominator_quantity
     electron_concentration = sweep(
         neighbours_of(electron_concentration, face_halos(electron_concentration, device_sides))
     )

time: 178 us -> 180 us (1.011)
  waiting for transfers between devices: 24.7 us -> 15.5 us
  other arithmetic: 50.8 us -> 57.4 us
  local copies, waits for them, and re-layouts: 13.6 us -> 16.5 us
    add x0 -> x2, other arithmetic: none -> 12.7 us  [the longest x1 8.85 us: per_device(): partial_top = partial_top + bernoulli_coefficients[d] * start_beside[d]]
    ppermute x5, waiting for transfers between devices: 9.4 us -> 0.01 us  [face_halos(): high = lax.ppermute(lax.slice_in_dim(block, 0, 1, axis=dim), axis, backward)]
    div x2 -> x1, other arithmetic: 18.4 us -> 10.9 us  [sweep(): return fraction_top_quantity / denominator_quantity]
    another operation x6 -> x5, other arithmetic: 14.6 us -> 10.2 us  [per_device(): both = jnp.stack([effective, initial_electrons])]
    div x0 -> x1, other arithmetic: none -> 4.29 us  [per_device(): electron_concentration = partial_top / denominator_quantity]
    concatenate x0 -> x1, other arithmetic: none -> 1.98 us  [neighbours_of(): jnp.concatenate([low, lax.slice_in_dim(block, 0, size - 1, axis=dim)], ax...]
    slice x3, local copies, waits for them, and re-layouts: 3.33 us -> 5.19 us  [neighbours_of(): lax.slice_in_dim(block, 0, size - 1, axis=dim)]
    unnamed x32 -> x40, local copies, waits for them, and re-layouts: 2.5 us -> 4.05 us
  transfers between devices with their start and end apart: 15 -> 15, of which waited for: 7 -> 6; matrix products, arithmetic and copies ran while one was open for 10% -> 15% of each run, Pallas kernels for 0% -> 0%
where the time goes in v6:
time: 180 us; the launch traced here: 178 us
  starting transfers between devices  59.4 us (33%)
  other arithmetic  57.4 us (32%)
  blocking collectives  17.6 us (10%)
  local copies, waits for them, and re-layouts  16.5 us (9%)
  waiting for transfers between devices  15.5 us (9%)
  matrix products  10.5 us (6%)
    ppermute x5, starting transfers between devices, face_halos(): lax.ppermute(lax.slice_in_dim(block, size - 1, size, axis=dim), axis, for...  23.5 us
    all_to_all x1, blocking collectives, per_device(): got_warm = lax.all_to_all(windows, 'slab', 0, 0, tiled=False)  17.6 us
    all_to_all x1, starting transfers between devices, per_device(): got = lax.all_to_all(piece, 'slab', 0, 0, tiled=False)  13.5 us
    div x1, other arithmetic, sweep(): return fraction_top_quantity / denominator_quantity  10.9 us
    another operation x5, other arithmetic, per_device(): both = jnp.stack([effective, initial_electrons])  10.2 us
    all_to_all x1, waiting for transfers between devices, per_device(): got = lax.all_to_all(piece, 'slab', 0, 0, tiled=False)  9.8 us
    ppermute x2, starting transfers between devices, per_device(): lax.ppermute(lax.slice_in_dim(stacked, size - depth, size, axis=dim), axi...  9.55 us
    add x1, other arithmetic, per_device(): partial_top = partial_top + bernoulli_coefficients[d] * start_beside[d]  8.85 us
  transfers between devices with their start and end apart: 15, of which 6 were waited for; matrix products, arithmetic and copies ran while one was open for 15% of the time, Pallas kernels for 0%

profile of v6, /device:TPU:1, one launch (start us, length us, event | category | flops | bytes accessed | tf_op | source)
XLA Modules:
  0.0 178.2 jit_solution(6786785246839992139)
XLA Ops:
  2.1 5.7 %select_add_fusion = f32[8,64,1024]{2,1,0:T(8,128)S(1)} fusion(f32[8,64,1024]{2,1,0:T(8,128)} %param.15, s32[8,64,1024]{2,1,0:T(8,128)} %param.19, f32[]{:T(128)} %bitcast.3, f32[]{:T(128)} %bitcast.2, f32[]{:T(128)} %bitcast.1, f32[]{:T(128)} %bitcast), kind=kLoop, calls=%fused_computation.115 | loop fusion | flops 6291456 | bytes 6291472 | tf_op jit(solution)/shard_map/add | solution.py:64
  8.0 6.3 %collective-permute-start.3 = (f32[2,1,64,1024]{3,2,1,0:T(8,128)S(1)}, f32[2,1,64,1024]{3,2,1,0:T(8,128)}, u32[]{:S(2)}, u32[]{:S(2)}) collective-permute-start(f32[2,1,64,1024]{3,2,1,0:T(8,128)S(1)} %get-tuple-element.41), channel_id=1, source_target_pairs={{0,4},{4,8},{8,12},{12,16},{16,20},{20,24},{24,28},{28,32},{32,36}... | collective-permute-start | bytes 1572872 | tf_op jit(solution)/shard_map/ppermute | solution.py:18
  14.4 3.1 %collective-permute-start.2 = (f32[2,8,1,1024]{3,2,1,0:T(1,128)S(1)}, f32[2,8,1,1024]{3,2,1,0:T(1,128)S(1)}, u32[]{:S(2)}, u32[]{:S(2)}) collective-permute-start(f32[2,8,1,1024]{3,2,1,0:T(1,128)S(1)} %get-tuple-element.45), channel_id=1, source_target_pairs={{0,1},{1,2},{2,3},{4,5},{5,6},{6,7},{8,9},{9,10},{10,11},{12,13},{... | collective-permute-start | bytes 196616 | tf_op jit(solution)/shard_map/ppermute | solution.py:18
  20.7 4.2 %fusion.2 = (f32[2,8,64,1023]{3,2,1,0:T(8,128)}, f32[2,8,64,1023]{3,2,1,0:T(8,128)}) fusion(f32[1,8,64,1024]{3,2,1,0:T(8,128)S(1)} %bitcast.197, f32[1,8,64,1024]{3,2,1,0:T(8,128)S(1)} %bitcast.203), kind=kLoop, calls=%fused_computation.20 | loop fusion | flops 2095104 | bytes 12574720 | tf_op jit(solution)/shard_map/stack | solution.py:68
  24.8 3.8 %fusion = (f32[2,8,63,1024]{3,2,1,0:T(8,128)}, f32[2,8,63,1024]{3,2,1,0:T(8,128)}) fusion(f32[1,8,64,1024]{3,2,1,0:T(8,128)S(1)} %bitcast.198, f32[1,8,64,1024]{3,2,1,0:T(8,128)S(1)} %bitcast.204), kind=kLoop, calls=%fused_computation.18 | loop fusion | flops 2064384 | bytes 12451840 | tf_op jit(solution)/shard_map/stack | solution.py:68
  28.6 2.1 %fusion.5 = f32[2,7,64,1024]{3,2,1,0:T(8,128)} fusion(f32[1,8,64,1024]{3,2,1,0:T(8,128)S(1)} %bitcast.199, f32[1,8,64,1024]{3,2,1,0:T(8,128)S(1)} %bitcast.205), kind=kLoop, calls=%fused_computation.34 | loop fusion | flops 917504 | bytes 7864320 | tf_op jit(solution)/shard_map/stack | solution.py:68
  30.8 8.8 %fusion.17 = (f32[8,64,1024]{2,1,0:T(8,128)S(1)}, f32[8,64,1024]{2,1,0:T(8,128)S(1)}, f32[8,64,1024]{2,1,0:T(8,128)S(1)}) fusion(f32[2,8,64,1023]{3,2,1,0:T(8,128)} %get-tuple-element.46, f32[2,8,64,1023]{3,2,1,0:T(8,128)} %get-tuple-element.47, f32[2,8,63,1024]{3,2,1,0:T(8,128)} %get-tuple-element.43, f32[2,8,1,1024]{3,2,1,0:T(1,128)S(1)} %collective-permute-done.2, ...), kind=kLoop, calls=%fused_computation.46 | loop fusion | flops 25165824 | bytes 27254784 | tf_op jit(solution)/shard_map/add | solution.py:81
  40.3 3.8 %add_add_fusion.1 = f32[8,64,1024]{2,1,0:T(8,128)S(1)} fusion(f32[8,64,1024]{2,1,0:T(8,128)S(1)} %copy-done.10, f32[8,64,1024]{2,1,0:T(8,128)S(1)} %select_add_fusion, f32[2,8,64,1023]{3,2,1,0:T(8,128)S(1)} %copy-done.3, f32[2,8,64,1023]{3,2,1,0:T(8,128)S(1)} %copy-done.2, f32[8,64,1024]{2,1,0:T(8,128)S(1)} %get-tuple-element.39, ...), kind=kLoop, calls=%fused_computation.106 | loop fusion | flops 22020096 | bytes 18866176 | tf_op jit(solution)/shard_map/add | solution.py:78
  47.1 4.3 %fusion.33 = (f32[8,64,1024]{2,1,0:T(8,128)S(1)}, f32[8,64,1024]{2,1,0:T(8,128)S(1)}, f32[8,64,1024]{2,1,0:T(8,128)}) fusion(f32[2,8,64,1024]{3,2,1,0:T(8,128)S(1)} %fusion.4, f32[8,64,1024]{2,1,0:T(8,128)S(1)} %get-tuple-element.29, f32[2,1,64,1024]{3,2,1,0:T(8,128)} %collective-permute-done, f32[2,7,64,1024]{3,2,1,0:T(8,128)S(1)} %copy-done.8, ...), kind=kLoop, calls=%fused_computation.63 | loop fusion | flops 15204352 | bytes 20971520 | tf_op jit(solution)/shard_map/div | solution.py:98
  51.5 2.4 %fusion.133 = (f32[8,63,1024]{2,1,0:T(8,128)}, f32[8,63,1024]{2,1,0:T(8,128)}) fusion(f32[8,64,1024]{2,1,0:T(8,128)S(1)} %get-tuple-element.34), kind=kLoop, calls=%fused_computation.233 | loop fusion | bytes 8257536 | tf_op jit(solution)/shard_map/slice | solution.py:30
  53.9 2.8 %fusion.131 = (f32[8,64,1023]{2,1,0:T(8,128)}, f32[8,64,1023]{2,1,0:T(8,128)}) fusion(f32[8,64,1024]{2,1,0:T(8,128)S(1)} %get-tuple-element.34), kind=kLoop, calls=%fused_computation.231 | loop fusion | bytes 8380416 | tf_op jit(solution)/shard_map/slice | solution.py:34
  58.0 6.1 %collective-permute-start.5 = (f32[1,64,1024]{2,1,0:T(8,128)S(1)}, f32[1,64,1024]{2,1,0:T(8,128)S(1)}, u32[]{:S(2)}, u32[]{:S(2)}) collective-permute-start(f32[1,64,1024]{2,1,0:T(8,128)S(1)} %get-tuple-element.64), channel_id=1, source_target_pairs={{0,4},{4,8},{8,12},{12,16},{16,20},{20,24},{24,28},{28,32},{32,36}... | collective-permute-start | bytes 786440 | tf_op jit(solution)/shard_map/ppermute | solution.py:18
  66.1 4.4 %collective-permute-start.7 = (f32[8,1,1024]{2,1,0:T(1,128)S(1)}, f32[8,1,1024]{2,1,0:T(1,128)S(1)}, u32[]{:S(2)}, u32[]{:S(2)}) collective-permute-start(f32[8,1,1024]{2,1,0:T(1,128)S(1)} %get-tuple-element.60), channel_id=1, source_target_pairs={{0,1},{1,2},{2,3},{4,5},{5,6},{6,7},{8,9},{9,10},{10,11},{12,13},{... | collective-permute-start | bytes 98312 | tf_op jit(solution)/shard_map/ppermute | solution.py:18
  70.5 2.3 %fusion.135 = (f32[7,64,1024]{2,1,0:T(8,128)}, f32[7,64,1024]{2,1,0:T(8,128)}) fusion(f32[8,64,1024]{2,1,0:T(8,128)S(1)} %get-tuple-element.34), kind=kLoop, calls=%fused_computation.235 | loop fusion | bytes 7340032 | tf_op jit(solution)/shard_map/slice | solution.py:30
  72.8 10.9 %fusion.50 = f32[8,64,1024]{2,1,0:T(8,128)S(1)} fusion(f32[8,64,1024]{2,1,0:T(8,128)} %param.17, f32[1,64,1024]{2,1,0:T(8,128)S(1)} %collective-permute-done.4, f32[7,64,1024]{2,1,0:T(8,128)} %get-tuple-element.67, f32[7,64,1024]{2,1,0:T(8,128)} %get-tuple-element.66, f32[1,64,1024]{2,1,0:T(8,128)S(1)} %collective-permute-done.5, ...), kind=kLoop, calls=%fused_computation.85 | loop fusion | flops 37224448 | bytes 37736448 | tf_op jit(solution)/shard_map/div | solution.py:96
  87.5 3.6 %collective-permute-start.9 = (f32[8,1,1024]{2,1,0:T(1,128)S(1)}, f32[8,1,1024]{2,1,0:T(1,128)S(1)}, u32[]{:S(2)}, u32[]{:S(2)}) collective-permute-start(f32[8,1,1024]{2,1,0:T(1,128)S(1)} %get-tuple-element.54), channel_id=1, source_target_pairs={{0,1},{1,2},{2,3},{4,5},{5,6},{6,7},{8,9},{9,10},{10,11},{12,13},{... | collective-permute-start | bytes 98312 | tf_op jit(solution)/shard_map/ppermute | solution.py:18
  92.1 7.9 %fusion.57 = f32[8,64,1024]{2,1,0:T(8,128)S(1)} fusion(f32[8,64,1024]{2,1,0:T(8,128)S(1)} %get-tuple-element.39, f32[8,1,1024]{2,1,0:T(1,128)S(1)} %collective-permute-done.8, f32[8,63,1024]{2,1,0:T(8,128)S(1)} %get-tuple-element.57, f32[8,64,1024]{2,1,0:T(8,128)S(1)} %get-tuple-element.38, f32[8,63,1024]{2,1,0:T(8,128)S(1)} %get-tuple-element.56, ...), kind=kLoop, calls=%fused_computation.96 | loop fusion | flops 46137344 | bytes 35115008 | tf_op jit(solution)/shard_map/mul | solution.py:114
  104.9 13.5 %all-to-all-start = ((f32[32,1,1536]{2,1,0:T(1,128)}), f32[32,1,1536]{2,1,0:T(1,128)S(1)}, u32[]{:S(2)}, u32[]{:S(2)}) async-start(f32[32,1,1536]{2,1,0:T(1,128)} %reshape.97), calls=%async_computation | async-start | bytes 393216 | tf_op jit(solution)/shard_map/all_to_all | solution.py:134
  118.4 9.8 %all-to-all-done = f32[32,1,1536]{2,1,0:T(1,128)S(1)} async-done(((f32[32,1,1536]{2,1,0:T(1,128)}), f32[32,1,1536]{2,1,0:T(1,128)S(1)}, u32[]{:S(2)}, u32[]{:S(2)}) %all-to-all-start) | async-done | bytes 196640 | tf_op jit(solution)/shard_map/all_to_all | solution.py:134
  132.4 5.7 %collective-permute-start.10 = (f32[3,3,32,128]{3,2,1,0:T(8,128)S(1)}, f32[3,3,32,128]{3,2,1,0:T(8,128)S(1)}, u32[]{:S(2)}, u32[]{:S(2)}) collective-permute-start(f32[3,3,32,128]{3,2,1,0:T(8,128)S(1)} %get-tuple-element.74), channel_id=1, source_target_pairs={{0,4},{4,8},{8,12},{12,16},{16,20},{20,24},{24,28},{28,32},{32,36}... | collective-permute-start | bytes 442376 | tf_op jit(solution)/shard_map/ppermute | solution.py:150
  141.0 3.1 %collective-permute-start.13 = (f32[3,14,8,128]{3,2,1,0:T(8,128)S(1)}, f32[3,14,8,128]{3,2,1,0:T(8,128)S(1)}, u32[]{:S(2)}, u32[]{:S(2)}) collective-permute-start(f32[3,14,8,128]{3,2,1,0:T(8,128)S(1)} %get-tuple-element.73), channel_id=1, source_target_pairs={{1,0},{2,1},{3,2},{5,4},{6,5},{7,6},{9,8},{10,9},{11,10},{13,12},{... | collective-permute-start | bytes 516104 | tf_op jit(solution)/shard_map/ppermute | solution.py:151
  144.1 3.8 %collective-permute-start.12 = (f32[3,14,8,128]{3,2,1,0:T(8,128)S(1)}, f32[3,14,8,128]{3,2,1,0:T(8,128)S(1)}, u32[]{:S(2)}, u32[]{:S(2)}) collective-permute-start(f32[3,14,8,128]{3,2,1,0:T(8,128)S(1)} %get-tuple-element.72), channel_id=1, source_target_pairs={{0,1},{1,2},{2,3},{4,5},{5,6},{6,7},{8,9},{9,10},{10,11},{12,13},{... | collective-permute-start | bytes 516104 | tf_op jit(solution)/shard_map/ppermute | solution.py:150
  152.7 17.6 %all_to_all.10 = f32[32,1,1536]{2,1,0:T(1,128)S(1)} all-to-all(f32[32,1,1536]{2,1,0:T(1,128)S(1)} %reshape.99), channel_id=1, replica_groups=mesh['slab'=32,'gy'=4] {'slab'}, dimensions={0} | all-to-all | bytes 393216 | tf_op jit(solution)/shard_map/all_to_all | solution.py:189
  174.4 3.8 %bitcast_multiply_fusion = f32[8,64,1024]{2,1,0:T(8,128)} fusion(f32[32,8,8,64]{3,0,1,2:T(8,128)S(1)} %fusion.66, f32[32,8,1024]{2,1,0:T(8,128)S(1)} %bitcast.207), kind=kOutput, calls=%fused_computation.100 | convolution fusion | flops 1611137024 | bytes 3670016 | tf_op jit(solution)/shard_map/scxy,scz->xyz/dot_general | solution.py:193
  (102 shorter events, 37.1 us)
Async XLA Ops:
  0.6 99.4 %copy-start = (f32[32,64]{1,0:T(8,128)S(1)}, f32[32,64]{1,0:T(8,128)}, u32[]{:S(2)}) copy-start(f32[32,64]{1,0:T(8,128)} %param.22) | copy-start | bytes 24580
  8.0 36.2 %collective-permute-start.3 = (f32[2,1,64,1024]{3,2,1,0:T(8,128)S(1)}, f32[2,1,64,1024]{3,2,1,0:T(8,128)}, u32[]{:S(2)}, u32[]{:S(2)}) collective-permute-start(f32[2,1,64,1024]{3,2,1,0:T(8,128)S(1)} %get-tuple-element.41), channel_id=1, source_target_pairs={{0,4},{4,8},{8,12},{12,16},{16,20},{20,24},{24,28},{28,32},{32,36}... | collective-permute-start | bytes 1572872 | tf_op jit(solution)/shard_map/ppermute | solution.py:18
  14.4 16.4 %collective-permute-start.2 = (f32[2,8,1,1024]{3,2,1,0:T(1,128)S(1)}, f32[2,8,1,1024]{3,2,1,0:T(1,128)S(1)}, u32[]{:S(2)}, u32[]{:S(2)}) collective-permute-start(f32[2,8,1,1024]{3,2,1,0:T(1,128)S(1)} %get-tuple-element.45), channel_id=1, source_target_pairs={{0,1},{1,2},{2,3},{4,5},{5,6},{6,7},{8,9},{9,10},{10,11},{12,13},{... | collective-permute-start | bytes 196616 | tf_op jit(solution)/shard_map/ppermute | solution.py:18
  17.4 13.3 %collective-permute-start.1 = (f32[2,8,1,1024]{3,2,1,0:T(1,128)S(1)}, f32[2,8,1,1024]{3,2,1,0:T(1,128)S(1)}, u32[]{:S(2)}, u32[]{:S(2)}) collective-permute-start(f32[2,8,1,1024]{3,2,1,0:T(1,128)S(1)} %get-tuple-element.44), channel_id=1, source_target_pairs={{1,0},{2,1},{3,2},{5,4},{6,5},{7,6},{9,8},{10,9},{11,10},{13,12},{... | collective-permute-start | bytes 196616 | tf_op jit(solution)/shard_map/ppermute | solution.py:19
  19.4 26.8 %collective-permute-start = (f32[2,1,64,1024]{3,2,1,0:T(8,128)S(1)}, f32[2,1,64,1024]{3,2,1,0:T(8,128)}, u32[]{:S(2)}, u32[]{:S(2)}) collective-permute-start(f32[2,1,64,1024]{3,2,1,0:T(8,128)S(1)} %get-tuple-element.40), channel_id=1, source_target_pairs={{4,0},{8,4},{12,8},{16,12},{20,16},{24,20},{28,24},{32,28},{36,32}... | collective-permute-start | bytes 1572872 | tf_op jit(solution)/shard_map/ppermute | solution.py:19
  30.8 72.1 %copy-start.15 = (f32[6,10]{1,0:T(8,128)}, f32[6,10]{1,0:T(8,128)S(1)}, u32[]{:S(2)}) copy-start(f32[6,10]{1,0:T(8,128)S(1)} %pad_dynamic-slice_fusion) | copy-start | bytes 724
  30.8 8.9 %copy-start.2 = (f32[2,8,64,1023]{3,2,1,0:T(8,128)S(1)}, f32[2,8,64,1023]{3,2,1,0:T(8,128)}, u32[]{:S(2)}) copy-start(f32[2,8,64,1023]{3,2,1,0:T(8,128)} %get-tuple-element.46) | copy-start | bytes 12570628
  30.8 8.9 %copy-start.3 = (f32[2,8,64,1023]{3,2,1,0:T(8,128)S(1)}, f32[2,8,64,1023]{3,2,1,0:T(8,128)}, u32[]{:S(2)}) copy-start(f32[2,8,64,1023]{3,2,1,0:T(8,128)} %get-tuple-element.47) | copy-start | bytes 12570628
  30.8 9.5 %copy-start.10 = (f32[8,64,1024]{2,1,0:T(8,128)S(1)}, f32[8,64,1024]{2,1,0:T(8,128)}, u32[]{:S(2)}) copy-start(f32[8,64,1024]{2,1,0:T(8,128)} %param.18) | copy-start | bytes 6291460
  56.7 16.0 %collective-permute-start.4 = (f32[1,64,1024]{2,1,0:T(8,128)S(1)}, f32[1,64,1024]{2,1,0:T(8,128)S(1)}, u32[]{:S(2)}, u32[]{:S(2)}) collective-permute-start(f32[1,64,1024]{2,1,0:T(8,128)S(1)} %get-tuple-element.65), channel_id=1, source_target_pairs={{4,0},{8,4},{12,8},{16,12},{20,16},{24,20},{28,24},{32,28},{36,32}... | collective-permute-start | bytes 786440 | tf_op jit(solution)/shard_map/ppermute | solution.py:19
  58.0 14.7 %collective-permute-start.5 = (f32[1,64,1024]{2,1,0:T(8,128)S(1)}, f32[1,64,1024]{2,1,0:T(8,128)S(1)}, u32[]{:S(2)}, u32[]{:S(2)}) collective-permute-start(f32[1,64,1024]{2,1,0:T(8,128)S(1)} %get-tuple-element.64), channel_id=1, source_target_pairs={{0,4},{4,8},{8,12},{12,16},{16,20},{20,24},{24,28},{28,32},{32,36}... | collective-permute-start | bytes 786440 | tf_op jit(solution)/shard_map/ppermute | solution.py:18
  64.1 8.6 %collective-permute-start.6 = (f32[8,1,1024]{2,1,0:T(1,128)S(1)}, f32[8,1,1024]{2,1,0:T(1,128)S(1)}, u32[]{:S(2)}, u32[]{:S(2)}) collective-permute-start(f32[8,1,1024]{2,1,0:T(1,128)S(1)} %get-tuple-element.61), channel_id=1, source_target_pairs={{1,0},{2,1},{3,2},{5,4},{6,5},{7,6},{9,8},{10,9},{11,10},{13,12},{... | collective-permute-start | bytes 98312 | tf_op jit(solution)/shard_map/ppermute | solution.py:19
  66.1 6.7 %collective-permute-start.7 = (f32[8,1,1024]{2,1,0:T(1,128)S(1)}, f32[8,1,1024]{2,1,0:T(1,128)S(1)}, u32[]{:S(2)}, u32[]{:S(2)}) collective-permute-start(f32[8,1,1024]{2,1,0:T(1,128)S(1)} %get-tuple-element.60), channel_id=1, source_target_pairs={{0,1},{1,2},{2,3},{4,5},{5,6},{6,7},{8,9},{9,10},{10,11},{12,13},{... | collective-permute-start | bytes 98312 | tf_op jit(solution)/shard_map/ppermute | solution.py:18
  83.6 8.5 %copy-start.1 = (f32[8,64,1024]{2,1,0:T(8,128)}, f32[8,64,1024]{2,1,0:T(8,128)S(1)}, u32[]{:S(2)}) copy-start(f32[8,64,1024]{2,1,0:T(8,128)S(1)} %fusion.50) | copy-start | bytes 6291460
  85.4 6.0 %collective-permute-start.8 = (f32[8,1,1024]{2,1,0:T(1,128)S(1)}, f32[8,1,1024]{2,1,0:T(1,128)S(1)}, u32[]{:S(2)}, u32[]{:S(2)}) collective-permute-start(f32[8,1,1024]{2,1,0:T(1,128)S(1)} %get-tuple-element.55), channel_id=1, source_target_pairs={{1,0},{2,1},{3,2},{5,4},{6,5},{7,6},{9,8},{10,9},{11,10},{13,12},{... | collective-permute-start | bytes 98312 | tf_op jit(solution)/shard_map/ppermute | solution.py:19
  87.5 4.7 %collective-permute-start.9 = (f32[8,1,1024]{2,1,0:T(1,128)S(1)}, f32[8,1,1024]{2,1,0:T(1,128)S(1)}, u32[]{:S(2)}, u32[]{:S(2)}) collective-permute-start(f32[8,1,1024]{2,1,0:T(1,128)S(1)} %get-tuple-element.54), channel_id=1, source_target_pairs={{0,1},{1,2},{2,3},{4,5},{5,6},{6,7},{8,9},{9,10},{10,11},{12,13},{... | collective-permute-start | bytes 98312 | tf_op jit(solution)/shard_map/ppermute | solution.py:18
  103.5 14.9 %copy-start.14 = (f32[8,32,128]{2,1,0:T(8,128)S(1)}, f32[8,32,128]{2,1,0:T(8,128)}, u32[]{:S(2)}) copy-start(f32[8,32,128]{2,1,0:T(8,128)} %param.24) | copy-start | bytes 393220
  104.9 23.3 %all-to-all-start = ((f32[32,1,1536]{2,1,0:T(1,128)}), f32[32,1,1536]{2,1,0:T(1,128)S(1)}, u32[]{:S(2)}, u32[]{:S(2)}) async-start(f32[32,1,1536]{2,1,0:T(1,128)} %reshape.97), calls=%async_computation | async-start | bytes 393216 | tf_op jit(solution)/shard_map/all_to_all | solution.py:134
  131.1 8.8 %collective-permute-start.11 = (f32[3,3,32,128]{3,2,1,0:T(8,128)S(1)}, f32[3,3,32,128]{3,2,1,0:T(8,128)S(1)}, u32[]{:S(2)}, u32[]{:S(2)}) collective-permute-start(f32[3,3,32,128]{3,2,1,0:T(8,128)S(1)} %get-tuple-element.75), channel_id=1, source_target_pairs={{4,0},{8,4},{12,8},{16,12},{20,16},{24,20},{28,24},{32,28},{36,32}... | collective-permute-start | bytes 442376 | tf_op jit(solution)/shard_map/ppermute | solution.py:151
  132.4 8.6 %collective-permute-start.10 = (f32[3,3,32,128]{3,2,1,0:T(8,128)S(1)}, f32[3,3,32,128]{3,2,1,0:T(8,128)S(1)}, u32[]{:S(2)}, u32[]{:S(2)}) collective-permute-start(f32[3,3,32,128]{3,2,1,0:T(8,128)S(1)} %get-tuple-element.74), channel_id=1, source_target_pairs={{0,4},{4,8},{8,12},{12,16},{16,20},{20,24},{24,28},{28,32},{32,36}... | collective-permute-start | bytes 442376 | tf_op jit(solution)/shard_map/ppermute | solution.py:150
  141.0 8.1 %collective-permute-start.13 = (f32[3,14,8,128]{3,2,1,0:T(8,128)S(1)}, f32[3,14,8,128]{3,2,1,0:T(8,128)S(1)}, u32[]{:S(2)}, u32[]{:S(2)}) collective-permute-start(f32[3,14,8,128]{3,2,1,0:T(8,128)S(1)} %get-tuple-element.73), channel_id=1, source_target_pairs={{1,0},{2,1},{3,2},{5,4},{6,5},{7,6},{9,8},{10,9},{11,10},{13,12},{... | collective-permute-start | bytes 516104 | tf_op jit(solution)/shard_map/ppermute | solution.py:151
  144.1 6.2 %collective-permute-start.12 = (f32[3,14,8,128]{3,2,1,0:T(8,128)S(1)}, f32[3,14,8,128]{3,2,1,0:T(8,128)S(1)}, u32[]{:S(2)}, u32[]{:S(2)}) collective-permute-start(f32[3,14,8,128]{3,2,1,0:T(8,128)S(1)} %get-tuple-element.72), channel_id=1, source_target_pairs={{0,1},{1,2},{2,3},{4,5},{5,6},{6,7},{8,9},{9,10},{10,11},{12,13},{... | collective-permute-start | bytes 516104 | tf_op jit(solution)/shard_map/ppermute | solution.py:150
  151.4 20.0 %copy-start.12 = (f32[8,32,128]{2,1,0:T(8,128)}, f32[8,32,128]{2,1,0:T(8,128)S(1)}, u32[]{:S(2)}) copy-start(f32[8,32,128]{2,1,0:T(8,128)S(1)} %fusion.96) | copy-start | bytes 393220
  151.9 19.8 %copy-start.16 = (f32[6,10]{1,0:T(8,128)S(1)}, f32[6,10]{1,0:T(8,128)}, u32[]{:S(2)}) copy-start(f32[6,10]{1,0:T(8,128)} %copy-done.15) | copy-start | bytes 724
  (8 other events, 25.3 us)

commit v7 on v5

--- a/solution.py
+++ b/solution.py
@@ -30,9 +30,10 @@
         out.append(jnp.concatenate([low, lax.slice_in_dim(block, 0, size - 1, axis=dim)], axis=dim))
     last = block.ndim - 1
     size = block.shape[last]
-    zero = jnp.zeros_like(lax.slice_in_dim(block, 0, 1, axis=last))
-    out.append(jnp.concatenate([lax.slice_in_dim(block, 1, size, axis=last), zero], axis=last))
-    out.append(jnp.concatenate([zero, lax.slice_in_dim(block, 0, size - 1, axis=last)], axis=last))
+    widths = [(0, 0)] * last + [(1, 1)]
+    padded = jnp.pad(block, widths)
+    out.append(lax.slice_in_dim(padded, 2, size + 2, axis=last))
+    out.append(lax.slice_in_dim(padded, 0, size, axis=last))
     return out
 
 

time: 178 us -> 182 us (1.022)
  starting transfers between devices: 57.7 us -> 64.9 us
  local copies, waits for them, and re-layouts: 13.6 us -> 7.79 us
  blocking collectives: 17.6 us -> 20.3 us
  waiting for transfers between devices: 24.7 us -> 26.8 us
    ppermute x2, waiting for transfers between devices: 2.94 us -> 11.6 us  [per_device(): lax.ppermute(lax.slice_in_dim(stacked, 0, depth, axis=dim), axis, backward)]
    ppermute x5, waiting for transfers between devices: 9.4 us -> 1.7 us  [face_halos(): high = lax.ppermute(lax.slice_in_dim(block, 0, 1, axis=dim), axis, backward)]
    ppermute x5, starting transfers between devices: 23.1 us -> 28.2 us  [face_halos(): lax.ppermute(lax.slice_in_dim(block, size - 1, size, axis=dim), axis, for...]
    another operation x6 -> x5, other arithmetic: 14.6 us -> 9.73 us  [per_device(): both = jnp.stack([effective, initial_electrons])]
    all_to_all x1, starting transfers between devices: 12.6 us -> 16.9 us  [per_device(): got = lax.all_to_all(piece, 'slab', 0, 0, tiled=False)]
    div x2, other arithmetic: 18.4 us -> 22.2 us  [sweep(): return fraction_top_quantity / denominator_quantity]
    ppermute x2, starting transfers between devices: 9.33 us -> 6.36 us  [per_device(): lax.ppermute(lax.slice_in_dim(stacked, size - depth, size, axis=dim), axi...]
    slice x2 -> x0, local copies, waits for them, and re-layouts: 2.93 us -> none  [neighbours_of(): lax.slice_in_dim(block, 1, size, axis=last)]
  transfers between devices with their start and end apart: 15 -> 15, of which waited for: 7 -> 9; matrix products, arithmetic and copies ran while one was open for 10% -> 6% of each run, Pallas kernels for 0% -> 0%
where the time goes in v7:
time: 182 us
  starting transfers between devices  64.9 us (36%)
  other arithmetic  50.2 us (28%)
  waiting for transfers between devices  26.8 us (15%)
  blocking collectives  20.3 us (11%)
  matrix products  10.5 us (6%)
  local copies, waits for them, and re-layouts  7.79 us (4%)
    ppermute x5, starting transfers between devices, face_halos(): lax.ppermute(lax.slice_in_dim(block, size - 1, size, axis=dim), axis, for...  28.2 us
    div x2, other arithmetic, sweep(): return fraction_top_quantity / denominator_quantity  22.2 us
    all_to_all x1, blocking collectives, per_device(): got_warm = lax.all_to_all(windows, 'slab', 0, 0, tiled=False)  20.3 us
    all_to_all x1, starting transfers between devices, per_device(): got = lax.all_to_all(piece, 'slab', 0, 0, tiled=False)  16.9 us
    ppermute x2, waiting for transfers between devices, per_device(): lax.ppermute(lax.slice_in_dim(stacked, 0, depth, axis=dim), axis, backward)  11.6 us
    ppermute x5, starting transfers between devices, face_halos(): high = lax.ppermute(lax.slice_in_dim(block, 0, 1, axis=dim), axis, backward)  10.2 us
    all_to_all x1, waiting for transfers between devices, per_device(): got = lax.all_to_all(piece, 'slab', 0, 0, tiled=False)  9.93 us
    another operation x5, other arithmetic, per_device(): both = jnp.stack([effective, initial_electrons])  9.73 us
  transfers between devices with their start and end apart: 15, of which 9 were waited for; matrix products, arithmetic and copies ran while one was open for 6% of the time, Pallas kernels for 0%

profile of v7, /device:TPU:1, one launch (start us, length us, event | category | flops | bytes accessed | tf_op | source)
XLA Modules:
  0.0 181.8 jit_solution(2589077769538711613)
XLA Ops:
  2.1 5.8 %select_add_fusion = f32[8,64,1024]{2,1,0:T(8,128)S(1)} fusion(f32[8,64,1024]{2,1,0:T(8,128)} %param.15, s32[8,64,1024]{2,1,0:T(8,128)} %param.19, f32[]{:T(128)} %bitcast.3, f32[]{:T(128)} %bitcast.2, f32[]{:T(128)} %bitcast.1, f32[]{:T(128)} %bitcast), kind=kLoop, calls=%fused_computation.128 | loop fusion | flops 6291456 | bytes 6291472 | tf_op jit(solution)/shard_map/add | solution.py:65
  8.0 3.3 %collective-permute-start.2 = (f32[2,8,1,1024]{3,2,1,0:T(1,128)S(1)}, f32[2,8,1,1024]{3,2,1,0:T(1,128)S(1)}, u32[]{:S(2)}, u32[]{:S(2)}) collective-permute-start(f32[2,8,1,1024]{3,2,1,0:T(1,128)S(1)} %get-tuple-element.39), channel_id=1, source_target_pairs={{1,0},{2,1},{3,2},{5,4},{6,5},{7,6},{9,8},{10,9},{11,10},{13,12},{... | collective-permute-start | bytes 196616 | tf_op jit(solution)/shard_map/ppermute | solution.py:19
  11.4 3.1 %collective-permute-start.3 = (f32[2,8,1,1024]{3,2,1,0:T(1,128)S(1)}, f32[2,8,1,1024]{3,2,1,0:T(1,128)S(1)}, u32[]{:S(2)}, u32[]{:S(2)}) collective-permute-start(f32[2,8,1,1024]{3,2,1,0:T(1,128)S(1)} %get-tuple-element.40), channel_id=1, source_target_pairs={{0,1},{1,2},{2,3},{4,5},{5,6},{6,7},{8,9},{9,10},{10,11},{12,13},{... | collective-permute-start | bytes 196616 | tf_op jit(solution)/shard_map/ppermute | solution.py:18
  16.8 5.5 %collective-permute-start.1 = (f32[2,1,64,1024]{3,2,1,0:T(8,128)}, f32[2,1,64,1024]{3,2,1,0:T(8,128)S(1)}, u32[]{:S(2)}, u32[]{:S(2)}) collective-permute-start(f32[2,1,64,1024]{3,2,1,0:T(8,128)} %get-tuple-element.36), channel_id=1, source_target_pairs={{0,4},{4,8},{8,12},{12,16},{16,20},{20,24},{24,28},{28,32},{32,36}... | collective-permute-start | bytes 1572872 | tf_op jit(solution)/shard_map/ppermute | solution.py:18
  22.3 2.3 %pad_maximum_fusion = f32[2,8,64,1024]{3,2,1,0:T(8,128)} fusion(f32[1,8,64,1024]{3,2,1,0:T(8,128)S(1)} %bitcast.215, f32[1,8,64,1024]{3,2,1,0:T(8,128)S(1)} %bitcast.209), kind=kLoop, calls=%fused_computation.8 | loop fusion | flops 1048576 | bytes 8388608 | tf_op jit(solution)/shard_map/stack | solution.py:69
  24.6 3.2 %fusion.2 = (f32[2,7,64,1024]{3,2,1,0:T(8,128)}, f32[2,7,64,1024]{3,2,1,0:T(8,128)}) fusion(f32[1,8,64,1024]{3,2,1,0:T(8,128)S(1)} %bitcast.210, f32[1,8,64,1024]{3,2,1,0:T(8,128)S(1)} %bitcast.216), kind=kLoop, calls=%fused_computation.31 | loop fusion | flops 1835008 | bytes 11534336 | tf_op jit(solution)/shard_map/stack | solution.py:69
  27.9 3.1 %fusion = (f32[2,8,63,1024]{3,2,1,0:T(8,128)S(1)}, f32[2,8,63,1024]{3,2,1,0:T(8,128)S(1)}) fusion(f32[1,8,64,1024]{3,2,1,0:T(8,128)S(1)} %bitcast.211, f32[1,8,64,1024]{3,2,1,0:T(8,128)} %bitcast.212), kind=kLoop, calls=%fused_computation.21 | loop fusion | flops 2064384 | bytes 12451840 | tf_op jit(solution)/shard_map/stack | solution.py:69
  34.3 11.9 %fusion.42 = (f32[8,64,1024]{2,1,0:T(8,128)S(1)}, f32[8,64,1024]{2,1,0:T(8,128)S(1)}, f32[8,64,1024]{2,1,0:T(8,128)S(1)}) fusion(f32[2,8,64,1024]{3,2,1,0:T(8,128)S(1)} %copy-done.2, f32[2,8,63,1024]{3,2,1,0:T(8,128)S(1)} %get-tuple-element.38, f32[2,8,1,1024]{3,2,1,0:T(1,128)S(1)} %collective-permute-done.3, ...), kind=kLoop, calls=%fused_computation.75 | loop fusion | flops 45613056 | bytes 33554432 | tf_op jit(solution)/shard_map/div | solution.py:83
  48.1 11.7 %collective-permute-start.5 = (f32[1,64,1024]{2,1,0:T(8,128)S(1)}, f32[1,64,1024]{2,1,0:T(8,128)S(1)}, u32[]{:S(2)}, u32[]{:S(2)}) collective-permute-start(f32[1,64,1024]{2,1,0:T(8,128)S(1)} %get-tuple-element.53), channel_id=1, source_target_pairs={{0,4},{4,8},{8,12},{12,16},{16,20},{20,24},{24,28},{28,32},{32,36}... | collective-permute-start | bytes 786440 | tf_op jit(solution)/shard_map/ppermute | solution.py:18
  59.9 2.4 %collective-permute-start.6 = (f32[8,1,1024]{2,1,0:T(1,128)S(1)}, f32[8,1,1024]{2,1,0:T(1,128)S(1)}, u32[]{:S(2)}, u32[]{:S(2)}) collective-permute-start(f32[8,1,1024]{2,1,0:T(1,128)S(1)} %get-tuple-element.50), channel_id=1, source_target_pairs={{1,0},{2,1},{3,2},{5,4},{6,5},{7,6},{9,8},{10,9},{11,10},{13,12},{... | collective-permute-start | bytes 98312 | tf_op jit(solution)/shard_map/ppermute | solution.py:19
  62.2 3.5 %collective-permute-start.7 = (f32[8,1,1024]{2,1,0:T(1,128)S(1)}, f32[8,1,1024]{2,1,0:T(1,128)S(1)}, u32[]{:S(2)}, u32[]{:S(2)}) collective-permute-start(f32[8,1,1024]{2,1,0:T(1,128)S(1)} %get-tuple-element.49), channel_id=1, source_target_pairs={{0,1},{1,2},{2,3},{4,5},{5,6},{6,7},{8,9},{9,10},{10,11},{12,13},{... | collective-permute-start | bytes 98312 | tf_op jit(solution)/shard_map/ppermute | solution.py:18
  66.7 10.4 %fusion.13 = f32[8,64,1024]{2,1,0:T(8,128)S(1)} fusion(f32[8,64,1024]{2,1,0:T(8,128)S(1)} %get-tuple-element.30, f32[8,64,1024]{2,1,0:T(8,128)S(1)} %copy-done.6, f32[1,64,1024]{2,1,0:T(8,128)S(1)} %collective-permute-done.4, f32[7,64,1024]{2,1,0:T(8,128)S(1)} %get-tuple-element.56, f32[7,64,1024]{2,1,0:T(8,128)S(1)} %get-tuple-element.55, ...), kind=kLoop, calls=%fused_computation.46 | loop fusion | flops 43515904 | bytes 35651584 | tf_op jit(solution)/shard_map/div | solution.py:83
  78.1 1.9 %collective-permute-start.8 = (f32[8,1,1024]{2,1,0:T(1,128)S(1)}, f32[8,1,1024]{2,1,0:T(1,128)S(1)}, u32[]{:S(2)}, u32[]{:S(2)}) collective-permute-start(f32[8,1,1024]{2,1,0:T(1,128)S(1)} %get-tuple-element.46), channel_id=1, source_target_pairs={{1,0},{2,1},{3,2},{5,4},{6,5},{7,6},{9,8},{10,9},{11,10},{13,12},{... | collective-permute-start | bytes 98312 | tf_op jit(solution)/shard_map/ppermute | solution.py:19
  80.0 4.4 %collective-permute-start.9 = (f32[8,1,1024]{2,1,0:T(1,128)S(1)}, f32[8,1,1024]{2,1,0:T(1,128)S(1)}, u32[]{:S(2)}, u32[]{:S(2)}) collective-permute-start(f32[8,1,1024]{2,1,0:T(1,128)S(1)} %get-tuple-element.45), channel_id=1, source_target_pairs={{0,1},{1,2},{2,3},{4,5},{5,6},{6,7},{8,9},{9,10},{10,11},{12,13},{... | collective-permute-start | bytes 98312 | tf_op jit(solution)/shard_map/ppermute | solution.py:18
  85.3 8.7 %fusion.20 = f32[8,64,1024]{2,1,0:T(8,128)S(1)} fusion(f32[8,64,1024]{2,1,0:T(8,128)S(1)} %fusion.13, f32[8,1,1024]{2,1,0:T(1,128)S(1)} %collective-permute-done.8, f32[8,63,1024]{2,1,0:T(8,128)S(1)} %get-tuple-element.48, f32[8,63,1024]{2,1,0:T(8,128)S(1)} %get-tuple-element.47, f32[8,1,1024]{2,1,0:T(1,128)S(1)} %collective-permute-done.9, ...), kind=kLoop, calls=%fused_computation.53 | loop fusion | flops 48234496 | bytes 30932992 | tf_op jit(solution)/shard_map/mul | solution.py:101
  98.9 16.9 %all-to-all-start = ((f32[32,1,1536]{2,1,0:T(1,128)}), f32[32,1,1536]{2,1,0:T(1,128)S(1)}, u32[]{:S(2)}, u32[]{:S(2)}) async-start(f32[32,1,1536]{2,1,0:T(1,128)} %reshape.97), calls=%async_computation | async-start | bytes 393216 | tf_op jit(solution)/shard_map/all_to_all | solution.py:121
  115.8 9.9 %all-to-all-done = f32[32,1,1536]{2,1,0:T(1,128)S(1)} async-done(((f32[32,1,1536]{2,1,0:T(1,128)}), f32[32,1,1536]{2,1,0:T(1,128)S(1)}, u32[]{:S(2)}, u32[]{:S(2)}) %all-to-all-start) | async-done | bytes 196640 | tf_op jit(solution)/shard_map/all_to_all | solution.py:121
  128.6 1.9 %collective-permute-start.10 = (f32[3,3,32,128]{3,2,1,0:T(8,128)S(1)}, f32[3,3,32,128]{3,2,1,0:T(8,128)S(1)}, u32[]{:S(2)}, u32[]{:S(2)}) collective-permute-start(f32[3,3,32,128]{3,2,1,0:T(8,128)S(1)} %get-tuple-element.63), channel_id=1, source_target_pairs={{0,4},{4,8},{8,12},{12,16},{16,20},{20,24},{24,28},{28,32},{32,36}... | collective-permute-start | bytes 442376 | tf_op jit(solution)/shard_map/ppermute | solution.py:137
  132.7 7.2 %collective-permute-done.11 = f32[3,3,32,128]{3,2,1,0:T(8,128)S(1)} collective-permute-done((f32[3,3,32,128]{3,2,1,0:T(8,128)S(1)}, f32[3,3,32,128]{3,2,1,0:T(8,128)S(1)}, u32[]{:S(2)}, u32[]{:S(2)}) %collective-permute-start.11) | collective-permute-done | bytes 147488 | tf_op jit(solution)/shard_map/ppermute | solution.py:138
  139.9 4.4 %collective-permute-start.12 = (f32[3,14,8,128]{3,2,1,0:T(8,128)S(1)}, f32[3,14,8,128]{3,2,1,0:T(8,128)S(1)}, u32[]{:S(2)}, u32[]{:S(2)}) collective-permute-start(f32[3,14,8,128]{3,2,1,0:T(8,128)S(1)} %get-tuple-element.61), channel_id=1, source_target_pairs={{0,1},{1,2},{2,3},{4,5},{5,6},{6,7},{8,9},{9,10},{10,11},{12,13},{... | collective-permute-start | bytes 516104 | tf_op jit(solution)/shard_map/ppermute | solution.py:137
  144.3 1.9 %collective-permute-start.13 = (f32[3,14,8,128]{3,2,1,0:T(8,128)S(1)}, f32[3,14,8,128]{3,2,1,0:T(8,128)S(1)}, u32[]{:S(2)}, u32[]{:S(2)}) collective-permute-start(f32[3,14,8,128]{3,2,1,0:T(8,128)S(1)} %get-tuple-element.62), channel_id=1, source_target_pairs={{1,0},{2,1},{3,2},{5,4},{6,5},{7,6},{9,8},{10,9},{11,10},{13,12},{... | collective-permute-start | bytes 516104 | tf_op jit(solution)/shard_map/ppermute | solution.py:138
  146.6 4.4 %collective-permute-done.13 = f32[3,14,8,128]{3,2,1,0:T(8,128)S(1)} collective-permute-done((f32[3,14,8,128]{3,2,1,0:T(8,128)S(1)}, f32[3,14,8,128]{3,2,1,0:T(8,128)S(1)}, u32[]{:S(2)}, u32[]{:S(2)}) %collective-permute-start.13) | collective-permute-done | bytes 172064 | tf_op jit(solution)/shard_map/ppermute | solution.py:138
  153.5 20.3 %all_to_all.10 = f32[32,1,1536]{2,1,0:T(1,128)S(1)} all-to-all(f32[32,1,1536]{2,1,0:T(1,128)S(1)} %reshape.99), channel_id=1, replica_groups=mesh['slab'=32,'gy'=4] {'slab'}, dimensions={0} | all-to-all | bytes 393216 | tf_op jit(solution)/shard_map/all_to_all | solution.py:176
  178.0 3.8 %bitcast_multiply_fusion = f32[8,64,1024]{2,1,0:T(8,128)} fusion(f32[32,8,8,64]{3,0,1,2:T(8,128)S(1)} %fusion.75, f32[32,8,1024]{2,1,0:T(8,128)S(1)} %bitcast.217), kind=kOutput, calls=%fused_computation.112 | convolution fusion | flops 1611137024 | bytes 3670016 | tf_op jit(solution)/shard_map/scxy,scz->xyz/dot_general | solution.py:180
  (93 shorter events, 28.5 us)
Async XLA Ops:
  0.6 93.4 %copy-start = (f32[32,64]{1,0:T(8,128)S(1)}, f32[32,64]{1,0:T(8,128)}, u32[]{:S(2)}) copy-start(f32[32,64]{1,0:T(8,128)} %param.22) | copy-start | bytes 24580
  8.0 23.0 %collective-permute-start.2 = (f32[2,8,1,1024]{3,2,1,0:T(1,128)S(1)}, f32[2,8,1,1024]{3,2,1,0:T(1,128)S(1)}, u32[]{:S(2)}, u32[]{:S(2)}) collective-permute-start(f32[2,8,1,1024]{3,2,1,0:T(1,128)S(1)} %get-tuple-element.39), channel_id=1, source_target_pairs={{1,0},{2,1},{3,2},{5,4},{6,5},{7,6},{9,8},{10,9},{11,10},{13,12},{... | collective-permute-start | bytes 196616 | tf_op jit(solution)/shard_map/ppermute | solution.py:19
  11.4 19.7 %collective-permute-start.3 = (f32[2,8,1,1024]{3,2,1,0:T(1,128)S(1)}, f32[2,8,1,1024]{3,2,1,0:T(1,128)S(1)}, u32[]{:S(2)}, u32[]{:S(2)}) collective-permute-start(f32[2,8,1,1024]{3,2,1,0:T(1,128)S(1)} %get-tuple-element.40), channel_id=1, source_target_pairs={{0,1},{1,2},{2,3},{4,5},{5,6},{6,7},{8,9},{9,10},{10,11},{12,13},{... | collective-permute-start | bytes 196616 | tf_op jit(solution)/shard_map/ppermute | solution.py:18
  15.5 17.2 %collective-permute-start = (f32[2,1,64,1024]{3,2,1,0:T(8,128)}, f32[2,1,64,1024]{3,2,1,0:T(8,128)S(1)}, u32[]{:S(2)}, u32[]{:S(2)}) collective-permute-start(f32[2,1,64,1024]{3,2,1,0:T(8,128)} %get-tuple-element.35), channel_id=1, source_target_pairs={{4,0},{8,4},{12,8},{16,12},{20,16},{24,20},{28,24},{32,28},{36,32}... | collective-permute-start | bytes 1572872 | tf_op jit(solution)/shard_map/ppermute | solution.py:19
  16.8 17.5 %collective-permute-start.1 = (f32[2,1,64,1024]{3,2,1,0:T(8,128)}, f32[2,1,64,1024]{3,2,1,0:T(8,128)S(1)}, u32[]{:S(2)}, u32[]{:S(2)}) collective-permute-start(f32[2,1,64,1024]{3,2,1,0:T(8,128)} %get-tuple-element.36), channel_id=1, source_target_pairs={{0,4},{4,8},{8,12},{12,16},{16,20},{20,24},{24,28},{28,32},{32,36}... | collective-permute-start | bytes 1572872 | tf_op jit(solution)/shard_map/ppermute | solution.py:18
  27.9 68.9 %copy-start.13 = (f32[6,10]{1,0:T(8,128)}, f32[6,10]{1,0:T(8,128)S(1)}, u32[]{:S(2)}) copy-start(f32[6,10]{1,0:T(8,128)S(1)} %pad_dynamic-slice_fusion) | copy-start | bytes 724
  27.9 6.4 %copy-start.2 = (f32[2,8,64,1024]{3,2,1,0:T(8,128)S(1)}, f32[2,8,64,1024]{3,2,1,0:T(8,128)}, u32[]{:S(2)}) copy-start(f32[2,8,64,1024]{3,2,1,0:T(8,128)} %pad_maximum_fusion) | copy-start | bytes 12582916
  27.9 6.4 %copy-start.4 = (f32[2,7,64,1024]{3,2,1,0:T(8,128)S(1)}, f32[2,7,64,1024]{3,2,1,0:T(8,128)}, u32[]{:S(2)}) copy-start(f32[2,7,64,1024]{3,2,1,0:T(8,128)} %get-tuple-element.33) | copy-start | bytes 11010052
  27.9 6.4 %copy-start.5 = (f32[2,7,64,1024]{3,2,1,0:T(8,128)S(1)}, f32[2,7,64,1024]{3,2,1,0:T(8,128)}, u32[]{:S(2)}) copy-start(f32[2,7,64,1024]{3,2,1,0:T(8,128)} %get-tuple-element.34) | copy-start | bytes 11010052
  46.8 19.9 %collective-permute-start.4 = (f32[1,64,1024]{2,1,0:T(8,128)S(1)}, f32[1,64,1024]{2,1,0:T(8,128)S(1)}, u32[]{:S(2)}, u32[]{:S(2)}) collective-permute-start(f32[1,64,1024]{2,1,0:T(8,128)S(1)} %get-tuple-element.54), channel_id=1, source_target_pairs={{4,0},{8,4},{12,8},{16,12},{20,16},{24,20},{28,24},{32,28},{36,32}... | collective-permute-start | bytes 786440 | tf_op jit(solution)/shard_map/ppermute | solution.py:19
  48.1 18.6 %collective-permute-start.5 = (f32[1,64,1024]{2,1,0:T(8,128)S(1)}, f32[1,64,1024]{2,1,0:T(8,128)S(1)}, u32[]{:S(2)}, u32[]{:S(2)}) collective-permute-start(f32[1,64,1024]{2,1,0:T(8,128)S(1)} %get-tuple-element.53), channel_id=1, source_target_pairs={{0,4},{4,8},{8,12},{12,16},{16,20},{20,24},{24,28},{28,32},{32,36}... | collective-permute-start | bytes 786440 | tf_op jit(solution)/shard_map/ppermute | solution.py:18
  59.9 6.4 %collective-permute-start.6 = (f32[8,1,1024]{2,1,0:T(1,128)S(1)}, f32[8,1,1024]{2,1,0:T(1,128)S(1)}, u32[]{:S(2)}, u32[]{:S(2)}) collective-permute-start(f32[8,1,1024]{2,1,0:T(1,128)S(1)} %get-tuple-element.50), channel_id=1, source_target_pairs={{1,0},{2,1},{3,2},{5,4},{6,5},{7,6},{9,8},{10,9},{11,10},{13,12},{... | collective-permute-start | bytes 98312 | tf_op jit(solution)/shard_map/ppermute | solution.py:19
  62.2 4.5 %collective-permute-start.7 = (f32[8,1,1024]{2,1,0:T(1,128)S(1)}, f32[8,1,1024]{2,1,0:T(1,128)S(1)}, u32[]{:S(2)}, u32[]{:S(2)}) collective-permute-start(f32[8,1,1024]{2,1,0:T(1,128)S(1)} %get-tuple-element.49), channel_id=1, source_target_pairs={{0,1},{1,2},{2,3},{4,5},{5,6},{6,7},{8,9},{9,10},{10,11},{12,13},{... | collective-permute-start | bytes 98312 | tf_op jit(solution)/shard_map/ppermute | solution.py:18
  77.1 8.2 %copy-start.1 = (f32[8,64,1024]{2,1,0:T(8,128)}, f32[8,64,1024]{2,1,0:T(8,128)S(1)}, u32[]{:S(2)}) copy-start(f32[8,64,1024]{2,1,0:T(8,128)S(1)} %fusion.13) | copy-start | bytes 6291460
  78.1 6.6 %collective-permute-start.8 = (f32[8,1,1024]{2,1,0:T(1,128)S(1)}, f32[8,1,1024]{2,1,0:T(1,128)S(1)}, u32[]{:S(2)}, u32[]{:S(2)}) collective-permute-start(f32[8,1,1024]{2,1,0:T(1,128)S(1)} %get-tuple-element.46), channel_id=1, source_target_pairs={{1,0},{2,1},{3,2},{5,4},{6,5},{7,6},{9,8},{10,9},{11,10},{13,12},{... | collective-permute-start | bytes 98312 | tf_op jit(solution)/shard_map/ppermute | solution.py:19
  80.0 5.2 %collective-permute-start.9 = (f32[8,1,1024]{2,1,0:T(1,128)S(1)}, f32[8,1,1024]{2,1,0:T(1,128)S(1)}, u32[]{:S(2)}, u32[]{:S(2)}) collective-permute-start(f32[8,1,1024]{2,1,0:T(1,128)S(1)} %get-tuple-element.45), channel_id=1, source_target_pairs={{0,1},{1,2},{2,3},{4,5},{5,6},{6,7},{8,9},{9,10},{10,11},{12,13},{... | collective-permute-start | bytes 98312 | tf_op jit(solution)/shard_map/ppermute | solution.py:18
  97.5 18.3 %copy-start.12 = (f32[8,32,128]{2,1,0:T(8,128)S(1)}, f32[8,32,128]{2,1,0:T(8,128)}, u32[]{:S(2)}) copy-start(f32[8,32,128]{2,1,0:T(8,128)} %param.24) | copy-start | bytes 393220
  98.9 26.9 %all-to-all-start = ((f32[32,1,1536]{2,1,0:T(1,128)}), f32[32,1,1536]{2,1,0:T(1,128)S(1)}, u32[]{:S(2)}, u32[]{:S(2)}) async-start(f32[32,1,1536]{2,1,0:T(1,128)} %reshape.97), calls=%async_computation | async-start | bytes 393216 | tf_op jit(solution)/shard_map/all_to_all | solution.py:121
  128.6 4.0 %collective-permute-start.10 = (f32[3,3,32,128]{3,2,1,0:T(8,128)S(1)}, f32[3,3,32,128]{3,2,1,0:T(8,128)S(1)}, u32[]{:S(2)}, u32[]{:S(2)}) collective-permute-start(f32[3,3,32,128]{3,2,1,0:T(8,128)S(1)} %get-tuple-element.63), channel_id=1, source_target_pairs={{0,4},{4,8},{8,12},{12,16},{16,20},{20,24},{24,28},{28,32},{32,36}... | collective-permute-start | bytes 442376 | tf_op jit(solution)/shard_map/ppermute | solution.py:137
  130.6 9.3 %collective-permute-start.11 = (f32[3,3,32,128]{3,2,1,0:T(8,128)S(1)}, f32[3,3,32,128]{3,2,1,0:T(8,128)S(1)}, u32[]{:S(2)}, u32[]{:S(2)}) collective-permute-start(f32[3,3,32,128]{3,2,1,0:T(8,128)S(1)} %get-tuple-element.64), channel_id=1, source_target_pairs={{4,0},{8,4},{12,8},{16,12},{20,16},{24,20},{28,24},{32,28},{36,32}... | collective-permute-start | bytes 442376 | tf_op jit(solution)/shard_map/ppermute | solution.py:138
  139.9 6.8 %collective-permute-start.12 = (f32[3,14,8,128]{3,2,1,0:T(8,128)S(1)}, f32[3,14,8,128]{3,2,1,0:T(8,128)S(1)}, u32[]{:S(2)}, u32[]{:S(2)}) collective-permute-start(f32[3,14,8,128]{3,2,1,0:T(8,128)S(1)} %get-tuple-element.61), channel_id=1, source_target_pairs={{0,1},{1,2},{2,3},{4,5},{5,6},{6,7},{8,9},{9,10},{10,11},{12,13},{... | collective-permute-start | bytes 516104 | tf_op jit(solution)/shard_map/ppermute | solution.py:137
  144.3 6.7 %collective-permute-start.13 = (f32[3,14,8,128]{3,2,1,0:T(8,128)S(1)}, f32[3,14,8,128]{3,2,1,0:T(8,128)S(1)}, u32[]{:S(2)}, u32[]{:S(2)}) collective-permute-start(f32[3,14,8,128]{3,2,1,0:T(8,128)S(1)} %get-tuple-element.62), channel_id=1, source_target_pairs={{1,0},{2,1},{3,2},{5,4},{6,5},{7,6},{9,8},{10,9},{11,10},{13,12},{... | collective-permute-start | bytes 516104 | tf_op jit(solution)/shard_map/ppermute | solution.py:138
  152.1 22.8 %copy-start.10 = (f32[8,32,128]{2,1,0:T(8,128)}, f32[8,32,128]{2,1,0:T(8,128)S(1)}, u32[]{:S(2)}) copy-start(f32[8,32,128]{2,1,0:T(8,128)S(1)} %fusion.105) | copy-start | bytes 393220
  152.7 22.5 %copy-start.14 = (f32[6,10]{1,0:T(8,128)S(1)}, f32[6,10]{1,0:T(8,128)}, u32[]{:S(2)}) copy-start(f32[6,10]{1,0:T(8,128)} %copy-done.13) | copy-start | bytes 724
  (6 other events, 20.5 us)

commit v8 on v5

--- a/solution.py
+++ b/solution.py
@@ -38,8 +38,7 @@
 
 def bernoulli(value):
     small = jnp.abs(value) < 0.0001
-    safe = jnp.where(small, jnp.float32(1.0), value)
-    return jnp.where(small, 1.0 - 0.5 * value, safe / (jnp.exp(safe) - 1.0))
+    return jnp.where(small, 1.0 - 0.5 * value, value / (jnp.exp(value) - 1.0))
 
 
 def per_device(

time: 178 us -> 177 us (level)
  no operation moved by 1% of the time
where the time goes in v8:
time: 177 us; the launch traced here: 175 us
  starting transfers between devices  57.7 us (33%)
  other arithmetic  49.3 us (28%)
  waiting for transfers between devices  24.8 us (14%)
  blocking collectives  17.6 us (10%)
  local copies, waits for them, and re-layouts  13.6 us (8%)
  matrix products  10.5 us (6%)
    ppermute x5, starting transfers between devices, face_halos(): lax.ppermute(lax.slice_in_dim(block, size - 1, size, axis=dim), axis, for...  23.1 us
    all_to_all x1, blocking collectives, per_device(): got_warm = lax.all_to_all(windows, 'slab', 0, 0, tiled=False)  17.6 us
    div x2, other arithmetic, sweep(): return fraction_top_quantity / denominator_quantity  17.4 us
    another operation x6, other arithmetic, per_device(): both = jnp.stack([effective, initial_electrons])  14.6 us
    all_to_all x1, starting transfers between devices, per_device(): got = lax.all_to_all(piece, 'slab', 0, 0, tiled=False)  12.6 us
    all_to_all x1, waiting for transfers between devices, per_device(): got = lax.all_to_all(piece, 'slab', 0, 0, tiled=False)  9.79 us
    ppermute x5, waiting for transfers between devices, face_halos(): high = lax.ppermute(lax.slice_in_dim(block, 0, 1, axis=dim), axis, backward)  9.4 us
    ppermute x2, starting transfers between devices, per_device(): lax.ppermute(lax.slice_in_dim(stacked, size - depth, size, axis=dim), axi...  9.33 us
  transfers between devices with their start and end apart: 15, of which 7 were waited for; matrix products, arithmetic and copies ran while one was open for 10% of the time, Pallas kernels for 0%

profile of v8, /device:TPU:1, one launch (start us, length us, event | category | flops | bytes accessed | tf_op | source)
XLA Modules:
  0.0 174.6 jit_solution(7460882304590384398)
XLA Ops:
  2.1 5.8 %select_add_fusion = f32[8,64,1024]{2,1,0:T(8,128)S(1)} fusion(f32[8,64,1024]{2,1,0:T(8,128)} %param.15, s32[8,64,1024]{2,1,0:T(8,128)} %param.19, f32[]{:T(128)} %bitcast.3, f32[]{:T(128)} %bitcast.2, f32[]{:T(128)} %bitcast.1, f32[]{:T(128)} %bitcast), kind=kLoop, calls=%fused_computation.118 | loop fusion | flops 6291456 | bytes 6291472 | tf_op jit(solution)/shard_map/add | solution.py:63
  8.6 4.5 %collective-permute-start.3 = (f32[2,8,1,1024]{3,2,1,0:T(1,128)}, f32[2,8,1,1024]{3,2,1,0:T(1,128)S(1)}, u32[]{:S(2)}, u32[]{:S(2)}) collective-permute-start(f32[2,8,1,1024]{3,2,1,0:T(1,128)} %get-tuple-element.40), channel_id=1, source_target_pairs={{0,1},{1,2},{2,3},{4,5},{5,6},{6,7},{8,9},{9,10},{10,11},{12,13},{... | collective-permute-start | bytes 196616 | tf_op jit(solution)/shard_map/ppermute | solution.py:18
  16.1 4.4 %collective-permute-start.1 = (f32[2,1,64,1024]{3,2,1,0:T(8,128)}, f32[2,1,64,1024]{3,2,1,0:T(8,128)S(1)}, u32[]{:S(2)}, u32[]{:S(2)}) collective-permute-start(f32[2,1,64,1024]{3,2,1,0:T(8,128)} %get-tuple-element.36), channel_id=1, source_target_pairs={{0,4},{4,8},{8,12},{12,16},{16,20},{20,24},{24,28},{28,32},{32,36}... | collective-permute-start | bytes 1572872 | tf_op jit(solution)/shard_map/ppermute | solution.py:18
  21.8 3.1 %fusion = f32[2,8,64,1023]{3,2,1,0:T(8,128)} fusion(f32[1,8,64,1024]{3,2,1,0:T(8,128)S(1)} %bitcast.209, f32[1,8,64,1024]{3,2,1,0:T(8,128)S(1)} %bitcast.216), kind=kLoop, calls=%fused_computation.18 | loop fusion | flops 1047552 | bytes 8384512 | tf_op jit(solution)/shard_map/stack | solution.py:67
  24.9 3.2 %select_maximum_fusion = f32[2,8,64,1024]{3,2,1,0:T(8,128)} fusion(f32[1,8,64,1024]{3,2,1,0:T(8,128)S(1)} %bitcast.217, f32[1,8,64,1024]{3,2,1,0:T(8,128)S(1)} %bitcast.210), kind=kLoop, calls=%fused_computation.21 | loop fusion | flops 4194304 | bytes 8388608 | tf_op jit(solution)/shard_map/stack | solution.py:67
  28.1 3.4 %fusion.3 = (f32[2,7,64,1024]{3,2,1,0:T(8,128)}, f32[2,7,64,1024]{3,2,1,0:T(8,128)}) fusion(f32[1,8,64,1024]{3,2,1,0:T(8,128)S(1)} %bitcast.211, f32[1,8,64,1024]{3,2,1,0:T(8,128)S(1)} %bitcast.218), kind=kLoop, calls=%fused_computation.33 | loop fusion | flops 1835008 | bytes 11534336 | tf_op jit(solution)/shard_map/stack | solution.py:67
  31.6 3.1 %fusion.1 = (f32[2,8,63,1024]{3,2,1,0:T(8,128)S(1)}, f32[2,8,63,1024]{3,2,1,0:T(8,128)S(1)}) fusion(f32[1,8,64,1024]{3,2,1,0:T(8,128)S(1)} %bitcast.212, f32[1,8,64,1024]{3,2,1,0:T(8,128)} %bitcast.213), kind=kLoop, calls=%fused_computation.19 | loop fusion | flops 2064384 | bytes 12451840 | tf_op jit(solution)/shard_map/stack | solution.py:67
  34.8 9.4 %collective-permute-done = f32[2,1,64,1024]{3,2,1,0:T(8,128)S(1)} collective-permute-done((f32[2,1,64,1024]{3,2,1,0:T(8,128)}, f32[2,1,64,1024]{3,2,1,0:T(8,128)S(1)}, u32[]{:S(2)}, u32[]{:S(2)}) %collective-permute-start) | collective-permute-done | bytes 524320 | tf_op jit(solution)/shard_map/ppermute | solution.py:19
  44.2 8.6 %fusion.17 = (f32[8,64,1024]{2,1,0:T(8,128)S(1)}, f32[8,64,1024]{2,1,0:T(8,128)S(1)}, f32[8,64,1024]{2,1,0:T(8,128)S(1)}) fusion(f32[2,8,64,1023]{3,2,1,0:T(8,128)S(1)} %copy-done.3, f32[2,8,64,1024]{3,2,1,0:T(8,128)S(1)} %copy-done.4, f32[2,8,63,1024]{3,2,1,0:T(8,128)S(1)} %get-tuple-element.38, f32[2,8,1,1024]{3,2,1,0:T(1,128)S(1)} %collective-permute-done.3, ...), kind=kLoop, calls=%fused_computation.47 | loop fusion | flops 42467328 | bytes 37744640 | tf_op jit(solution)/shard_map/div | solution.py:81
  53.5 2.1 %fusion.129 = (f32[8,64,1023]{2,1,0:T(8,128)S(1)}, f32[8,64,1023]{2,1,0:T(8,128)}) fusion(f32[8,64,1024]{2,1,0:T(8,128)S(1)} %get-tuple-element.30), kind=kLoop, calls=%fused_computation.234 | loop fusion | bytes 8380416 | tf_op jit(solution)/shard_map/slice | solution.py:34
  56.9 5.5 %collective-permute-start.5 = (f32[1,64,1024]{2,1,0:T(8,128)S(1)}, f32[1,64,1024]{2,1,0:T(8,128)S(1)}, u32[]{:S(2)}, u32[]{:S(2)}) collective-permute-start(f32[1,64,1024]{2,1,0:T(8,128)S(1)} %get-tuple-element.57), channel_id=1, source_target_pairs={{0,4},{4,8},{8,12},{12,16},{16,20},{20,24},{24,28},{28,32},{32,36}... | collective-permute-start | bytes 786440 | tf_op jit(solution)/shard_map/ppermute | solution.py:18
  64.4 4.9 %collective-permute-start.7 = (f32[8,1,1024]{2,1,0:T(1,128)S(1)}, f32[8,1,1024]{2,1,0:T(1,128)S(1)}, u32[]{:S(2)}, u32[]{:S(2)}) collective-permute-start(f32[8,1,1024]{2,1,0:T(1,128)S(1)} %get-tuple-element.53), channel_id=1, source_target_pairs={{0,1},{1,2},{2,3},{4,5},{5,6},{6,7},{8,9},{9,10},{10,11},{12,13},{... | collective-permute-start | bytes 98312 | tf_op jit(solution)/shard_map/ppermute | solution.py:18
  69.2 2.3 %fusion.133 = (f32[7,64,1024]{2,1,0:T(8,128)}, f32[7,64,1024]{2,1,0:T(8,128)}) fusion(f32[8,64,1024]{2,1,0:T(8,128)S(1)} %get-tuple-element.30), kind=kLoop, calls=%fused_computation.238 | loop fusion | bytes 7340032 | tf_op jit(solution)/shard_map/slice | solution.py:30
  71.6 8.8 %fusion.50 = f32[8,64,1024]{2,1,0:T(8,128)S(1)} fusion(f32[8,64,1024]{2,1,0:T(8,128)S(1)} %copy-done.6, f32[1,64,1024]{2,1,0:T(8,128)S(1)} %collective-permute-done.4, f32[7,64,1024]{2,1,0:T(8,128)} %get-tuple-element.60, f32[7,64,1024]{2,1,0:T(8,128)} %get-tuple-element.59, f32[1,64,1024]{2,1,0:T(8,128)S(1)} %collective-permute-done.5, ...), kind=kLoop, calls=%fused_computation.87 | loop fusion | flops 40370176 | bytes 39837696 | tf_op jit(solution)/shard_map/div | solution.py:81
  85.2 3.8 %collective-permute-start.9 = (f32[8,1,1024]{2,1,0:T(1,128)S(1)}, f32[8,1,1024]{2,1,0:T(1,128)S(1)}, u32[]{:S(2)}, u32[]{:S(2)}) collective-permute-start(f32[8,1,1024]{2,1,0:T(1,128)S(1)} %get-tuple-element.47), channel_id=1, source_target_pairs={{0,1},{1,2},{2,3},{4,5},{5,6},{6,7},{8,9},{9,10},{10,11},{12,13},{... | collective-permute-start | bytes 98312 | tf_op jit(solution)/shard_map/ppermute | solution.py:18
  89.8 7.8 %fusion.57 = f32[8,64,1024]{2,1,0:T(8,128)S(1)} fusion(f32[8,1,1024]{2,1,0:T(1,128)S(1)} %collective-permute-done.8, f32[8,63,1024]{2,1,0:T(8,128)S(1)} %get-tuple-element.50, f32[8,63,1024]{2,1,0:T(8,128)S(1)} %get-tuple-element.49, f32[8,1,1024]{2,1,0:T(1,128)S(1)} %collective-permute-done.9, f32[8,64,1024]{2,1,0:T(8,128)S(1)} %fusion.50, ...), kind=kLoop, calls=%fused_computation.98 | loop fusion | flops 45088768 | bytes 37216256 | tf_op jit(solution)/shard_map/mul | solution.py:99
  102.4 12.6 %all-to-all-start = ((f32[32,1,1536]{2,1,0:T(1,128)}), f32[32,1,1536]{2,1,0:T(1,128)S(1)}, u32[]{:S(2)}, u32[]{:S(2)}) async-start(f32[32,1,1536]{2,1,0:T(1,128)} %reshape.97), calls=%async_computation | async-start | bytes 393216 | tf_op jit(solution)/shard_map/all_to_all | solution.py:119
  115.1 9.8 %all-to-all-done = f32[32,1,1536]{2,1,0:T(1,128)S(1)} async-done(((f32[32,1,1536]{2,1,0:T(1,128)}), f32[32,1,1536]{2,1,0:T(1,128)S(1)}, u32[]{:S(2)}, u32[]{:S(2)}) %all-to-all-start) | async-done | bytes 196640 | tf_op jit(solution)/shard_map/all_to_all | solution.py:119
  129.0 5.5 %collective-permute-start.10 = (f32[3,3,32,128]{3,2,1,0:T(8,128)S(1)}, f32[3,3,32,128]{3,2,1,0:T(8,128)S(1)}, u32[]{:S(2)}, u32[]{:S(2)}) collective-permute-start(f32[3,3,32,128]{3,2,1,0:T(8,128)S(1)} %get-tuple-element.67), channel_id=1, source_target_pairs={{0,4},{4,8},{8,12},{12,16},{16,20},{20,24},{24,28},{28,32},{32,36}... | collective-permute-start | bytes 442376 | tf_op jit(solution)/shard_map/ppermute | solution.py:135
  134.6 2.0 %collective-permute-done.11 = f32[3,3,32,128]{3,2,1,0:T(8,128)S(1)} collective-permute-done((f32[3,3,32,128]{3,2,1,0:T(8,128)S(1)}, f32[3,3,32,128]{3,2,1,0:T(8,128)S(1)}, u32[]{:S(2)}, u32[]{:S(2)}) %collective-permute-start.11) | collective-permute-done | bytes 147488 | tf_op jit(solution)/shard_map/ppermute | solution.py:136
  137.4 3.1 %collective-permute-start.13 = (f32[3,14,8,128]{3,2,1,0:T(8,128)S(1)}, f32[3,14,8,128]{3,2,1,0:T(8,128)S(1)}, u32[]{:S(2)}, u32[]{:S(2)}) collective-permute-start(f32[3,14,8,128]{3,2,1,0:T(8,128)S(1)} %get-tuple-element.66), channel_id=1, source_target_pairs={{1,0},{2,1},{3,2},{5,4},{6,5},{7,6},{9,8},{10,9},{11,10},{13,12},{... | collective-permute-start | bytes 516104 | tf_op jit(solution)/shard_map/ppermute | solution.py:136
  140.5 3.8 %collective-permute-start.12 = (f32[3,14,8,128]{3,2,1,0:T(8,128)S(1)}, f32[3,14,8,128]{3,2,1,0:T(8,128)S(1)}, u32[]{:S(2)}, u32[]{:S(2)}) collective-permute-start(f32[3,14,8,128]{3,2,1,0:T(8,128)S(1)} %get-tuple-element.65), channel_id=1, source_target_pairs={{0,1},{1,2},{2,3},{4,5},{5,6},{6,7},{8,9},{9,10},{10,11},{12,13},{... | collective-permute-start | bytes 516104 | tf_op jit(solution)/shard_map/ppermute | solution.py:135
  149.1 17.6 %all_to_all.10 = f32[32,1,1536]{2,1,0:T(1,128)S(1)} all-to-all(f32[32,1,1536]{2,1,0:T(1,128)S(1)} %reshape.99), channel_id=1, replica_groups=mesh['slab'=32,'gy'=4] {'slab'}, dimensions={0} | all-to-all | bytes 393216 | tf_op jit(solution)/shard_map/all_to_all | solution.py:174
  170.8 3.8 %bitcast_multiply_fusion = f32[8,64,1024]{2,1,0:T(8,128)} fusion(f32[32,8,8,64]{3,0,1,2:T(8,128)S(1)} %fusion.66, f32[32,8,1024]{2,1,0:T(8,128)S(1)} %bitcast.219), kind=kOutput, calls=%fused_computation.102 | convolution fusion | flops 1611137024 | bytes 3670016 | tf_op jit(solution)/shard_map/scxy,scz->xyz/dot_general | solution.py:178
  (92 shorter events, 34.6 us)
Async XLA Ops:
  0.6 97.0 %copy-start = (f32[32,64]{1,0:T(8,128)S(1)}, f32[32,64]{1,0:T(8,128)}, u32[]{:S(2)}) copy-start(f32[32,64]{1,0:T(8,128)} %param.22) | copy-start | bytes 24580
  8.6 26.2 %collective-permute-start.3 = (f32[2,8,1,1024]{3,2,1,0:T(1,128)}, f32[2,8,1,1024]{3,2,1,0:T(1,128)S(1)}, u32[]{:S(2)}, u32[]{:S(2)}) collective-permute-start(f32[2,8,1,1024]{3,2,1,0:T(1,128)} %get-tuple-element.40), channel_id=1, source_target_pairs={{0,1},{1,2},{2,3},{4,5},{5,6},{6,7},{8,9},{9,10},{10,11},{12,13},{... | collective-permute-start | bytes 196616 | tf_op jit(solution)/shard_map/ppermute | solution.py:18
  13.1 21.7 %collective-permute-start.2 = (f32[2,8,1,1024]{3,2,1,0:T(1,128)S(1)}, f32[2,8,1,1024]{3,2,1,0:T(1,128)S(1)}, u32[]{:S(2)}, u32[]{:S(2)}) collective-permute-start(f32[2,8,1,1024]{3,2,1,0:T(1,128)S(1)} %get-tuple-element.39), channel_id=1, source_target_pairs={{1,0},{2,1},{3,2},{5,4},{6,5},{7,6},{9,8},{10,9},{11,10},{13,12},{... | collective-permute-start | bytes 196616 | tf_op jit(solution)/shard_map/ppermute | solution.py:19
  16.1 18.7 %collective-permute-start.1 = (f32[2,1,64,1024]{3,2,1,0:T(8,128)}, f32[2,1,64,1024]{3,2,1,0:T(8,128)S(1)}, u32[]{:S(2)}, u32[]{:S(2)}) collective-permute-start(f32[2,1,64,1024]{3,2,1,0:T(8,128)} %get-tuple-element.36), channel_id=1, source_target_pairs={{0,4},{4,8},{8,12},{12,16},{16,20},{20,24},{24,28},{28,32},{32,36}... | collective-permute-start | bytes 1572872 | tf_op jit(solution)/shard_map/ppermute | solution.py:18
  20.5 23.7 %collective-permute-start = (f32[2,1,64,1024]{3,2,1,0:T(8,128)}, f32[2,1,64,1024]{3,2,1,0:T(8,128)S(1)}, u32[]{:S(2)}, u32[]{:S(2)}) collective-permute-start(f32[2,1,64,1024]{3,2,1,0:T(8,128)} %get-tuple-element.35), channel_id=1, source_target_pairs={{4,0},{8,4},{12,8},{16,12},{20,16},{24,20},{28,24},{32,28},{36,32}... | collective-permute-start | bytes 1572872 | tf_op jit(solution)/shard_map/ppermute | solution.py:19
  31.6 12.6 %copy-start.3 = (f32[2,8,64,1023]{3,2,1,0:T(8,128)S(1)}, f32[2,8,64,1023]{3,2,1,0:T(8,128)}, u32[]{:S(2)}) copy-start(f32[2,8,64,1023]{3,2,1,0:T(8,128)} %fusion) | copy-start | bytes 12570628
  31.6 12.6 %copy-start.4 = (f32[2,8,64,1024]{3,2,1,0:T(8,128)S(1)}, f32[2,8,64,1024]{3,2,1,0:T(8,128)}, u32[]{:S(2)}) copy-start(f32[2,8,64,1024]{3,2,1,0:T(8,128)} %select_maximum_fusion) | copy-start | bytes 12582916
  31.6 12.6 %copy-start.5 = (f32[2,7,64,1024]{3,2,1,0:T(8,128)S(1)}, f32[2,7,64,1024]{3,2,1,0:T(8,128)}, u32[]{:S(2)}) copy-start(f32[2,7,64,1024]{3,2,1,0:T(8,128)} %get-tuple-element.33) | copy-start | bytes 11010052
  55.6 15.9 %collective-permute-start.4 = (f32[1,64,1024]{2,1,0:T(8,128)S(1)}, f32[1,64,1024]{2,1,0:T(8,128)S(1)}, u32[]{:S(2)}, u32[]{:S(2)}) collective-permute-start(f32[1,64,1024]{2,1,0:T(8,128)S(1)} %get-tuple-element.58), channel_id=1, source_target_pairs={{4,0},{8,4},{12,8},{16,12},{20,16},{24,20},{28,24},{32,28},{36,32}... | collective-permute-start | bytes 786440 | tf_op jit(solution)/shard_map/ppermute | solution.py:19
  56.9 14.7 %collective-permute-start.5 = (f32[1,64,1024]{2,1,0:T(8,128)S(1)}, f32[1,64,1024]{2,1,0:T(8,128)S(1)}, u32[]{:S(2)}, u32[]{:S(2)}) collective-permute-start(f32[1,64,1024]{2,1,0:T(8,128)S(1)} %get-tuple-element.57), channel_id=1, source_target_pairs={{0,4},{4,8},{8,12},{12,16},{16,20},{20,24},{24,28},{28,32},{32,36}... | collective-permute-start | bytes 786440 | tf_op jit(solution)/shard_map/ppermute | solution.py:18
  62.4 9.1 %collective-permute-start.6 = (f32[8,1,1024]{2,1,0:T(1,128)S(1)}, f32[8,1,1024]{2,1,0:T(1,128)S(1)}, u32[]{:S(2)}, u32[]{:S(2)}) collective-permute-start(f32[8,1,1024]{2,1,0:T(1,128)S(1)} %get-tuple-element.54), channel_id=1, source_target_pairs={{1,0},{2,1},{3,2},{5,4},{6,5},{7,6},{9,8},{10,9},{11,10},{13,12},{... | collective-permute-start | bytes 98312 | tf_op jit(solution)/shard_map/ppermute | solution.py:19
  64.3 7.2 %copy-start.6 = (f32[8,64,1024]{2,1,0:T(8,128)S(1)}, f32[8,64,1024]{2,1,0:T(8,128)}, u32[]{:S(2)}) copy-start(f32[8,64,1024]{2,1,0:T(8,128)} %param.17) | copy-start | bytes 6291460
  64.4 7.2 %copy-start.7 = (f32[8,64,1024]{2,1,0:T(8,128)S(1)}, f32[8,64,1024]{2,1,0:T(8,128)}, u32[]{:S(2)}) copy-start(f32[8,64,1024]{2,1,0:T(8,128)} %param.18) | copy-start | bytes 6291460
  64.4 7.2 %collective-permute-start.7 = (f32[8,1,1024]{2,1,0:T(1,128)S(1)}, f32[8,1,1024]{2,1,0:T(1,128)S(1)}, u32[]{:S(2)}, u32[]{:S(2)}) collective-permute-start(f32[8,1,1024]{2,1,0:T(1,128)S(1)} %get-tuple-element.53), channel_id=1, source_target_pairs={{0,1},{1,2},{2,3},{4,5},{5,6},{6,7},{8,9},{9,10},{10,11},{12,13},{... | collective-permute-start | bytes 98312 | tf_op jit(solution)/shard_map/ppermute | solution.py:18
  80.4 9.4 %copy-start.1 = (f32[8,64,1024]{2,1,0:T(8,128)}, f32[8,64,1024]{2,1,0:T(8,128)S(1)}, u32[]{:S(2)}) copy-start(f32[8,64,1024]{2,1,0:T(8,128)S(1)} %fusion.50) | copy-start | bytes 6291460
  83.2 6.0 %collective-permute-start.8 = (f32[8,1,1024]{2,1,0:T(1,128)S(1)}, f32[8,1,1024]{2,1,0:T(1,128)S(1)}, u32[]{:S(2)}, u32[]{:S(2)}) collective-permute-start(f32[8,1,1024]{2,1,0:T(1,128)S(1)} %get-tuple-element.48), channel_id=1, source_target_pairs={{1,0},{2,1},{3,2},{5,4},{6,5},{7,6},{9,8},{10,9},{11,10},{13,12},{... | collective-permute-start | bytes 98312 | tf_op jit(solution)/shard_map/ppermute | solution.py:19
  85.2 4.7 %collective-permute-start.9 = (f32[8,1,1024]{2,1,0:T(1,128)S(1)}, f32[8,1,1024]{2,1,0:T(1,128)S(1)}, u32[]{:S(2)}, u32[]{:S(2)}) collective-permute-start(f32[8,1,1024]{2,1,0:T(1,128)S(1)} %get-tuple-element.47), channel_id=1, source_target_pairs={{0,1},{1,2},{2,3},{4,5},{5,6},{6,7},{8,9},{9,10},{10,11},{12,13},{... | collective-permute-start | bytes 98312 | tf_op jit(solution)/shard_map/ppermute | solution.py:18
  101.0 14.0 %copy-start.12 = (f32[8,32,128]{2,1,0:T(8,128)S(1)}, f32[8,32,128]{2,1,0:T(8,128)}, u32[]{:S(2)}) copy-start(f32[8,32,128]{2,1,0:T(8,128)} %param.24) | copy-start | bytes 393220
  102.4 22.4 %all-to-all-start = ((f32[32,1,1536]{2,1,0:T(1,128)}), f32[32,1,1536]{2,1,0:T(1,128)S(1)}, u32[]{:S(2)}, u32[]{:S(2)}) async-start(f32[32,1,1536]{2,1,0:T(1,128)} %reshape.97), calls=%async_computation | async-start | bytes 393216 | tf_op jit(solution)/shard_map/all_to_all | solution.py:119
  127.7 8.8 %collective-permute-start.11 = (f32[3,3,32,128]{3,2,1,0:T(8,128)S(1)}, f32[3,3,32,128]{3,2,1,0:T(8,128)S(1)}, u32[]{:S(2)}, u32[]{:S(2)}) collective-permute-start(f32[3,3,32,128]{3,2,1,0:T(8,128)S(1)} %get-tuple-element.68), channel_id=1, source_target_pairs={{4,0},{8,4},{12,8},{16,12},{20,16},{24,20},{28,24},{32,28},{36,32}... | collective-permute-start | bytes 442376 | tf_op jit(solution)/shard_map/ppermute | solution.py:136
  129.0 8.4 %collective-permute-start.10 = (f32[3,3,32,128]{3,2,1,0:T(8,128)S(1)}, f32[3,3,32,128]{3,2,1,0:T(8,128)S(1)}, u32[]{:S(2)}, u32[]{:S(2)}) collective-permute-start(f32[3,3,32,128]{3,2,1,0:T(8,128)S(1)} %get-tuple-element.67), channel_id=1, source_target_pairs={{0,4},{4,8},{8,12},{12,16},{16,20},{20,24},{24,28},{28,32},{32,36}... | collective-permute-start | bytes 442376 | tf_op jit(solution)/shard_map/ppermute | solution.py:135
  137.4 8.1 %collective-permute-start.13 = (f32[3,14,8,128]{3,2,1,0:T(8,128)S(1)}, f32[3,14,8,128]{3,2,1,0:T(8,128)S(1)}, u32[]{:S(2)}, u32[]{:S(2)}) collective-permute-start(f32[3,14,8,128]{3,2,1,0:T(8,128)S(1)} %get-tuple-element.66), channel_id=1, source_target_pairs={{1,0},{2,1},{3,2},{5,4},{6,5},{7,6},{9,8},{10,9},{11,10},{13,12},{... | collective-permute-start | bytes 516104 | tf_op jit(solution)/shard_map/ppermute | solution.py:136
  140.5 6.2 %collective-permute-start.12 = (f32[3,14,8,128]{3,2,1,0:T(8,128)S(1)}, f32[3,14,8,128]{3,2,1,0:T(8,128)S(1)}, u32[]{:S(2)}, u32[]{:S(2)}) collective-permute-start(f32[3,14,8,128]{3,2,1,0:T(8,128)S(1)} %get-tuple-element.65), channel_id=1, source_target_pairs={{0,1},{1,2},{2,3},{4,5},{5,6},{6,7},{8,9},{9,10},{10,11},{12,13},{... | collective-permute-start | bytes 516104 | tf_op jit(solution)/shard_map/ppermute | solution.py:135
  147.7 20.0 %copy-start.10 = (f32[8,32,128]{2,1,0:T(8,128)}, f32[8,32,128]{2,1,0:T(8,128)S(1)}, u32[]{:S(2)}) copy-start(f32[8,32,128]{2,1,0:T(8,128)S(1)} %fusion.96) | copy-start | bytes 393220
  (4 other events, 11.7 us)

commit v9 on v8

--- a/solution.py
+++ b/solution.py
@@ -58,11 +58,14 @@
     slab_cells = electrostatic_voltages.shape[0]
     slabs = lax.axis_size("slab")
     me = lax.axis_index("slab")
-    effective = electrostatic_voltages
-    for grain in range(GRAINS):
-        effective = effective + jnp.where(
-            crystal_orientation_class == grain, crystal_barrier_shift[grain], jnp.float32(0.0)
-        )
+    shifts = [crystal_barrier_shift[grain] for grain in range(GRAINS)]
+    cls = crystal_orientation_class
+    shift = jnp.where(
+        cls < 2,
+        jnp.where(cls == 0, shifts[0], shifts[1]),
+        jnp.where(cls == 2, shifts[2], shifts[3]),
+    )
+    effective = electrostatic_voltages + shift
     device_sides = (("slab", 0), ("gy", 1))
     both = jnp.stack([effective, initial_electrons])
     both_halos = face_halos(both, (("slab", 1), ("gy", 2)))

time: 177 us -> 177 us (level)
  no operation moved by 1% of the time
where the time goes in v9:
time: 177 us; the launch traced here: 174 us
  starting transfers between devices  57.7 us (33%)
  other arithmetic  49.2 us (28%)
  waiting for transfers between devices  24.8 us (14%)
  blocking collectives  17.6 us (10%)
  local copies, waits for them, and re-layouts  13.6 us (8%)
  matrix products  10.5 us (6%)
    ppermute x5, starting transfers between devices, face_halos(): lax.ppermute(lax.slice_in_dim(block, size - 1, size, axis=dim), axis, for...  23.1 us
    all_to_all x1, blocking collectives, per_device(): got_warm = lax.all_to_all(windows, 'slab', 0, 0, tiled=False)  17.6 us
    div x2, other arithmetic, sweep(): return fraction_top_quantity / denominator_quantity  17.4 us
    another operation x6, other arithmetic, per_device(): both = jnp.stack([effective, initial_electrons])  14.6 us
    all_to_all x1, starting transfers between devices, per_device(): got = lax.all_to_all(piece, 'slab', 0, 0, tiled=False)  12.6 us
    all_to_all x1, waiting for transfers between devices, per_device(): got = lax.all_to_all(piece, 'slab', 0, 0, tiled=False)  9.79 us
    ppermute x5, waiting for transfers between devices, face_halos(): high = lax.ppermute(lax.slice_in_dim(block, 0, 1, axis=dim), axis, backward)  9.4 us
    ppermute x2, starting transfers between devices, per_device(): lax.ppermute(lax.slice_in_dim(stacked, size - depth, size, axis=dim), axi...  9.33 us
  transfers between devices with their start and end apart: 15, of which 7 were waited for; matrix products, arithmetic and copies ran while one was open for 10% of the time, Pallas kernels for 0%

profile of v9, /device:TPU:1, one launch (start us, length us, event | category | flops | bytes accessed | tf_op | source)
XLA Modules:
  0.0 174.4 jit_solution(14438105452260125960)
XLA Ops:
  2.1 5.7 %select_add_fusion = f32[8,64,1024]{2,1,0:T(8,128)S(1)} fusion(f32[8,64,1024]{2,1,0:T(8,128)} %param.15, s32[8,64,1024]{2,1,0:T(8,128)} %param.19, f32[]{:T(128)} %bitcast.3, f32[]{:T(128)} %bitcast.2, f32[]{:T(128)} %bitcast.1, f32[]{:T(128)} %bitcast), kind=kLoop, calls=%fused_computation.118 | loop fusion | flops 3670016 | bytes 6291472 | tf_op jit(solution)/shard_map/add | solution.py:68
  8.5 4.5 %collective-permute-start.3 = (f32[2,8,1,1024]{3,2,1,0:T(1,128)}, f32[2,8,1,1024]{3,2,1,0:T(1,128)S(1)}, u32[]{:S(2)}, u32[]{:S(2)}) collective-permute-start(f32[2,8,1,1024]{3,2,1,0:T(1,128)} %get-tuple-element.40), channel_id=1, source_target_pairs={{0,1},{1,2},{2,3},{4,5},{5,6},{6,7},{8,9},{9,10},{10,11},{12,13},{... | collective-permute-start | bytes 196616 | tf_op jit(solution)/shard_map/ppermute | solution.py:18
  16.0 4.4 %collective-permute-start.1 = (f32[2,1,64,1024]{3,2,1,0:T(8,128)}, f32[2,1,64,1024]{3,2,1,0:T(8,128)S(1)}, u32[]{:S(2)}, u32[]{:S(2)}) collective-permute-start(f32[2,1,64,1024]{3,2,1,0:T(8,128)} %get-tuple-element.36), channel_id=1, source_target_pairs={{0,4},{4,8},{8,12},{12,16},{16,20},{20,24},{24,28},{28,32},{32,36}... | collective-permute-start | bytes 1572872 | tf_op jit(solution)/shard_map/ppermute | solution.py:18
  21.7 3.1 %fusion = f32[2,8,64,1023]{3,2,1,0:T(8,128)} fusion(f32[1,8,64,1024]{3,2,1,0:T(8,128)S(1)} %bitcast.209, f32[1,8,64,1024]{3,2,1,0:T(8,128)S(1)} %bitcast.216), kind=kLoop, calls=%fused_computation.18 | loop fusion | flops 1047552 | bytes 8384512 | tf_op jit(solution)/shard_map/stack | solution.py:70
  24.8 3.2 %select_maximum_fusion = f32[2,8,64,1024]{3,2,1,0:T(8,128)} fusion(f32[1,8,64,1024]{3,2,1,0:T(8,128)S(1)} %bitcast.217, f32[1,8,64,1024]{3,2,1,0:T(8,128)S(1)} %bitcast.210), kind=kLoop, calls=%fused_computation.21 | loop fusion | flops 4194304 | bytes 8388608 | tf_op jit(solution)/shard_map/stack | solution.py:70
  28.0 3.4 %fusion.3 = (f32[2,7,64,1024]{3,2,1,0:T(8,128)}, f32[2,7,64,1024]{3,2,1,0:T(8,128)}) fusion(f32[1,8,64,1024]{3,2,1,0:T(8,128)S(1)} %bitcast.211, f32[1,8,64,1024]{3,2,1,0:T(8,128)S(1)} %bitcast.218), kind=kLoop, calls=%fused_computation.33 | loop fusion | flops 1835008 | bytes 11534336 | tf_op jit(solution)/shard_map/stack | solution.py:70
  31.5 3.1 %fusion.1 = (f32[2,8,63,1024]{3,2,1,0:T(8,128)S(1)}, f32[2,8,63,1024]{3,2,1,0:T(8,128)S(1)}) fusion(f32[1,8,64,1024]{3,2,1,0:T(8,128)S(1)} %bitcast.212, f32[1,8,64,1024]{3,2,1,0:T(8,128)} %bitcast.213), kind=kLoop, calls=%fused_computation.19 | loop fusion | flops 2064384 | bytes 12451840 | tf_op jit(solution)/shard_map/stack | solution.py:70
  34.7 9.4 %collective-permute-done = f32[2,1,64,1024]{3,2,1,0:T(8,128)S(1)} collective-permute-done((f32[2,1,64,1024]{3,2,1,0:T(8,128)}, f32[2,1,64,1024]{3,2,1,0:T(8,128)S(1)}, u32[]{:S(2)}, u32[]{:S(2)}) %collective-permute-start) | collective-permute-done | bytes 524320 | tf_op jit(solution)/shard_map/ppermute | solution.py:19
  44.1 8.6 %fusion.17 = (f32[8,64,1024]{2,1,0:T(8,128)S(1)}, f32[8,64,1024]{2,1,0:T(8,128)S(1)}, f32[8,64,1024]{2,1,0:T(8,128)S(1)}) fusion(f32[2,8,64,1023]{3,2,1,0:T(8,128)S(1)} %copy-done.3, f32[2,8,64,1024]{3,2,1,0:T(8,128)S(1)} %copy-done.4, f32[2,8,63,1024]{3,2,1,0:T(8,128)S(1)} %get-tuple-element.38, f32[2,8,1,1024]{3,2,1,0:T(1,128)S(1)} %collective-permute-done.3, ...), kind=kLoop, calls=%fused_computation.47 | loop fusion | flops 42467328 | bytes 37744640 | tf_op jit(solution)/shard_map/div | solution.py:84
  53.4 2.1 %fusion.129 = (f32[8,64,1023]{2,1,0:T(8,128)S(1)}, f32[8,64,1023]{2,1,0:T(8,128)}) fusion(f32[8,64,1024]{2,1,0:T(8,128)S(1)} %get-tuple-element.30), kind=kLoop, calls=%fused_computation.234 | loop fusion | bytes 8380416 | tf_op jit(solution)/shard_map/slice | solution.py:34
  56.8 5.5 %collective-permute-start.5 = (f32[1,64,1024]{2,1,0:T(8,128)S(1)}, f32[1,64,1024]{2,1,0:T(8,128)S(1)}, u32[]{:S(2)}, u32[]{:S(2)}) collective-permute-start(f32[1,64,1024]{2,1,0:T(8,128)S(1)} %get-tuple-element.57), channel_id=1, source_target_pairs={{0,4},{4,8},{8,12},{12,16},{16,20},{20,24},{24,28},{28,32},{32,36}... | collective-permute-start | bytes 786440 | tf_op jit(solution)/shard_map/ppermute | solution.py:18
  64.3 4.9 %collective-permute-start.7 = (f32[8,1,1024]{2,1,0:T(1,128)S(1)}, f32[8,1,1024]{2,1,0:T(1,128)S(1)}, u32[]{:S(2)}, u32[]{:S(2)}) collective-permute-start(f32[8,1,1024]{2,1,0:T(1,128)S(1)} %get-tuple-element.53), channel_id=1, source_target_pairs={{0,1},{1,2},{2,3},{4,5},{5,6},{6,7},{8,9},{9,10},{10,11},{12,13},{... | collective-permute-start | bytes 98312 | tf_op jit(solution)/shard_map/ppermute | solution.py:18
  69.1 2.3 %fusion.133 = (f32[7,64,1024]{2,1,0:T(8,128)}, f32[7,64,1024]{2,1,0:T(8,128)}) fusion(f32[8,64,1024]{2,1,0:T(8,128)S(1)} %get-tuple-element.30), kind=kLoop, calls=%fused_computation.238 | loop fusion | bytes 7340032 | tf_op jit(solution)/shard_map/slice | solution.py:30
  71.5 8.8 %fusion.50 = f32[8,64,1024]{2,1,0:T(8,128)S(1)} fusion(f32[8,64,1024]{2,1,0:T(8,128)S(1)} %copy-done.6, f32[1,64,1024]{2,1,0:T(8,128)S(1)} %collective-permute-done.4, f32[7,64,1024]{2,1,0:T(8,128)} %get-tuple-element.60, f32[7,64,1024]{2,1,0:T(8,128)} %get-tuple-element.59, f32[1,64,1024]{2,1,0:T(8,128)S(1)} %collective-permute-done.5, ...), kind=kLoop, calls=%fused_computation.87 | loop fusion | flops 40370176 | bytes 39837696 | tf_op jit(solution)/shard_map/div | solution.py:84
  85.0 3.8 %collective-permute-start.9 = (f32[8,1,1024]{2,1,0:T(1,128)S(1)}, f32[8,1,1024]{2,1,0:T(1,128)S(1)}, u32[]{:S(2)}, u32[]{:S(2)}) collective-permute-start(f32[8,1,1024]{2,1,0:T(1,128)S(1)} %get-tuple-element.47), channel_id=1, source_target_pairs={{0,1},{1,2},{2,3},{4,5},{5,6},{6,7},{8,9},{9,10},{10,11},{12,13},{... | collective-permute-start | bytes 98312 | tf_op jit(solution)/shard_map/ppermute | solution.py:18
  89.7 7.8 %fusion.57 = f32[8,64,1024]{2,1,0:T(8,128)S(1)} fusion(f32[8,1,1024]{2,1,0:T(1,128)S(1)} %collective-permute-done.8, f32[8,63,1024]{2,1,0:T(8,128)S(1)} %get-tuple-element.50, f32[8,63,1024]{2,1,0:T(8,128)S(1)} %get-tuple-element.49, f32[8,1,1024]{2,1,0:T(1,128)S(1)} %collective-permute-done.9, f32[8,64,1024]{2,1,0:T(8,128)S(1)} %fusion.50, ...), kind=kLoop, calls=%fused_computation.98 | loop fusion | flops 45088768 | bytes 37216256 | tf_op jit(solution)/shard_map/mul | solution.py:102
  102.3 12.6 %all-to-all-start = ((f32[32,1,1536]{2,1,0:T(1,128)}), f32[32,1,1536]{2,1,0:T(1,128)S(1)}, u32[]{:S(2)}, u32[]{:S(2)}) async-start(f32[32,1,1536]{2,1,0:T(1,128)} %reshape.97), calls=%async_computation | async-start | bytes 393216 | tf_op jit(solution)/shard_map/all_to_all | solution.py:122
  114.9 9.8 %all-to-all-done = f32[32,1,1536]{2,1,0:T(1,128)S(1)} async-done(((f32[32,1,1536]{2,1,0:T(1,128)}), f32[32,1,1536]{2,1,0:T(1,128)S(1)}, u32[]{:S(2)}, u32[]{:S(2)}) %all-to-all-start) | async-done | bytes 196640 | tf_op jit(solution)/shard_map/all_to_all | solution.py:122
  128.9 5.5 %collective-permute-start.10 = (f32[3,3,32,128]{3,2,1,0:T(8,128)S(1)}, f32[3,3,32,128]{3,2,1,0:T(8,128)S(1)}, u32[]{:S(2)}, u32[]{:S(2)}) collective-permute-start(f32[3,3,32,128]{3,2,1,0:T(8,128)S(1)} %get-tuple-element.67), channel_id=1, source_target_pairs={{0,4},{4,8},{8,12},{12,16},{16,20},{20,24},{24,28},{28,32},{32,36}... | collective-permute-start | bytes 442376 | tf_op jit(solution)/shard_map/ppermute | solution.py:138
  134.4 2.0 %collective-permute-done.11 = f32[3,3,32,128]{3,2,1,0:T(8,128)S(1)} collective-permute-done((f32[3,3,32,128]{3,2,1,0:T(8,128)S(1)}, f32[3,3,32,128]{3,2,1,0:T(8,128)S(1)}, u32[]{:S(2)}, u32[]{:S(2)}) %collective-permute-start.11) | collective-permute-done | bytes 147488 | tf_op jit(solution)/shard_map/ppermute | solution.py:139
  137.3 3.1 %collective-permute-start.13 = (f32[3,14,8,128]{3,2,1,0:T(8,128)S(1)}, f32[3,14,8,128]{3,2,1,0:T(8,128)S(1)}, u32[]{:S(2)}, u32[]{:S(2)}) collective-permute-start(f32[3,14,8,128]{3,2,1,0:T(8,128)S(1)} %get-tuple-element.66), channel_id=1, source_target_pairs={{1,0},{2,1},{3,2},{5,4},{6,5},{7,6},{9,8},{10,9},{11,10},{13,12},{... | collective-permute-start | bytes 516104 | tf_op jit(solution)/shard_map/ppermute | solution.py:139
  140.4 3.8 %collective-permute-start.12 = (f32[3,14,8,128]{3,2,1,0:T(8,128)S(1)}, f32[3,14,8,128]{3,2,1,0:T(8,128)S(1)}, u32[]{:S(2)}, u32[]{:S(2)}) collective-permute-start(f32[3,14,8,128]{3,2,1,0:T(8,128)S(1)} %get-tuple-element.65), channel_id=1, source_target_pairs={{0,1},{1,2},{2,3},{4,5},{5,6},{6,7},{8,9},{9,10},{10,11},{12,13},{... | collective-permute-start | bytes 516104 | tf_op jit(solution)/shard_map/ppermute | solution.py:138
  149.0 17.6 %all_to_all.10 = f32[32,1,1536]{2,1,0:T(1,128)S(1)} all-to-all(f32[32,1,1536]{2,1,0:T(1,128)S(1)} %reshape.99), channel_id=1, replica_groups=mesh['slab'=32,'gy'=4] {'slab'}, dimensions={0} | all-to-all | bytes 393216 | tf_op jit(solution)/shard_map/all_to_all | solution.py:177
  170.7 3.8 %bitcast_multiply_fusion = f32[8,64,1024]{2,1,0:T(8,128)} fusion(f32[32,8,8,64]{3,0,1,2:T(8,128)S(1)} %fusion.66, f32[32,8,1024]{2,1,0:T(8,128)S(1)} %bitcast.219), kind=kOutput, calls=%fused_computation.102 | convolution fusion | flops 1611137024 | bytes 3670016 | tf_op jit(solution)/shard_map/scxy,scz->xyz/dot_general | solution.py:181
  (92 shorter events, 34.6 us)
Async XLA Ops:
  0.6 96.8 %copy-start = (f32[32,64]{1,0:T(8,128)S(1)}, f32[32,64]{1,0:T(8,128)}, u32[]{:S(2)}) copy-start(f32[32,64]{1,0:T(8,128)} %param.22) | copy-start | bytes 24580
  8.5 26.2 %collective-permute-start.3 = (f32[2,8,1,1024]{3,2,1,0:T(1,128)}, f32[2,8,1,1024]{3,2,1,0:T(1,128)S(1)}, u32[]{:S(2)}, u32[]{:S(2)}) collective-permute-start(f32[2,8,1,1024]{3,2,1,0:T(1,128)} %get-tuple-element.40), channel_id=1, source_target_pairs={{0,1},{1,2},{2,3},{4,5},{5,6},{6,7},{8,9},{9,10},{10,11},{12,13},{... | collective-permute-start | bytes 196616 | tf_op jit(solution)/shard_map/ppermute | solution.py:18
  13.0 21.7 %collective-permute-start.2 = (f32[2,8,1,1024]{3,2,1,0:T(1,128)S(1)}, f32[2,8,1,1024]{3,2,1,0:T(1,128)S(1)}, u32[]{:S(2)}, u32[]{:S(2)}) collective-permute-start(f32[2,8,1,1024]{3,2,1,0:T(1,128)S(1)} %get-tuple-element.39), channel_id=1, source_target_pairs={{1,0},{2,1},{3,2},{5,4},{6,5},{7,6},{9,8},{10,9},{11,10},{13,12},{... | collective-permute-start | bytes 196616 | tf_op jit(solution)/shard_map/ppermute | solution.py:19
  16.0 18.7 %collective-permute-start.1 = (f32[2,1,64,1024]{3,2,1,0:T(8,128)}, f32[2,1,64,1024]{3,2,1,0:T(8,128)S(1)}, u32[]{:S(2)}, u32[]{:S(2)}) collective-permute-start(f32[2,1,64,1024]{3,2,1,0:T(8,128)} %get-tuple-element.36), channel_id=1, source_target_pairs={{0,4},{4,8},{8,12},{12,16},{16,20},{20,24},{24,28},{28,32},{32,36}... | collective-permute-start | bytes 1572872 | tf_op jit(solution)/shard_map/ppermute | solution.py:18
  20.4 23.7 %collective-permute-start = (f32[2,1,64,1024]{3,2,1,0:T(8,128)}, f32[2,1,64,1024]{3,2,1,0:T(8,128)S(1)}, u32[]{:S(2)}, u32[]{:S(2)}) collective-permute-start(f32[2,1,64,1024]{3,2,1,0:T(8,128)} %get-tuple-element.35), channel_id=1, source_target_pairs={{4,0},{8,4},{12,8},{16,12},{20,16},{24,20},{28,24},{32,28},{36,32}... | collective-permute-start | bytes 1572872 | tf_op jit(solution)/shard_map/ppermute | solution.py:19
  31.5 12.6 %copy-start.3 = (f32[2,8,64,1023]{3,2,1,0:T(8,128)S(1)}, f32[2,8,64,1023]{3,2,1,0:T(8,128)}, u32[]{:S(2)}) copy-start(f32[2,8,64,1023]{3,2,1,0:T(8,128)} %fusion) | copy-start | bytes 12570628
  31.5 12.6 %copy-start.4 = (f32[2,8,64,1024]{3,2,1,0:T(8,128)S(1)}, f32[2,8,64,1024]{3,2,1,0:T(8,128)}, u32[]{:S(2)}) copy-start(f32[2,8,64,1024]{3,2,1,0:T(8,128)} %select_maximum_fusion) | copy-start | bytes 12582916
  31.5 12.6 %copy-start.5 = (f32[2,7,64,1024]{3,2,1,0:T(8,128)S(1)}, f32[2,7,64,1024]{3,2,1,0:T(8,128)}, u32[]{:S(2)}) copy-start(f32[2,7,64,1024]{3,2,1,0:T(8,128)} %get-tuple-element.33) | copy-start | bytes 11010052
  55.5 15.9 %collective-permute-start.4 = (f32[1,64,1024]{2,1,0:T(8,128)S(1)}, f32[1,64,1024]{2,1,0:T(8,128)S(1)}, u32[]{:S(2)}, u32[]{:S(2)}) collective-permute-start(f32[1,64,1024]{2,1,0:T(8,128)S(1)} %get-tuple-element.58), channel_id=1, source_target_pairs={{4,0},{8,4},{12,8},{16,12},{20,16},{24,20},{28,24},{32,28},{36,32}... | collective-permute-start | bytes 786440 | tf_op jit(solution)/shard_map/ppermute | solution.py:19
  56.8 14.7 %collective-permute-start.5 = (f32[1,64,1024]{2,1,0:T(8,128)S(1)}, f32[1,64,1024]{2,1,0:T(8,128)S(1)}, u32[]{:S(2)}, u32[]{:S(2)}) collective-permute-start(f32[1,64,1024]{2,1,0:T(8,128)S(1)} %get-tuple-element.57), channel_id=1, source_target_pairs={{0,4},{4,8},{8,12},{12,16},{16,20},{20,24},{24,28},{28,32},{32,36}... | collective-permute-start | bytes 786440 | tf_op jit(solution)/shard_map/ppermute | solution.py:18
  62.3 9.1 %collective-permute-start.6 = (f32[8,1,1024]{2,1,0:T(1,128)S(1)}, f32[8,1,1024]{2,1,0:T(1,128)S(1)}, u32[]{:S(2)}, u32[]{:S(2)}) collective-permute-start(f32[8,1,1024]{2,1,0:T(1,128)S(1)} %get-tuple-element.54), channel_id=1, source_target_pairs={{1,0},{2,1},{3,2},{5,4},{6,5},{7,6},{9,8},{10,9},{11,10},{13,12},{... | collective-permute-start | bytes 98312 | tf_op jit(solution)/shard_map/ppermute | solution.py:19
  64.2 7.2 %copy-start.6 = (f32[8,64,1024]{2,1,0:T(8,128)S(1)}, f32[8,64,1024]{2,1,0:T(8,128)}, u32[]{:S(2)}) copy-start(f32[8,64,1024]{2,1,0:T(8,128)} %param.17) | copy-start | bytes 6291460
  64.2 7.2 %copy-start.7 = (f32[8,64,1024]{2,1,0:T(8,128)S(1)}, f32[8,64,1024]{2,1,0:T(8,128)}, u32[]{:S(2)}) copy-start(f32[8,64,1024]{2,1,0:T(8,128)} %param.18) | copy-start | bytes 6291460
  64.3 7.2 %collective-permute-start.7 = (f32[8,1,1024]{2,1,0:T(1,128)S(1)}, f32[8,1,1024]{2,1,0:T(1,128)S(1)}, u32[]{:S(2)}, u32[]{:S(2)}) collective-permute-start(f32[8,1,1024]{2,1,0:T(1,128)S(1)} %get-tuple-element.53), channel_id=1, source_target_pairs={{0,1},{1,2},{2,3},{4,5},{5,6},{6,7},{8,9},{9,10},{10,11},{12,13},{... | collective-permute-start | bytes 98312 | tf_op jit(solution)/shard_map/ppermute | solution.py:18
  80.3 9.4 %copy-start.1 = (f32[8,64,1024]{2,1,0:T(8,128)}, f32[8,64,1024]{2,1,0:T(8,128)S(1)}, u32[]{:S(2)}) copy-start(f32[8,64,1024]{2,1,0:T(8,128)S(1)} %fusion.50) | copy-start | bytes 6291460
  83.1 6.0 %collective-permute-start.8 = (f32[8,1,1024]{2,1,0:T(1,128)S(1)}, f32[8,1,1024]{2,1,0:T(1,128)S(1)}, u32[]{:S(2)}, u32[]{:S(2)}) collective-permute-start(f32[8,1,1024]{2,1,0:T(1,128)S(1)} %get-tuple-element.48), channel_id=1, source_target_pairs={{1,0},{2,1},{3,2},{5,4},{6,5},{7,6},{9,8},{10,9},{11,10},{13,12},{... | collective-permute-start | bytes 98312 | tf_op jit(solution)/shard_map/ppermute | solution.py:19
  85.0 4.7 %collective-permute-start.9 = (f32[8,1,1024]{2,1,0:T(1,128)S(1)}, f32[8,1,1024]{2,1,0:T(1,128)S(1)}, u32[]{:S(2)}, u32[]{:S(2)}) collective-permute-start(f32[8,1,1024]{2,1,0:T(1,128)S(1)} %get-tuple-element.47), channel_id=1, source_target_pairs={{0,1},{1,2},{2,3},{4,5},{5,6},{6,7},{8,9},{9,10},{10,11},{12,13},{... | collective-permute-start | bytes 98312 | tf_op jit(solution)/shard_map/ppermute | solution.py:18
  100.9 14.0 %copy-start.12 = (f32[8,32,128]{2,1,0:T(8,128)S(1)}, f32[8,32,128]{2,1,0:T(8,128)}, u32[]{:S(2)}) copy-start(f32[8,32,128]{2,1,0:T(8,128)} %param.24) | copy-start | bytes 393220
  102.3 22.4 %all-to-all-start = ((f32[32,1,1536]{2,1,0:T(1,128)}), f32[32,1,1536]{2,1,0:T(1,128)S(1)}, u32[]{:S(2)}, u32[]{:S(2)}) async-start(f32[32,1,1536]{2,1,0:T(1,128)} %reshape.97), calls=%async_computation | async-start | bytes 393216 | tf_op jit(solution)/shard_map/all_to_all | solution.py:122
  127.6 8.8 %collective-permute-start.11 = (f32[3,3,32,128]{3,2,1,0:T(8,128)S(1)}, f32[3,3,32,128]{3,2,1,0:T(8,128)S(1)}, u32[]{:S(2)}, u32[]{:S(2)}) collective-permute-start(f32[3,3,32,128]{3,2,1,0:T(8,128)S(1)} %get-tuple-element.68), channel_id=1, source_target_pairs={{4,0},{8,4},{12,8},{16,12},{20,16},{24,20},{28,24},{32,28},{36,32}... | collective-permute-start | bytes 442376 | tf_op jit(solution)/shard_map/ppermute | solution.py:139
  128.9 8.4 %collective-permute-start.10 = (f32[3,3,32,128]{3,2,1,0:T(8,128)S(1)}, f32[3,3,32,128]{3,2,1,0:T(8,128)S(1)}, u32[]{:S(2)}, u32[]{:S(2)}) collective-permute-start(f32[3,3,32,128]{3,2,1,0:T(8,128)S(1)} %get-tuple-element.67), channel_id=1, source_target_pairs={{0,4},{4,8},{8,12},{12,16},{16,20},{20,24},{24,28},{28,32},{32,36}... | collective-permute-start | bytes 442376 | tf_op jit(solution)/shard_map/ppermute | solution.py:138
  137.3 8.1 %collective-permute-start.13 = (f32[3,14,8,128]{3,2,1,0:T(8,128)S(1)}, f32[3,14,8,128]{3,2,1,0:T(8,128)S(1)}, u32[]{:S(2)}, u32[]{:S(2)}) collective-permute-start(f32[3,14,8,128]{3,2,1,0:T(8,128)S(1)} %get-tuple-element.66), channel_id=1, source_target_pairs={{1,0},{2,1},{3,2},{5,4},{6,5},{7,6},{9,8},{10,9},{11,10},{13,12},{... | collective-permute-start | bytes 516104 | tf_op jit(solution)/shard_map/ppermute | solution.py:139
  140.4 6.2 %collective-permute-start.12 = (f32[3,14,8,128]{3,2,1,0:T(8,128)S(1)}, f32[3,14,8,128]{3,2,1,0:T(8,128)S(1)}, u32[]{:S(2)}, u32[]{:S(2)}) collective-permute-start(f32[3,14,8,128]{3,2,1,0:T(8,128)S(1)} %get-tuple-element.65), channel_id=1, source_target_pairs={{0,1},{1,2},{2,3},{4,5},{5,6},{6,7},{8,9},{9,10},{10,11},{12,13},{... | collective-permute-start | bytes 516104 | tf_op jit(solution)/shard_map/ppermute | solution.py:138
  147.6 20.0 %copy-start.10 = (f32[8,32,128]{2,1,0:T(8,128)}, f32[8,32,128]{2,1,0:T(8,128)S(1)}, u32[]{:S(2)}) copy-start(f32[8,32,128]{2,1,0:T(8,128)S(1)} %fusion.96) | copy-start | bytes 393220
  (4 other events, 11.6 us)
